TPU v7x, 256 devices: a whole 4x4x8 slice. The times are simulated.
256 devices in a mesh: sub: 64 (over z, x, core), row: 4 (over y).
Axes of the slice: x: 4, y: 4, z: 8, core: 2. Of those that a mesh axis runs over, the one named last changes fastest.
Arguments:
- residual: float32 [32, 64, 2048], P(None, 'sub', 'row')
- factor: float32 [64, 3072, 3072], P('sub', 'row'), may hold values from -0.0390625 to 0.0390625
- basis: float32 [96, 64, 2048], P(None, 'sub', 'row'), may hold values from -0.015625 to 0.015625
- send_rows: int32 [64, 2, 512], P('sub'), may hold values from 0 to 2047, as said below
Outputs:
- coeffs: float32 [96, 32], replicated
- rfactor: float32 [32, 32], replicated
- block_q: float32 [32, 64, 2048], P(None, 'sub', 'row')
Inputs may be any that keep to these rules, and one draw needn't show every extreme that they name: Within each send_rows[s, side, :] the rows are distinct.
All inputs are finite; a program needn't handle non-finite values.
Results may differ from a plain program's by a relative error of at most 0.000073.
Values sent between devices are 32-bit elements; how exact they have to be, the bound alone decides.
No kernel may reach another device: no remote copies, remote signals or barrier semaphores. Data moves between devices by JAX's collectives and lax.ppermute only.
A program may use at most 64 MiB of HBM per device.

v0:
```python
import jax
import jax.numpy as jnp
from jax import lax
from jax.sharding import PartitionSpec as P

HIGH = lax.Precision.HIGHEST


def from_behind(value, axis, steps):
    count = lax.axis_size(axis)
    leading, last = (max(0, -steps), min(count, count - steps))
    return lax.ppermute(value, axis, [(source, source + steps) for source in range(leading, last)])


def contract_rows(left_mat, right_mat):
    return lax.dot_general(left_mat, right_mat, (((1,), (1,)), ((), ())), precision=HIGH)


def contract_first(left_mat, right_mat):
    return lax.dot_general(left_mat, right_mat, (((0,), (0,)), ((), ())), precision=HIGH)


def second_sum(inner):
    return lax.psum(inner, ("sub", "row"))


def per_device(residual, factor, basis, send_rows):
    slab = residual.shape[2]
    row_count = lax.axis_size("row")
    sub_rows = slab * row_count
    total_rows = sub_rows * lax.axis_size("sub")
    own_rows = residual[:, 0, :]
    whole = lax.all_gather(own_rows, "row", axis=1, tiled=True)
    index_rows = send_rows[0]
    to_lower = jnp.take(whole, index_rows[0], axis=1)
    to_upper = jnp.take(whole, index_rows[1], axis=1)
    from_lower = from_behind(to_upper, "sub", 1)
    from_upper = from_behind(to_lower, "sub", -1)
    extended = jnp.concatenate([whole, from_lower, from_upper], axis=1)
    factor_rows = factor[0]
    share = factor_rows.shape[0]
    margin = from_lower.shape[1]
    row_pos = lax.axis_index("row")
    global_rows = row_pos * share + lax.iota(jnp.int32, share)
    columns = lax.iota(jnp.int32, factor_rows.shape[1])
    full = factor_rows + (global_rows[:, None] == columns[None, :]).astype(jnp.float32)
    inner = contract_rows(extended, full)
    partial_value = jnp.dot(inner, full, precision=HIGH)
    summed = lax.psum(partial_value, "row")
    mine = lax.dynamic_slice_in_dim(summed, row_pos * slab, slab, 1)
    margins = summed[:, sub_rows:]
    back_upper = from_behind(margins[:, :margin], "sub", -1)
    back_lower = from_behind(margins[:, margin:], "sub", 1)
    my_rows = row_pos * slab + lax.iota(jnp.int32, slab)
    select_upper = (index_rows[1][:, None] == my_rows[None, :]).astype(jnp.float32)
    select_lower = (index_rows[0][:, None] == my_rows[None, :]).astype(jnp.float32)
    block_t = (
        mine
        + jnp.dot(back_upper, select_upper, precision=HIGH)
        + jnp.dot(back_lower, select_lower, precision=HIGH)
    )
    vectors = basis[:, 0, :]
    first = lax.psum(contract_rows(vectors, block_t), ("sub", "row"))
    once = block_t - contract_first(first, vectors)
    inner_two = contract_rows(vectors, once)
    second = second_sum(inner_two)
    twice = once - contract_first(second, vectors)
    gram = lax.psum(contract_rows(twice, twice), ("sub", "row")) / total_rows
    lower_tri = jnp.linalg.cholesky(gram)
    solved = jax.scipy.linalg.solve_triangular(lower_tri, twice, lower=True)
    return (first + second, lower_tri.T, solved[:, None, :])


def solution(mesh):
    placed = (
        P(None, "sub", "row"),
        P("sub", "row", None),
        P(None, "sub", "row"),
        P("sub", None, None),
    )
    return jax.shard_map(
        per_device,
        mesh=mesh,
        in_specs=placed,
        out_specs=(P(), P(), P(None, "sub", "row")),
        check_vma=False,
    )
```

profile of v0, /device:TPU:38, one launch (start us, length us, event | category | flops | bytes accessed | tf_op | source)
XLA Modules:
  0.0 364.7 jit_solution(2224883184185922251)
XLA Ops:
  7.2 0.8 fusion.30
  8.0 1.0 copy.12
  9.0 15.1 %all-gather = f32[32,1,2048]{0,2,1:T(8,128)S(1)} all-gather(f32[32,1,512]{0,2,1:T(8,128)S(1)} %copy.12), channel_id=2, replica_groups=mesh['sub'=64,'row'=4] {'row'}, dimensions={2}, use_global_device_ids=true | all-gather | bytes 327680 | tf_op jit(solution)/shard_map/all_gather | solution.py:33
  24.1 1.0 gather_fusion
  25.3 1.9 collective-permute-start
  27.3 1.0 gather_fusion.1
  28.5 3.6 collective-permute-start.1
  33.1 2.9 collective-permute-done.1
  36.1 11.7 %fusion.1 = f32[32,768]{1,0:T(8,128)S(1)} fusion(f32[1,768,3072]{2,1,0:T(8,128)} %param.7, s32[768]{0:T(1024)S(1)} %iota_add_fusion, f32[32,512]{1,0:T(8,128)S(1)} %copy.15, f32[32,512]{1,0:T(8,128)S(1)} %copy.14, f32[32,2048]{1,0:T(8,128)S(1)} %copy.13), kind=kOutput, calls=%fused_computation.5 | convolution fusion | flops 913244160 | bytes 9931776 | tf_op jit(solution)/shard_map/dot_general | solution.py:16
  47.8 7.4 %fusion = f32[32,3072]{1,0:T(8,128)} fusion(f32[32,768]{1,0:T(8,128)S(1)} %fusion.1, f32[1,768,3072]{2,1,0:T(8,128)S(1)} %copy-done, s32[768]{0:T(1024)S(1)} %iota_add_fusion), kind=kOutput, calls=%fused_computation.4 | convolution fusion | flops 913047552 | bytes 9931776 | tf_op jit(solution)/shard_map/dot_general | solution.py:48
  55.3 53.8 %all-reduce.2.cloned.1.call-done = f32[32,3072]{1,0:T(8,128)} async-done(((f32[32,3072]{1,0:T(8,128)}), f32[32,3072]{1,0:T(8,128)}) %all-reduce.2.cloned.1.call-update) | async-done | bytes 393232 | tf_op jit(solution)/shard_map/psum | solution.py:49
  109.1 0.9 fusion.29
  110.0 1.9 collective-permute-start.3
  111.9 3.8 %collective-permute-start.2 = (f32[32,512]{1,0:T(8,128)S(1)}, f32[32,512]{1,0:T(8,128)S(1)}, u32[]{:S(2)}, u32[]{:S(2)}) collective-permute-start(f32[32,512]{1,0:T(8,128)S(1)} %get-tuple-element.10), channel_id=1, source_target_pairs={{4,0},{8,4},{12,8},{16,12},{20,16},{24,20},{28,24},{32,28},{36,32}... | collective-permute-start | bytes 196616 | tf_op jit(solution)/shard_map/ppermute | solution.py:12
  116.3 1.2 collective-permute-done.2
  117.5 1.4 fusion.4
  119.2 78.5 %psum.29 = f32[96,32]{0,1:T(8,128)S(1)} all-reduce(f32[96,32]{0,1:T(8,128)S(1)} %convolution_bitcast_fusion.2), channel_id=1, replica_groups=mesh['sub'=64,'row'=4] {'sub','row'}, use_global_device_ids=true, to_apply=%region_1.3 | all-reduce | flops 3072 | bytes 24576 | tf_op jit(solution)/shard_map/psum | solution.py:63
  198.2 76.7 %psum.30 = f32[96,32]{0,1:T(8,128)S(1)} all-reduce(f32[96,32]{0,1:T(8,128)S(1)} %convolution_bitcast_fusion.1), channel_id=1, replica_groups=mesh['sub'=64,'row'=4] {'sub','row'}, use_global_device_ids=true, to_apply=%region_2.4 | all-reduce | flops 3072 | bytes 24576 | tf_op jit(solution)/shard_map/psum | solution.py:24
  276.0 73.4 %psum.31 = f32[32,32]{0,1:T(8,128)S(1)} all-reduce(f32[32,32]{0,1:T(8,128)S(1)} %fusion.31), channel_id=1, replica_groups=mesh['sub'=64,'row'=4] {'sub','row'}, use_global_device_ids=true, to_apply=%region_3.5 | all-reduce | flops 1024 | bytes 8192 | tf_op jit(solution)/shard_map/psum | solution.py:68
  349.5 2.9 cholesky.18
  353.1 0.7 select_bitcast_fusion.2
  353.7 2.4 custom-call.7
  356.5 0.7 copy.19
  357.2 0.7 copy.18
  (34 shorter events, 4.9 us)
Async XLA Ops:
  7.2 101.9 %all-reduce.2.cloned.1.call-start = ((), (), s32[]{:S(2)}) async-start(), calls=%async_computation | async-start | bytes 786432 | tf_op jit(solution)/shard_map/psum | solution.py:49
  25.3 7.7 %collective-permute-start = (f32[32,512]{0,1:T(8,128)S(1)}, f32[32,512]{0,1:T(8,128)S(1)}, u32[]{:S(2)}, u32[]{:S(2)}) collective-permute-start(f32[32,512]{0,1:T(8,128)S(1)} %select_bitcast_fusion.1), channel_id=1, source_target_pairs={{0,4},{4,8},{8,12},{12,16},{16,20},{20,24},{24,28},{28,32},{32,36}... | collective-permute-start | bytes 196616 | tf_op jit(solution)/shard_map/ppermute | solution.py:12
  28.5 7.5 %collective-permute-start.1 = (f32[32,512]{0,1:T(8,128)S(1)}, f32[32,512]{0,1:T(8,128)S(1)}, u32[]{:S(2)}, u32[]{:S(2)}) collective-permute-start(f32[32,512]{0,1:T(8,128)S(1)} %select_bitcast_fusion), channel_id=1, source_target_pairs={{4,0},{8,4},{12,8},{16,12},{20,16},{24,20},{28,24},{32,28},{36,32}... | collective-permute-start | bytes 196616 | tf_op jit(solution)/shard_map/ppermute | solution.py:12
  36.1 11.8 %copy-start = (f32[1,768,3072]{2,1,0:T(8,128)S(1)}, f32[1,768,3072]{2,1,0:T(8,128)}, u32[]{:S(2)}) copy-start(f32[1,768,3072]{2,1,0:T(8,128)} %param.7) | copy-start | bytes 28311556
  36.1 82.8 %copy-start.1 = (f32[96,1,512]{2,1,0:T(1,128)S(1)}, f32[96,1,512]{2,1,0:T(1,128)}, u32[]{:S(2)}) copy-start(f32[96,1,512]{2,1,0:T(1,128)} %param.8) | copy-start | bytes 589828
  110.0 5.8 %collective-permute-start.3 = (f32[32,512]{1,0:T(8,128)S(1)}, f32[32,512]{1,0:T(8,128)S(1)}, u32[]{:S(2)}, u32[]{:S(2)}) collective-permute-start(f32[32,512]{1,0:T(8,128)S(1)} %get-tuple-element.11), channel_id=1, source_target_pairs={{0,4},{4,8},{8,12},{12,16},{16,20},{20,24},{24,28},{28,32},{32,36}... | collective-permute-start | bytes 196616 | tf_op jit(solution)/shard_map/ppermute | solution.py:12
  111.9 5.5 %collective-permute-start.2 = (f32[32,512]{1,0:T(8,128)S(1)}, f32[32,512]{1,0:T(8,128)S(1)}, u32[]{:S(2)}, u32[]{:S(2)}) collective-permute-start(f32[32,512]{1,0:T(8,128)S(1)} %get-tuple-element.10), channel_id=1, source_target_pairs={{4,0},{8,4},{12,8},{16,12},{20,16},{24,20},{28,24},{32,28},{36,32}... | collective-permute-start | bytes 196616 | tf_op jit(solution)/shard_map/ppermute | solution.py:12
Sparse Core Ops, SparseCore 0:
  55.4 53.6 all-reduce.1
where the time goes:
time: 368 us; the launch traced here: 365 us
  blocking collectives  244 us (66%)
  waiting for transfers between devices  58.5 us (16%)
  matrix products  22.6 us (6%)
  between operations  14.3 us (4%)
  starting transfers between devices  11.3 us (3%)
  other arithmetic  7.62 us (2%)
  local copies, waits for them, and re-layouts  6.64 us (2%)
    psum x1, blocking collectives, per_device(): first = lax.psum(contract_rows(vectors, block_t), ('sub', 'row'))  78.5 us
    psum x1, blocking collectives, second_sum(): return lax.psum(inner, ('sub', 'row'))  76.7 us
    psum x1, blocking collectives, per_device(): gram = lax.psum(contract_rows(twice, twice), ('sub', 'row')) / total_rows  73.4 us
    psum x1, waiting for transfers between devices, per_device(): summed = lax.psum(partial_value, 'row')  53.8 us
    all_gather x1, blocking collectives, per_device(): whole = lax.all_gather(own_rows, 'row', axis=1, tiled=True)  15.1 us
    dot_general x4, matrix products, contract_rows(): lax.dot_general(left_mat, right_mat, (((1,), (1,)), ((), ())), precision=...  12.6 us
    ppermute x4, starting transfers between devices, from_behind(): lax.ppermute(value, axis, [(source, source + steps) for source in range(l...  11.3 us
    dot_general x1, matrix products, per_device(): partial_value = jnp.dot(inner, full, precision=HIGH)  7.41 us
  transfers between devices with their start and end apart: 5, of which 4 were waited for; matrix products, arithmetic and copies ran while one was open for 1% of the time, Pallas kernels for 0%

commit v1 on v0

v1 whole, which is shorter than its diff:
```python
import jax
import jax.numpy as jnp
from jax import lax
from jax.sharding import PartitionSpec as P

HIGH = lax.Precision.HIGHEST


def from_behind(value, axis, steps):
    count = lax.axis_size(axis)
    leading, last = (max(0, -steps), min(count, count - steps))
    return lax.ppermute(value, axis, [(source, source + steps) for source in range(leading, last)])


def swap(value, axis, mask):
    count = lax.axis_size(axis)
    return lax.ppermute(value, axis, [(source, source ^ mask) for source in range(count)])


def contract_rows(left_mat, right_mat):
    return lax.dot_general(left_mat, right_mat, (((1,), (1,)), ((), ())), precision=HIGH)


def contract_first(left_mat, right_mat):
    return lax.dot_general(left_mat, right_mat, (((0,), (0,)), ((), ())), precision=HIGH)


def gather_rows(own, axis):
    pos = lax.axis_index(axis)
    block = own
    step = 1
    while step < lax.axis_size(axis):
        other = swap(block, axis, step)
        upper = (pos & step) != 0
        block = jnp.where(upper, jnp.concatenate([other, block], axis=1), jnp.concatenate([block, other], axis=1))
        step *= 2
    return block


def scatter_rows(value, axis):
    pos = lax.axis_index(axis)
    step = lax.axis_size(axis) // 2
    block = value
    while step >= 1:
        half = block.shape[1] // 2
        upper = ((pos // step) % 2).astype(jnp.int32)
        keep = lax.dynamic_slice_in_dim(block, upper * half, half, 1)
        send = lax.dynamic_slice_in_dim(block, (1 - upper) * half, half, 1)
        block = keep + swap(send, axis, step)
        step //= 2
    return block


def all_sum(value, axes):
    for axis in axes:
        step = 1
        while step < lax.axis_size(axis):
            value = value + swap(value, axis, step)
            step *= 2
    return value


def per_device(residual, factor, basis, send_rows):
    slab = residual.shape[2]
    row_count = lax.axis_size("row")
    sub_rows = slab * row_count
    total_rows = sub_rows * lax.axis_size("sub")
    own_rows = residual[:, 0, :]
    whole = gather_rows(own_rows, "row")
    index_rows = send_rows[0]
    to_lower = jnp.take(whole, index_rows[0], axis=1)
    to_upper = jnp.take(whole, index_rows[1], axis=1)
    from_lower = from_behind(to_upper, "sub", 1)
    from_upper = from_behind(to_lower, "sub", -1)
    extended = jnp.concatenate([whole, from_lower, from_upper], axis=1)
    factor_rows = factor[0]
    share = factor_rows.shape[0]
    margin = from_lower.shape[1]
    row_pos = lax.axis_index("row")
    global_rows = row_pos * share + lax.iota(jnp.int32, share)
    columns = lax.iota(jnp.int32, factor_rows.shape[1])
    full = factor_rows + (global_rows[:, None] == columns[None, :]).astype(jnp.float32)
    inner = contract_rows(extended, full)
    partial_value = jnp.dot(inner, full, precision=HIGH)
    back_upper = from_behind(partial_value[:, sub_rows:sub_rows + margin], "sub", -1)
    back_lower = from_behind(partial_value[:, sub_rows + margin:], "sub", 1)
    all_rows = lax.iota(jnp.int32, sub_rows)
    select_upper = (index_rows[1][:, None] == all_rows[None, :]).astype(jnp.float32)
    select_lower = (index_rows[0][:, None] == all_rows[None, :]).astype(jnp.float32)
    gathered = (
        partial_value[:, :sub_rows]
        + jnp.dot(back_upper, select_upper, precision=HIGH)
        + jnp.dot(back_lower, select_lower, precision=HIGH)
    )
    block_t = scatter_rows(gathered, "row")
    vectors = basis[:, 0, :]
    count = vectors.shape[0]
    vecs = block_t.shape[0]
    first_part = contract_rows(vectors, block_t)
    basis_gram = contract_rows(vectors, vectors)
    block_gram = contract_rows(block_t, block_t)
    packed = jnp.concatenate(
        [
            jnp.concatenate([first_part, basis_gram], axis=1),
            jnp.concatenate([block_gram, jnp.zeros((vecs, count), jnp.float32)], axis=1),
        ],
        axis=0,
    )
    summed = all_sum(packed, ("sub", "row"))
    first, basis_gram, block_gram = lax.optimization_barrier(
        (summed[:count, :vecs], summed[:count, vecs:], summed[count:, :vecs])
    )
    second = first - jnp.dot(basis_gram, first, precision=HIGH)
    coeffs = first + second
    once = block_t - contract_first(first, vectors)
    twice = once - contract_first(second, vectors)
    cross = contract_first(first, coeffs)
    gram = (
        block_gram - cross - cross.T + contract_first(coeffs, jnp.dot(basis_gram, coeffs, precision=HIGH))
    ) / total_rows
    lower_tri = jnp.linalg.cholesky(gram)
    solved = jax.scipy.linalg.solve_triangular(lower_tri, twice, lower=True)
    return (coeffs, lower_tri.T, solved[:, None, :])


def solution(mesh):
    placed = (
        P(None, "sub", "row"),
        P("sub", "row", None),
        P(None, "sub", "row"),
        P("sub", None, None),
    )
    return jax.shard_map(
        per_device,
        mesh=mesh,
        in_specs=placed,
        out_specs=(P(), P(), P(None, "sub", "row")),
        check_vma=False,
    )
```

time: 368 us -> 123 us (0.33)
  blocking collectives: 244 us -> 0 us
  starting transfers between devices: 11.3 us -> 40.9 us
  waiting for transfers between devices: 58.5 us -> 42.4 us
  between operations: 14.3 us -> 1.06 us
    psum x3 -> x0, blocking collectives: 229 us -> none  [the longest x1 78.5 us: per_device(): first = lax.psum(contract_rows(vectors, block_t), ('sub', 'row'))]
    psum x1 -> x0, waiting for transfers between devices: 53.8 us -> none  [per_device(): summed = lax.psum(partial_value, 'row')]
    ppermute x0 -> x12, waiting for transfers between devices: none -> 39.1 us  [swap(): lax.ppermute(value, axis, [(source, source ^ mask) for source in range(co...]
    ppermute x0 -> x12, starting transfers between devices: none -> 26.9 us  [swap(): lax.ppermute(value, axis, [(source, source ^ mask) for source in range(co...]
    all_gather x1 -> x0, blocking collectives: 15.1 us -> none  [per_device(): whole = lax.all_gather(own_rows, 'row', axis=1, tiled=True)]
  transfers between devices with their start and end apart: 5 -> 16, of which waited for: 4 -> 14; matrix products, arithmetic and copies ran while one was open for 1% -> 4% of each run, Pallas kernels for 0% -> 0%
where the time goes in v1:
time: 123 us; the launch traced here: 122 us
  waiting for transfers between devices  42.4 us (34%)
  starting transfers between devices  40.9 us (33%)
  matrix products  24.1 us (20%)
  other arithmetic  7.42 us (6%)
  local copies, waits for them, and re-layouts  6.51 us (5%)
    ppermute x12, waiting for transfers between devices, swap(): lax.ppermute(value, axis, [(source, source ^ mask) for source in range(co...  39.1 us
    ppermute x12, starting transfers between devices, swap(): lax.ppermute(value, axis, [(source, source ^ mask) for source in range(co...  26.9 us
    ppermute x4, starting transfers between devices, from_behind(): lax.ppermute(value, axis, [(source, source + steps) for source in range(l...  14 us
    dot_general x4, matrix products, contract_rows(): lax.dot_general(left_mat, right_mat, (((1,), (1,)), ((), ())), precision=...  12.6 us
    dot_general x1, matrix products, per_device(): partial_value = jnp.dot(inner, full, precision=HIGH)  6.66 us
    another operation x3, other arithmetic, per_device(): lower_tri = jnp.linalg.cholesky(gram)  3.6 us
    ppermute x4, waiting for transfers between devices, from_behind(): lax.ppermute(value, axis, [(source, source + steps) for source in range(l...  3.27 us
    another operation x2, other arithmetic, per_device(): solved = jax.scipy.linalg.solve_triangular(lower_tri, twice, lower=True)  3.09 us
  transfers between devices with their start and end apart: 16, of which 14 were waited for; matrix products, arithmetic and copies ran while one was open for 4% of the time, Pallas kernels for 0%

profile of v1, /device:TPU:38, one launch (start us, length us, event | category | flops | bytes accessed | tf_op | source)
XLA Modules:
  0.0 122.3 jit_solution(809849439283805262)
XLA Ops:
  5.8 3.3 %collective-permute-start.1 = (f32[32,1024]{1,0:T(8,128)S(1)}, f32[32,1024]{1,0:T(8,128)S(1)}, u32[]{:S(2)}, u32[]{:S(2)}) collective-permute-start(f32[32,1024]{1,0:T(8,128)S(1)} %maximum_select_fusion), channel_id=1, source_target_pairs={{0,2},{1,3},{2,0},{3,1},{4,6},{5,7},{6,4},{7,5},{8,10},{9,11},{10,... | collective-permute-start | bytes 393224 | tf_op jit(solution)/shard_map/ppermute | solution.py:17
  9.1 3.3 %collective-permute-done.1 = f32[32,1024]{1,0:T(8,128)S(1)} collective-permute-done((f32[32,1024]{1,0:T(8,128)S(1)}, f32[32,1024]{1,0:T(8,128)S(1)}, u32[]{:S(2)}, u32[]{:S(2)}) %collective-permute-start.1) | collective-permute-done | bytes 131104 | tf_op jit(solution)/shard_map/ppermute | solution.py:17
  14.4 1.9 %collective-permute-start.2 = (f32[32,512]{0,1:T(8,128)S(1)}, f32[32,512]{0,1:T(8,128)S(1)}, u32[]{:S(2)}, u32[]{:S(2)}) collective-permute-start(f32[32,512]{0,1:T(8,128)S(1)} %select_bitcast_fusion.1), channel_id=1, source_target_pairs={{0,4},{4,8},{8,12},{12,16},{16,20},{20,24},{24,28},{28,32},{32,36}... | collective-permute-start | bytes 196616 | tf_op jit(solution)/shard_map/ppermute | solution.py:12
  17.5 3.8 %collective-permute-start.3 = (f32[32,512]{0,1:T(8,128)S(1)}, f32[32,512]{0,1:T(8,128)S(1)}, u32[]{:S(2)}, u32[]{:S(2)}) collective-permute-start(f32[32,512]{0,1:T(8,128)S(1)} %select_bitcast_fusion), channel_id=1, source_target_pairs={{4,0},{8,4},{12,8},{16,12},{20,16},{24,20},{28,24},{32,28},{36,32}... | collective-permute-start | bytes 196616 | tf_op jit(solution)/shard_map/ppermute | solution.py:12
  22.1 2.8 %collective-permute-done.3 = f32[32,512]{0,1:T(8,128)S(1)} collective-permute-done((f32[32,512]{0,1:T(8,128)S(1)}, f32[32,512]{0,1:T(8,128)S(1)}, u32[]{:S(2)}, u32[]{:S(2)}) %collective-permute-start.3) | collective-permute-done | bytes 65568 | tf_op jit(solution)/shard_map/ppermute | solution.py:12
  25.1 11.7 %fusion.1 = f32[32,768]{1,0:T(8,128)S(1)} fusion(f32[1,768,3072]{2,1,0:T(8,128)} %param.7, s32[768]{0:T(1024)S(1)} %iota_add_fusion, f32[32,512]{1,0:T(8,128)S(1)} %copy.19, f32[32,512]{1,0:T(8,128)S(1)} %copy.18, f32[32,2048]{1,0:T(8,128)S(1)} %copy.17), kind=kOutput, calls=%fused_computation.5 | convolution fusion | flops 913244160 | bytes 9931776 | tf_op jit(solution)/shard_map/dot_general | solution.py:21
  36.9 6.7 %fusion = f32[32,3072]{1,0:T(8,128)S(1)} fusion(f32[32,768]{1,0:T(8,128)S(1)} %fusion.1, f32[1,768,3072]{2,1,0:T(8,128)S(1)} %copy-done, s32[768]{0:T(1024)S(1)} %iota_add_fusion), kind=kOutput, calls=%fused_computation.4 | convolution fusion | flops 913047552 | bytes 9931776 | tf_op jit(solution)/shard_map/dot_general | solution.py:84
  43.6 6.1 %collective-permute-start.5 = (f32[32,512]{1,0:T(8,128)S(1)}, f32[32,512]{1,0:T(8,128)S(1)}, u32[]{:S(2)}, u32[]{:S(2)}) collective-permute-start(f32[32,512]{1,0:T(8,128)S(1)} %get-tuple-element.17), channel_id=1, source_target_pairs={{0,4},{4,8},{8,12},{12,16},{16,20},{20,24},{24,28},{28,32},{32,36}... | collective-permute-start | bytes 196616 | tf_op jit(solution)/shard_map/ppermute | solution.py:12
  49.7 2.1 %collective-permute-start.4 = (f32[32,512]{1,0:T(8,128)S(1)}, f32[32,512]{1,0:T(8,128)S(1)}, u32[]{:S(2)}, u32[]{:S(2)}) collective-permute-start(f32[32,512]{1,0:T(8,128)S(1)} %get-tuple-element.16), channel_id=1, source_target_pairs={{4,0},{8,4},{12,8},{16,12},{20,16},{24,20},{28,24},{32,28},{36,32}... | collective-permute-start | bytes 196616 | tf_op jit(solution)/shard_map/ppermute | solution.py:12
  55.2 3.3 %collective-permute-start.6 = (f32[32,1024]{1,0:T(8,128)S(1)}, f32[32,1024]{1,0:T(8,128)S(1)}, u32[]{:S(2)}, u32[]{:S(2)}) collective-permute-start(f32[32,1024]{1,0:T(8,128)S(1)} %constant_dynamic-slice_fusion.1), channel_id=1, source_target_pairs={{0,2},{1,3},{2,0},{3,1},{4,6},{5,7},{6,4},{7,5},{8,10},{9,11},{10,... | collective-permute-start | bytes 393224 | tf_op jit(solution)/shard_map/ppermute | solution.py:17
  58.5 3.3 %collective-permute-done.6 = f32[32,1024]{1,0:T(8,128)S(1)} collective-permute-done((f32[32,1024]{1,0:T(8,128)S(1)}, f32[32,1024]{1,0:T(8,128)S(1)}, u32[]{:S(2)}, u32[]{:S(2)}) %collective-permute-start.6) | collective-permute-done | bytes 131104 | tf_op jit(solution)/shard_map/ppermute | solution.py:17
  63.8 2.3 %collective-permute-done.7 = f32[32,512]{1,0:T(8,128)S(1)} collective-permute-done((f32[32,512]{1,0:T(8,128)S(1)}, f32[32,512]{1,0:T(8,128)S(1)}, u32[]{:S(2)}, u32[]{:S(2)}) %collective-permute-start.7) | collective-permute-done | bytes 65568 | tf_op jit(solution)/shard_map/ppermute | solution.py:17
  69.4 4.3 %collective-permute-done.9 = f32[128,128]{0,1:T(8,128)S(1)} collective-permute-done((f32[128,128]{0,1:T(8,128)S(1)}, f32[128,128]{0,1:T(8,128)S(1)}, u32[]{:S(2)}, u32[]{:S(2)}) %collective-permute-start.9) | collective-permute-done | bytes 65568 | tf_op jit(solution)/shard_map/ppermute | solution.py:17
  74.6 5.1 %collective-permute-done.10 = f32[128,128]{0,1:T(8,128)S(1)} collective-permute-done((f32[128,128]{0,1:T(8,128)S(1)}, f32[128,128]{0,1:T(8,128)S(1)}, u32[]{:S(2)}, u32[]{:S(2)}) %collective-permute-start.10) | collective-permute-done | bytes 65568 | tf_op jit(solution)/shard_map/ppermute | solution.py:17
  79.9 4.2 %collective-permute-done.11 = f32[128,128]{0,1:T(8,128)S(1)} collective-permute-done((f32[128,128]{0,1:T(8,128)S(1)}, f32[128,128]{0,1:T(8,128)S(1)}, u32[]{:S(2)}, u32[]{:S(2)}) %collective-permute-start.11) | collective-permute-done | bytes 65568 | tf_op jit(solution)/shard_map/ppermute | solution.py:17
  84.0 7.0 %collective-permute-start.12 = (f32[128,128]{0,1:T(8,128)S(1)}, f32[128,128]{0,1:T(8,128)S(1)}, u32[]{:S(2)}, u32[]{:S(2)}) collective-permute-start(f32[128,128]{0,1:T(8,128)S(1)} %add.112), channel_id=1, source_target_pairs={{0,64},{4,68},{8,72},{12,76},{16,80},{20,84},{24,88},{28,92},{32,9... | collective-permute-start | bytes 196616 | tf_op jit(solution)/shard_map/ppermute | solution.py:17
  91.0 2.2 %collective-permute-done.12 = f32[128,128]{0,1:T(8,128)S(1)} collective-permute-done((f32[128,128]{0,1:T(8,128)S(1)}, f32[128,128]{0,1:T(8,128)S(1)}, u32[]{:S(2)}, u32[]{:S(2)}) %collective-permute-start.12) | collective-permute-done | bytes 65568 | tf_op jit(solution)/shard_map/ppermute | solution.py:17
  94.9 6.6 %collective-permute-done.13 = f32[128,128]{0,1:T(8,128)S(1)} collective-permute-done((f32[128,128]{0,1:T(8,128)S(1)}, f32[128,128]{0,1:T(8,128)S(1)}, u32[]{:S(2)}, u32[]{:S(2)}) %collective-permute-start.13) | collective-permute-done | bytes 65568 | tf_op jit(solution)/shard_map/ppermute | solution.py:17
  101.6 2.0 %collective-permute-start.14 = (f32[128,128]{0,1:T(8,128)S(1)}, f32[128,128]{0,1:T(8,128)S(1)}, u32[]{:S(2)}, u32[]{:S(2)}) collective-permute-start(f32[128,128]{0,1:T(8,128)S(1)} %add.114), channel_id=1, source_target_pairs={{0,1},{1,0},{2,3},{3,2},{4,5},{5,4},{6,7},{7,6},{8,9},{9,8},{10,11... | collective-permute-start | bytes 196616 | tf_op jit(solution)/shard_map/ppermute | solution.py:17
  103.6 2.8 %collective-permute-done.14 = f32[128,128]{0,1:T(8,128)S(1)} collective-permute-done((f32[128,128]{0,1:T(8,128)S(1)}, f32[128,128]{0,1:T(8,128)S(1)}, u32[]{:S(2)}, u32[]{:S(2)}) %collective-permute-start.14) | collective-permute-done | bytes 65568 | tf_op jit(solution)/shard_map/ppermute | solution.py:17
  106.4 3.7 %collective-permute-start.15 = (f32[128,128]{0,1:T(8,128)S(1)}, f32[128,128]{0,1:T(8,128)S(1)}, u32[]{:S(2)}, u32[]{:S(2)}) collective-permute-start(f32[128,128]{0,1:T(8,128)S(1)} %add.115), channel_id=1, source_target_pairs={{0,2},{1,3},{2,0},{3,1},{4,6},{5,7},{6,4},{7,5},{8,10},{9,11},{10,... | collective-permute-start | bytes 196616 | tf_op jit(solution)/shard_map/ppermute | solution.py:17
  110.1 2.2 %collective-permute-done.15 = f32[128,128]{0,1:T(8,128)S(1)} collective-permute-done((f32[128,128]{0,1:T(8,128)S(1)}, f32[128,128]{0,1:T(8,128)S(1)}, u32[]{:S(2)}, u32[]{:S(2)}) %collective-permute-start.15) | collective-permute-done | bytes 65568 | tf_op jit(solution)/shard_map/ppermute | solution.py:17
  114.0 2.9 %cholesky.18 = f32[32,32]{1,0:T(8,128)S(1)} custom-call(f32[32,32]{1,0:T(8,128)S(1)} %fusion.28), custom_call_target="Cholesky" | custom-call | tf_op jit(solution)/shard_map/jit(cholesky)/cholesky | solution.py:121
  118.2 2.4 %custom-call.7 = f32[1,32,32]{1,2,0:T(8,128)S(1)} custom-call(f32[1,32,32]{2,1,0:T(8,128)S(1)} %get-tuple-element.20), custom_call_target="InvertDiagBlocksLowerTriangular" | custom-call | tf_op jit(solution)/shard_map/jit(_solve_triangular)/triangular_solve | solution.py:122
  (76 shorter events, 25.0 us)
Async XLA Ops:
  1.5 4.3 %collective-permute-start = (f32[32,512]{1,0:T(8,128)S(1)}, f32[32,512]{1,0:T(8,128)S(1)}, u32[]{:S(2)}, u32[]{:S(2)}) collective-permute-start(f32[32,512]{1,0:T(8,128)S(1)} %bitcast.58), channel_id=1, source_target_pairs={{0,1},{1,0},{2,3},{3,2},{4,5},{5,4},{6,7},{7,6},{8,9},{9,8},{10,11... | collective-permute-start | bytes 196616 | tf_op jit(solution)/shard_map/ppermute | solution.py:17
  5.8 6.6 %collective-permute-start.1 = (f32[32,1024]{1,0:T(8,128)S(1)}, f32[32,1024]{1,0:T(8,128)S(1)}, u32[]{:S(2)}, u32[]{:S(2)}) collective-permute-start(f32[32,1024]{1,0:T(8,128)S(1)} %maximum_select_fusion), channel_id=1, source_target_pairs={{0,2},{1,3},{2,0},{3,1},{4,6},{5,7},{6,4},{7,5},{8,10},{9,11},{10,... | collective-permute-start | bytes 393224 | tf_op jit(solution)/shard_map/ppermute | solution.py:17
  14.4 7.7 %collective-permute-start.2 = (f32[32,512]{0,1:T(8,128)S(1)}, f32[32,512]{0,1:T(8,128)S(1)}, u32[]{:S(2)}, u32[]{:S(2)}) collective-permute-start(f32[32,512]{0,1:T(8,128)S(1)} %select_bitcast_fusion.1), channel_id=1, source_target_pairs={{0,4},{4,8},{8,12},{12,16},{16,20},{20,24},{24,28},{28,32},{32,36}... | collective-permute-start | bytes 196616 | tf_op jit(solution)/shard_map/ppermute | solution.py:12
  17.5 7.5 %collective-permute-start.3 = (f32[32,512]{0,1:T(8,128)S(1)}, f32[32,512]{0,1:T(8,128)S(1)}, u32[]{:S(2)}, u32[]{:S(2)}) collective-permute-start(f32[32,512]{0,1:T(8,128)S(1)} %select_bitcast_fusion), channel_id=1, source_target_pairs={{4,0},{8,4},{12,8},{16,12},{20,16},{24,20},{28,24},{32,28},{36,32}... | collective-permute-start | bytes 196616 | tf_op jit(solution)/shard_map/ppermute | solution.py:12
  25.1 11.8 %copy-start = (f32[1,768,3072]{2,1,0:T(8,128)S(1)}, f32[1,768,3072]{2,1,0:T(8,128)}, u32[]{:S(2)}) copy-start(f32[1,768,3072]{2,1,0:T(8,128)} %param.7) | copy-start | bytes 28311556
  25.1 38.4 %copy-start.1 = (f32[96,1,512]{2,1,0:T(1,128)S(1)}, f32[96,1,512]{2,1,0:T(1,128)}, u32[]{:S(2)}) copy-start(f32[96,1,512]{2,1,0:T(1,128)} %param.8) | copy-start | bytes 589828
  43.6 8.3 %collective-permute-start.5 = (f32[32,512]{1,0:T(8,128)S(1)}, f32[32,512]{1,0:T(8,128)S(1)}, u32[]{:S(2)}, u32[]{:S(2)}) collective-permute-start(f32[32,512]{1,0:T(8,128)S(1)} %get-tuple-element.17), channel_id=1, source_target_pairs={{0,4},{4,8},{8,12},{12,16},{16,20},{20,24},{24,28},{28,32},{32,36}... | collective-permute-start | bytes 196616 | tf_op jit(solution)/shard_map/ppermute | solution.py:12
  49.7 3.8 %collective-permute-start.4 = (f32[32,512]{1,0:T(8,128)S(1)}, f32[32,512]{1,0:T(8,128)S(1)}, u32[]{:S(2)}, u32[]{:S(2)}) collective-permute-start(f32[32,512]{1,0:T(8,128)S(1)} %get-tuple-element.16), channel_id=1, source_target_pairs={{4,0},{8,4},{12,8},{16,12},{20,16},{24,20},{28,24},{32,28},{36,32}... | collective-permute-start | bytes 196616 | tf_op jit(solution)/shard_map/ppermute | solution.py:12
  55.2 6.6 %collective-permute-start.6 = (f32[32,1024]{1,0:T(8,128)S(1)}, f32[32,1024]{1,0:T(8,128)S(1)}, u32[]{:S(2)}, u32[]{:S(2)}) collective-permute-start(f32[32,1024]{1,0:T(8,128)S(1)} %constant_dynamic-slice_fusion.1), channel_id=1, source_target_pairs={{0,2},{1,3},{2,0},{3,1},{4,6},{5,7},{6,4},{7,5},{8,10},{9,11},{10,... | collective-permute-start | bytes 393224 | tf_op jit(solution)/shard_map/ppermute | solution.py:17
  61.8 4.4 %collective-permute-start.7 = (f32[32,512]{1,0:T(8,128)S(1)}, f32[32,512]{1,0:T(8,128)S(1)}, u32[]{:S(2)}, u32[]{:S(2)}) collective-permute-start(f32[32,512]{1,0:T(8,128)S(1)} %constant_dynamic-slice_fusion), channel_id=1, source_target_pairs={{0,1},{1,0},{2,3},{3,2},{4,5},{5,4},{6,7},{7,6},{8,9},{9,8},{10,11... | collective-permute-start | bytes 196616 | tf_op jit(solution)/shard_map/ppermute | solution.py:17
  66.8 2.5 %collective-permute-start.8 = (f32[128,128]{0,1:T(8,128)S(1)}, f32[128,128]{0,1:T(8,128)S(1)}, u32[]{:S(2)}, u32[]{:S(2)}) collective-permute-start(f32[128,128]{0,1:T(8,128)S(1)} %select_maximum_fusion), channel_id=1, source_target_pairs={{0,4},{4,0},{8,12},{12,8},{16,20},{20,16},{24,28},{28,24},{32,36},... | collective-permute-start | bytes 196616 | tf_op jit(solution)/shard_map/ppermute | solution.py:17
  69.4 4.4 %collective-permute-start.9 = (f32[128,128]{0,1:T(8,128)S(1)}, f32[128,128]{0,1:T(8,128)S(1)}, u32[]{:S(2)}, u32[]{:S(2)}) collective-permute-start(f32[128,128]{0,1:T(8,128)S(1)} %fusion.54), channel_id=1, source_target_pairs={{0,8},{4,12},{8,0},{12,4},{16,24},{20,28},{24,16},{28,20},{32,40},... | collective-permute-start | bytes 196616 | tf_op jit(solution)/shard_map/ppermute | solution.py:17
  73.8 5.9 %collective-permute-start.10 = (f32[128,128]{0,1:T(8,128)S(1)}, f32[128,128]{0,1:T(8,128)S(1)}, u32[]{:S(2)}, u32[]{:S(2)}) collective-permute-start(f32[128,128]{0,1:T(8,128)S(1)} %add.110), channel_id=1, source_target_pairs={{0,16},{4,20},{8,24},{12,28},{16,0},{20,4},{24,8},{28,12},{32,48},... | collective-permute-start | bytes 196616 | tf_op jit(solution)/shard_map/ppermute | solution.py:17
  79.7 4.4 %collective-permute-start.11 = (f32[128,128]{0,1:T(8,128)S(1)}, f32[128,128]{0,1:T(8,128)S(1)}, u32[]{:S(2)}, u32[]{:S(2)}) collective-permute-start(f32[128,128]{0,1:T(8,128)S(1)} %add.111), channel_id=1, source_target_pairs={{0,32},{4,36},{8,40},{12,44},{16,48},{20,52},{24,56},{28,60},{32,0... | collective-permute-start | bytes 196616 | tf_op jit(solution)/shard_map/ppermute | solution.py:17
  84.0 9.3 %collective-permute-start.12 = (f32[128,128]{0,1:T(8,128)S(1)}, f32[128,128]{0,1:T(8,128)S(1)}, u32[]{:S(2)}, u32[]{:S(2)}) collective-permute-start(f32[128,128]{0,1:T(8,128)S(1)} %add.112), channel_id=1, source_target_pairs={{0,64},{4,68},{8,72},{12,76},{16,80},{20,84},{24,88},{28,92},{32,9... | collective-permute-start | bytes 196616 | tf_op jit(solution)/shard_map/ppermute | solution.py:17
  93.3 8.3 %collective-permute-start.13 = (f32[128,128]{0,1:T(8,128)S(1)}, f32[128,128]{0,1:T(8,128)S(1)}, u32[]{:S(2)}, u32[]{:S(2)}) collective-permute-start(f32[128,128]{0,1:T(8,128)S(1)} %add.113), channel_id=1, source_target_pairs={{0,128},{4,132},{8,136},{12,140},{16,144},{20,148},{24,152},{28,15... | collective-permute-start | bytes 196616 | tf_op jit(solution)/shard_map/ppermute | solution.py:17
  101.6 4.8 %collective-permute-start.14 = (f32[128,128]{0,1:T(8,128)S(1)}, f32[128,128]{0,1:T(8,128)S(1)}, u32[]{:S(2)}, u32[]{:S(2)}) collective-permute-start(f32[128,128]{0,1:T(8,128)S(1)} %add.114), channel_id=1, source_target_pairs={{0,1},{1,0},{2,3},{3,2},{4,5},{5,4},{6,7},{7,6},{8,9},{9,8},{10,11... | collective-permute-start | bytes 196616 | tf_op jit(solution)/shard_map/ppermute | solution.py:17
  106.4 6.0 %collective-permute-start.15 = (f32[128,128]{0,1:T(8,128)S(1)}, f32[128,128]{0,1:T(8,128)S(1)}, u32[]{:S(2)}, u32[]{:S(2)}) collective-permute-start(f32[128,128]{0,1:T(8,128)S(1)} %add.115), channel_id=1, source_target_pairs={{0,2},{1,3},{2,0},{3,1},{4,6},{5,7},{6,4},{7,5},{8,10},{9,11},{10,... | collective-permute-start | bytes 196616 | tf_op jit(solution)/shard_map/ppermute | solution.py:17
  112.7 9.7 %copy-start.2 = (f32[96,32]{0,1:T(8,128)}, f32[96,32]{0,1:T(8,128)S(1)}, u32[]{:S(2)}) copy-start(f32[96,32]{0,1:T(8,128)S(1)} %get-tuple-element.24) | copy-start | bytes 36868

commit v2 on v1

--- a/solution.py
+++ b/solution.py
@@ -77,11 +77,14 @@
     share = factor_rows.shape[0]
     margin = from_lower.shape[1]
     row_pos = lax.axis_index("row")
-    global_rows = row_pos * share + lax.iota(jnp.int32, share)
-    columns = lax.iota(jnp.int32, factor_rows.shape[1])
-    full = factor_rows + (global_rows[:, None] == columns[None, :]).astype(jnp.float32)
-    inner = contract_rows(extended, full)
-    partial_value = jnp.dot(inner, full, precision=HIGH)
+    start = row_pos * share
+    inner = lax.dynamic_slice_in_dim(extended, start, share, 1) + lax.dot_general(
+        extended, factor_rows, (((1,), (1,)), ((), ())), precision=lax.Precision.HIGH
+    )
+    product = jnp.dot(inner, factor_rows, precision=lax.Precision.HIGH)
+    partial_value = lax.dynamic_update_slice_in_dim(
+        product, lax.dynamic_slice_in_dim(product, start, share, 1) + inner, start, 1
+    )
     back_upper = from_behind(partial_value[:, sub_rows:sub_rows + margin], "sub", -1)
     back_lower = from_behind(partial_value[:, sub_rows + margin:], "sub", 1)
     all_rows = lax.iota(jnp.int32, sub_rows)

time: 123 us -> 114 us (0.927)
  matrix products: 24.1 us -> 17.6 us
  starting transfers between devices: 40.9 us -> 39.4 us
    dot_general x4 -> x3, matrix products: 12.6 us -> 0.82 us  [contract_rows(): lax.dot_general(left_mat, right_mat, (((1,), (1,)), ((), ())), precision=...]
    dot_general x1 -> x2, matrix products: 6.66 us -> 11.9 us  [the longest x1 8.59 us: per_device(): lax.dot_general(extended, factor_rows, (((1,), (1,)), ((), ())), precisio...]
    ppermute x12, waiting for transfers between devices: 39.1 us -> 40.4 us  [swap(): lax.ppermute(value, axis, [(source, source ^ mask) for source in range(co...]
    ppermute x4, starting transfers between devices: 14 us -> 12.7 us  [from_behind(): lax.ppermute(value, axis, [(source, source + steps) for source in range(l...]
  transfers between devices with their start and end apart: 16 -> 16, of which waited for: 14 -> 14; matrix products, arithmetic and copies ran while one was open for 4% -> 3% of each run, Pallas kernels for 0% -> 0%
where the time goes in v2:
time: 114 us; the launch traced here: 113 us
  waiting for transfers between devices  42.5 us (37%)
  starting transfers between devices  39.4 us (35%)
  matrix products  17.6 us (15%)
  other arithmetic  7.07 us (6%)
  local copies, waits for them, and re-layouts  5.88 us (5%)
    ppermute x12, waiting for transfers between devices, swap(): lax.ppermute(value, axis, [(source, source ^ mask) for source in range(co...  40.4 us
    ppermute x12, starting transfers between devices, swap(): lax.ppermute(value, axis, [(source, source ^ mask) for source in range(co...  26.7 us
    ppermute x4, starting transfers between devices, from_behind(): lax.ppermute(value, axis, [(source, source + steps) for source in range(l...  12.7 us
    dot_general x1, matrix products, per_device(): lax.dot_general(extended, factor_rows, (((1,), (1,)), ((), ())), precisio...  8.59 us
    another operation x3, other arithmetic, per_device(): lower_tri = jnp.linalg.cholesky(gram)  3.6 us
    dot_general x1, matrix products, per_device(): product = jnp.dot(inner, factor_rows, precision=lax.Precision.HIGH)  3.29 us
    another operation x2, other arithmetic, per_device(): solved = jax.scipy.linalg.solve_triangular(lower_tri, twice, lower=True)  3.09 us
  transfers between devices with their start and end apart: 16, of which 14 were waited for; matrix products, arithmetic and copies ran while one was open for 3% of the time, Pallas kernels for 0%

profile of v2, /device:TPU:38, one launch (start us, length us, event | category | flops | bytes accessed | tf_op | source)
XLA Modules:
  0.0 113.5 jit_solution(16172124603108658752)
XLA Ops:
  3.8 1.9 %collective-permute-done = f32[32,512]{1,0:T(8,128)S(1)} collective-permute-done((f32[32,512]{1,0:T(8,128)S(1)}, f32[32,512]{1,0:T(8,128)S(1)}, u32[]{:S(2)}, u32[]{:S(2)}) %collective-permute-start) | collective-permute-done | bytes 65568 | tf_op jit(solution)/shard_map/ppermute | solution.py:17
  5.8 3.3 %collective-permute-start.1 = (f32[32,1024]{1,0:T(8,128)S(1)}, f32[32,1024]{1,0:T(8,128)S(1)}, u32[]{:S(2)}, u32[]{:S(2)}) collective-permute-start(f32[32,1024]{1,0:T(8,128)S(1)} %maximum_select_fusion.1), channel_id=1, source_target_pairs={{0,2},{1,3},{2,0},{3,1},{4,6},{5,7},{6,4},{7,5},{8,10},{9,11},{10,... | collective-permute-start | bytes 393224 | tf_op jit(solution)/shard_map/ppermute | solution.py:17
  9.1 3.3 %collective-permute-done.1 = f32[32,1024]{1,0:T(8,128)S(1)} collective-permute-done((f32[32,1024]{1,0:T(8,128)S(1)}, f32[32,1024]{1,0:T(8,128)S(1)}, u32[]{:S(2)}, u32[]{:S(2)}) %collective-permute-start.1) | collective-permute-done | bytes 131104 | tf_op jit(solution)/shard_map/ppermute | solution.py:17
  13.8 1.9 %collective-permute-start.2 = (f32[32,512]{1,0:T(8,128)S(1)}, f32[32,512]{1,0:T(8,128)S(1)}, u32[]{:S(2)}, u32[]{:S(2)}) collective-permute-start(f32[32,512]{1,0:T(8,128)S(1)} %select_bitcast_fusion.1), channel_id=1, source_target_pairs={{0,4},{4,8},{8,12},{12,16},{16,20},{20,24},{24,28},{28,32},{32,36}... | collective-permute-start | bytes 196616 | tf_op jit(solution)/shard_map/ppermute | solution.py:12
  16.9 3.6 %collective-permute-start.3 = (f32[32,512]{1,0:T(8,128)S(1)}, f32[32,512]{1,0:T(8,128)S(1)}, u32[]{:S(2)}, u32[]{:S(2)}) collective-permute-start(f32[32,512]{1,0:T(8,128)S(1)} %select_bitcast_fusion), channel_id=1, source_target_pairs={{4,0},{8,4},{12,8},{16,12},{20,16},{24,20},{28,24},{32,28},{36,32}... | collective-permute-start | bytes 196616 | tf_op jit(solution)/shard_map/ppermute | solution.py:12
  22.5 8.6 %fusion.2 = f32[32,768]{1,0:T(8,128)S(1)} fusion(f32[1,768,3072]{2,1,0:T(8,128)} %param.7, f32[32,512]{1,0:T(8,128)S(1)} %collective-permute-done.3, f32[32,512]{1,0:T(8,128)S(1)} %collective-permute-done.2, f32[32,2048]{1,0:T(8,128)S(1)} %maximum_select_fusion), kind=kOutput, calls=%fused_computation.4 | convolution fusion | flops 453181440 | bytes 9928704 | tf_op jit(solution)/shard_map/dot_general | solution.py:81
  31.1 3.3 %fusion = f32[32,3072]{1,0:T(8,128)S(1)} fusion(f32[1,768,3072]{2,1,0:T(8,128)S(1)} %copy-done, f32[32,768]{1,0:T(8,128)S(1)} %fusion.2, f32[32,3072]{1,0:T(8,128)S(1)} %pad_maximum_fusion, s32[]{:T(128)S(6)} %select_n.64), kind=kOutput, calls=%fused_computation.2 | convolution fusion | flops 453009408 | bytes 10027012 | tf_op jit(solution)/shard_map/dot_general | solution.py:84
  34.5 5.3 %collective-permute-start.5 = (f32[32,512]{1,0:T(8,128)S(1)}, f32[32,512]{1,0:T(8,128)S(1)}, u32[]{:S(2)}, u32[]{:S(2)}) collective-permute-start(f32[32,512]{1,0:T(8,128)S(1)} %get-tuple-element.14), channel_id=1, source_target_pairs={{0,4},{4,8},{8,12},{12,16},{16,20},{20,24},{24,28},{28,32},{32,36}... | collective-permute-start | bytes 196616 | tf_op jit(solution)/shard_map/ppermute | solution.py:12
  39.8 1.9 %collective-permute-start.4 = (f32[32,512]{1,0:T(8,128)S(1)}, f32[32,512]{1,0:T(8,128)S(1)}, u32[]{:S(2)}, u32[]{:S(2)}) collective-permute-start(f32[32,512]{1,0:T(8,128)S(1)} %get-tuple-element.13), channel_id=1, source_target_pairs={{4,0},{8,4},{12,8},{16,12},{20,16},{24,20},{28,24},{32,28},{36,32}... | collective-permute-start | bytes 196616 | tf_op jit(solution)/shard_map/ppermute | solution.py:12
  45.3 3.3 %collective-permute-start.6 = (f32[32,1024]{1,0:T(8,128)S(1)}, f32[32,1024]{1,0:T(8,128)S(1)}, u32[]{:S(2)}, u32[]{:S(2)}) collective-permute-start(f32[32,1024]{1,0:T(8,128)S(1)} %constant_dynamic-slice_fusion.1), channel_id=1, source_target_pairs={{0,2},{1,3},{2,0},{3,1},{4,6},{5,7},{6,4},{7,5},{8,10},{9,11},{10,... | collective-permute-start | bytes 393224 | tf_op jit(solution)/shard_map/ppermute | solution.py:17
  48.6 3.3 %collective-permute-done.6 = f32[32,1024]{1,0:T(8,128)S(1)} collective-permute-done((f32[32,1024]{1,0:T(8,128)S(1)}, f32[32,1024]{1,0:T(8,128)S(1)}, u32[]{:S(2)}, u32[]{:S(2)}) %collective-permute-start.6) | collective-permute-done | bytes 131104 | tf_op jit(solution)/shard_map/ppermute | solution.py:17
  54.1 2.4 %collective-permute-done.7 = f32[32,512]{1,0:T(8,128)S(1)} collective-permute-done((f32[32,512]{1,0:T(8,128)S(1)}, f32[32,512]{1,0:T(8,128)S(1)}, u32[]{:S(2)}, u32[]{:S(2)}) %collective-permute-start.7) | collective-permute-done | bytes 65568 | tf_op jit(solution)/shard_map/ppermute | solution.py:17
  57.1 2.2 %collective-permute-start.8 = (f32[128,128]{0,1:T(8,128)S(1)}, f32[128,128]{0,1:T(8,128)S(1)}, u32[]{:S(2)}, u32[]{:S(2)}) collective-permute-start(f32[128,128]{0,1:T(8,128)S(1)} %select_maximum_fusion), channel_id=1, source_target_pairs={{0,4},{4,0},{8,12},{12,8},{16,20},{20,16},{24,28},{28,24},{32,36},... | collective-permute-start | bytes 196616 | tf_op jit(solution)/shard_map/ppermute | solution.py:17
  60.4 4.3 %collective-permute-done.9 = f32[128,128]{0,1:T(8,128)S(1)} collective-permute-done((f32[128,128]{0,1:T(8,128)S(1)}, f32[128,128]{0,1:T(8,128)S(1)}, u32[]{:S(2)}, u32[]{:S(2)}) %collective-permute-start.9) | collective-permute-done | bytes 65568 | tf_op jit(solution)/shard_map/ppermute | solution.py:17
  65.5 5.1 %collective-permute-done.10 = f32[128,128]{0,1:T(8,128)S(1)} collective-permute-done((f32[128,128]{0,1:T(8,128)S(1)}, f32[128,128]{0,1:T(8,128)S(1)}, u32[]{:S(2)}, u32[]{:S(2)}) %collective-permute-start.10) | collective-permute-done | bytes 65568 | tf_op jit(solution)/shard_map/ppermute | solution.py:17
  70.8 4.2 %collective-permute-done.11 = f32[128,128]{0,1:T(8,128)S(1)} collective-permute-done((f32[128,128]{0,1:T(8,128)S(1)}, f32[128,128]{0,1:T(8,128)S(1)}, u32[]{:S(2)}, u32[]{:S(2)}) %collective-permute-start.11) | collective-permute-done | bytes 65568 | tf_op jit(solution)/shard_map/ppermute | solution.py:17
  75.0 7.2 %collective-permute-start.12 = (f32[128,128]{0,1:T(8,128)S(1)}, f32[128,128]{0,1:T(8,128)S(1)}, u32[]{:S(2)}, u32[]{:S(2)}) collective-permute-start(f32[128,128]{0,1:T(8,128)S(1)} %add.110), channel_id=1, source_target_pairs={{0,64},{4,68},{8,72},{12,76},{16,80},{20,84},{24,88},{28,92},{32,9... | collective-permute-start | bytes 196616 | tf_op jit(solution)/shard_map/ppermute | solution.py:17
  82.2 2.2 %collective-permute-done.12 = f32[128,128]{0,1:T(8,128)S(1)} collective-permute-done((f32[128,128]{0,1:T(8,128)S(1)}, f32[128,128]{0,1:T(8,128)S(1)}, u32[]{:S(2)}, u32[]{:S(2)}) %collective-permute-start.12) | collective-permute-done | bytes 65568 | tf_op jit(solution)/shard_map/ppermute | solution.py:17
  85.7 7.0 %collective-permute-done.13 = f32[128,128]{0,1:T(8,128)S(1)} collective-permute-done((f32[128,128]{0,1:T(8,128)S(1)}, f32[128,128]{0,1:T(8,128)S(1)}, u32[]{:S(2)}, u32[]{:S(2)}) %collective-permute-start.13) | collective-permute-done | bytes 65568 | tf_op jit(solution)/shard_map/ppermute | solution.py:17
  94.1 3.5 %collective-permute-done.14 = f32[128,128]{0,1:T(8,128)S(1)} collective-permute-done((f32[128,128]{0,1:T(8,128)S(1)}, f32[128,128]{0,1:T(8,128)S(1)}, u32[]{:S(2)}, u32[]{:S(2)}) %collective-permute-start.14) | collective-permute-done | bytes 65568 | tf_op jit(solution)/shard_map/ppermute | solution.py:17
  97.7 3.6 %collective-permute-start.15 = (f32[128,128]{0,1:T(8,128)S(1)}, f32[128,128]{0,1:T(8,128)S(1)}, u32[]{:S(2)}, u32[]{:S(2)}) collective-permute-start(f32[128,128]{0,1:T(8,128)S(1)} %add.113), channel_id=1, source_target_pairs={{0,2},{1,3},{2,0},{3,1},{4,6},{5,7},{6,4},{7,5},{8,10},{9,11},{10,... | collective-permute-start | bytes 196616 | tf_op jit(solution)/shard_map/ppermute | solution.py:17
  101.3 2.3 %collective-permute-done.15 = f32[128,128]{0,1:T(8,128)S(1)} collective-permute-done((f32[128,128]{0,1:T(8,128)S(1)}, f32[128,128]{0,1:T(8,128)S(1)}, u32[]{:S(2)}, u32[]{:S(2)}) %collective-permute-start.15) | collective-permute-done | bytes 65568 | tf_op jit(solution)/shard_map/ppermute | solution.py:17
  105.1 2.9 %cholesky.18 = f32[32,32]{1,0:T(8,128)S(1)} custom-call(f32[32,32]{1,0:T(8,128)S(1)} %fusion.23), custom_call_target="Cholesky" | custom-call | tf_op jit(solution)/shard_map/jit(cholesky)/cholesky | solution.py:124
  109.4 2.4 %custom-call.7 = f32[1,32,32]{1,2,0:T(8,128)S(1)} custom-call(f32[1,32,32]{2,1,0:T(8,128)S(1)} %get-tuple-element.15), custom_call_target="InvertDiagBlocksLowerTriangular" | custom-call | tf_op jit(solution)/shard_map/jit(_solve_triangular)/triangular_solve | solution.py:125
  (72 shorter events, 23.4 us)
Async XLA Ops:
  1.5 4.3 %collective-permute-start = (f32[32,512]{1,0:T(8,128)S(1)}, f32[32,512]{1,0:T(8,128)S(1)}, u32[]{:S(2)}, u32[]{:S(2)}) collective-permute-start(f32[32,512]{1,0:T(8,128)S(1)} %bitcast.58), channel_id=1, source_target_pairs={{0,1},{1,0},{2,3},{3,2},{4,5},{5,4},{6,7},{7,6},{8,9},{9,8},{10,11... | collective-permute-start | bytes 196616 | tf_op jit(solution)/shard_map/ppermute | solution.py:17
  5.8 6.6 %collective-permute-start.1 = (f32[32,1024]{1,0:T(8,128)S(1)}, f32[32,1024]{1,0:T(8,128)S(1)}, u32[]{:S(2)}, u32[]{:S(2)}) collective-permute-start(f32[32,1024]{1,0:T(8,128)S(1)} %maximum_select_fusion.1), channel_id=1, source_target_pairs={{0,2},{1,3},{2,0},{3,1},{4,6},{5,7},{6,4},{7,5},{8,10},{9,11},{10,... | collective-permute-start | bytes 393224 | tf_op jit(solution)/shard_map/ppermute | solution.py:17
  13.8 6.8 %collective-permute-start.2 = (f32[32,512]{1,0:T(8,128)S(1)}, f32[32,512]{1,0:T(8,128)S(1)}, u32[]{:S(2)}, u32[]{:S(2)}) collective-permute-start(f32[32,512]{1,0:T(8,128)S(1)} %select_bitcast_fusion.1), channel_id=1, source_target_pairs={{0,4},{4,8},{8,12},{12,16},{16,20},{20,24},{24,28},{28,32},{32,36}... | collective-permute-start | bytes 196616 | tf_op jit(solution)/shard_map/ppermute | solution.py:12
  16.9 5.5 %collective-permute-start.3 = (f32[32,512]{1,0:T(8,128)S(1)}, f32[32,512]{1,0:T(8,128)S(1)}, u32[]{:S(2)}, u32[]{:S(2)}) collective-permute-start(f32[32,512]{1,0:T(8,128)S(1)} %select_bitcast_fusion), channel_id=1, source_target_pairs={{4,0},{8,4},{12,8},{16,12},{20,16},{24,20},{28,24},{32,28},{36,32}... | collective-permute-start | bytes 196616 | tf_op jit(solution)/shard_map/ppermute | solution.py:12
  20.6 10.5 %copy-start = (f32[1,768,3072]{2,1,0:T(8,128)S(1)}, f32[1,768,3072]{2,1,0:T(8,128)}, u32[]{:S(2)}) copy-start(f32[1,768,3072]{2,1,0:T(8,128)} %param.7) | copy-start | bytes 28311556
  31.1 22.6 %copy-start.1 = (f32[96,1,512]{2,1,0:T(1,128)S(1)}, f32[96,1,512]{2,1,0:T(1,128)}, u32[]{:S(2)}) copy-start(f32[96,1,512]{2,1,0:T(1,128)} %param.8) | copy-start | bytes 589828
  34.5 7.2 %collective-permute-start.5 = (f32[32,512]{1,0:T(8,128)S(1)}, f32[32,512]{1,0:T(8,128)S(1)}, u32[]{:S(2)}, u32[]{:S(2)}) collective-permute-start(f32[32,512]{1,0:T(8,128)S(1)} %get-tuple-element.14), channel_id=1, source_target_pairs={{0,4},{4,8},{8,12},{12,16},{16,20},{20,24},{24,28},{28,32},{32,36}... | collective-permute-start | bytes 196616 | tf_op jit(solution)/shard_map/ppermute | solution.py:12
  39.8 3.8 %collective-permute-start.4 = (f32[32,512]{1,0:T(8,128)S(1)}, f32[32,512]{1,0:T(8,128)S(1)}, u32[]{:S(2)}, u32[]{:S(2)}) collective-permute-start(f32[32,512]{1,0:T(8,128)S(1)} %get-tuple-element.13), channel_id=1, source_target_pairs={{4,0},{8,4},{12,8},{16,12},{20,16},{24,20},{28,24},{32,28},{36,32}... | collective-permute-start | bytes 196616 | tf_op jit(solution)/shard_map/ppermute | solution.py:12
  45.3 6.6 %collective-permute-start.6 = (f32[32,1024]{1,0:T(8,128)S(1)}, f32[32,1024]{1,0:T(8,128)S(1)}, u32[]{:S(2)}, u32[]{:S(2)}) collective-permute-start(f32[32,1024]{1,0:T(8,128)S(1)} %constant_dynamic-slice_fusion.1), channel_id=1, source_target_pairs={{0,2},{1,3},{2,0},{3,1},{4,6},{5,7},{6,4},{7,5},{8,10},{9,11},{10,... | collective-permute-start | bytes 393224 | tf_op jit(solution)/shard_map/ppermute | solution.py:17
  51.9 4.6 %collective-permute-start.7 = (f32[32,512]{1,0:T(8,128)S(1)}, f32[32,512]{1,0:T(8,128)S(1)}, u32[]{:S(2)}, u32[]{:S(2)}) collective-permute-start(f32[32,512]{1,0:T(8,128)S(1)} %constant_dynamic-slice_fusion), channel_id=1, source_target_pairs={{0,1},{1,0},{2,3},{3,2},{4,5},{5,4},{6,7},{7,6},{8,9},{9,8},{10,11... | collective-permute-start | bytes 196616 | tf_op jit(solution)/shard_map/ppermute | solution.py:17
  57.1 3.1 %collective-permute-start.8 = (f32[128,128]{0,1:T(8,128)S(1)}, f32[128,128]{0,1:T(8,128)S(1)}, u32[]{:S(2)}, u32[]{:S(2)}) collective-permute-start(f32[128,128]{0,1:T(8,128)S(1)} %select_maximum_fusion), channel_id=1, source_target_pairs={{0,4},{4,0},{8,12},{12,8},{16,20},{20,16},{24,28},{28,24},{32,36},... | collective-permute-start | bytes 196616 | tf_op jit(solution)/shard_map/ppermute | solution.py:17
  60.3 4.4 %collective-permute-start.9 = (f32[128,128]{0,1:T(8,128)S(1)}, f32[128,128]{0,1:T(8,128)S(1)}, u32[]{:S(2)}, u32[]{:S(2)}) collective-permute-start(f32[128,128]{0,1:T(8,128)S(1)} %fusion.48), channel_id=1, source_target_pairs={{0,8},{4,12},{8,0},{12,4},{16,24},{20,28},{24,16},{28,20},{32,40},... | collective-permute-start | bytes 196616 | tf_op jit(solution)/shard_map/ppermute | solution.py:17
  64.7 5.9 %collective-permute-start.10 = (f32[128,128]{0,1:T(8,128)S(1)}, f32[128,128]{0,1:T(8,128)S(1)}, u32[]{:S(2)}, u32[]{:S(2)}) collective-permute-start(f32[128,128]{0,1:T(8,128)S(1)} %add.108), channel_id=1, source_target_pairs={{0,16},{4,20},{8,24},{12,28},{16,0},{20,4},{24,8},{28,12},{32,48},... | collective-permute-start | bytes 196616 | tf_op jit(solution)/shard_map/ppermute | solution.py:17
  70.6 4.4 %collective-permute-start.11 = (f32[128,128]{0,1:T(8,128)S(1)}, f32[128,128]{0,1:T(8,128)S(1)}, u32[]{:S(2)}, u32[]{:S(2)}) collective-permute-start(f32[128,128]{0,1:T(8,128)S(1)} %add.109), channel_id=1, source_target_pairs={{0,32},{4,36},{8,40},{12,44},{16,48},{20,52},{24,56},{28,60},{32,0... | collective-permute-start | bytes 196616 | tf_op jit(solution)/shard_map/ppermute | solution.py:17
  75.0 9.4 %collective-permute-start.12 = (f32[128,128]{0,1:T(8,128)S(1)}, f32[128,128]{0,1:T(8,128)S(1)}, u32[]{:S(2)}, u32[]{:S(2)}) collective-permute-start(f32[128,128]{0,1:T(8,128)S(1)} %add.110), channel_id=1, source_target_pairs={{0,64},{4,68},{8,72},{12,76},{16,80},{20,84},{24,88},{28,92},{32,9... | collective-permute-start | bytes 196616 | tf_op jit(solution)/shard_map/ppermute | solution.py:17
  84.4 8.3 %collective-permute-start.13 = (f32[128,128]{0,1:T(8,128)S(1)}, f32[128,128]{0,1:T(8,128)S(1)}, u32[]{:S(2)}, u32[]{:S(2)}) collective-permute-start(f32[128,128]{0,1:T(8,128)S(1)} %add.111), channel_id=1, source_target_pairs={{0,128},{4,132},{8,136},{12,140},{16,144},{20,148},{24,152},{28,15... | collective-permute-start | bytes 196616 | tf_op jit(solution)/shard_map/ppermute | solution.py:17
  92.7 5.0 %collective-permute-start.14 = (f32[128,128]{0,1:T(8,128)S(1)}, f32[128,128]{0,1:T(8,128)S(1)}, u32[]{:S(2)}, u32[]{:S(2)}) collective-permute-start(f32[128,128]{0,1:T(8,128)S(1)} %add.112), channel_id=1, source_target_pairs={{0,1},{1,0},{2,3},{3,2},{4,5},{5,4},{6,7},{7,6},{8,9},{9,8},{10,11... | collective-permute-start | bytes 196616 | tf_op jit(solution)/shard_map/ppermute | solution.py:17
  97.7 5.9 %collective-permute-start.15 = (f32[128,128]{0,1:T(8,128)S(1)}, f32[128,128]{0,1:T(8,128)S(1)}, u32[]{:S(2)}, u32[]{:S(2)}) collective-permute-start(f32[128,128]{0,1:T(8,128)S(1)} %add.113), channel_id=1, source_target_pairs={{0,2},{1,3},{2,0},{3,1},{4,6},{5,7},{6,4},{7,5},{8,10},{9,11},{10,... | collective-permute-start | bytes 196616 | tf_op jit(solution)/shard_map/ppermute | solution.py:17
  103.8 9.7 %copy-start.2 = (f32[96,32]{0,1:T(8,128)}, f32[96,32]{0,1:T(8,128)S(1)}, u32[]{:S(2)}) copy-start(f32[96,32]{0,1:T(8,128)S(1)} %get-tuple-element.19) | copy-start | bytes 36868

commit v3 on v2

--- a/solution.py
+++ b/solution.py
@@ -25,38 +25,43 @@
     return lax.dot_general(left_mat, right_mat, (((0,), (0,)), ((), ())), precision=HIGH)
 
 
+def ring_masks(size):
+    near = {2: [1], 4: [1, 3], 8: [1, 2, 6]}
+    masks = near.get(size) or [1 << b for b in range(size.bit_length() - 1)]
+    return [(1 << b, mask) for b, mask in enumerate(masks)]
+
+
 def gather_rows(own, axis):
     pos = lax.axis_index(axis)
     block = own
-    step = 1
-    while step < lax.axis_size(axis):
-        other = swap(block, axis, step)
+    for step, mask in ring_masks(lax.axis_size(axis)):
+        other = swap(block, axis, mask)
         upper = (pos & step) != 0
         block = jnp.where(upper, jnp.concatenate([other, block], axis=1), jnp.concatenate([block, other], axis=1))
-        step *= 2
     return block
 
 
 def scatter_rows(value, axis):
     pos = lax.axis_index(axis)
-    step = lax.axis_size(axis) // 2
     block = value
-    while step >= 1:
+    for step, mask in reversed(ring_masks(lax.axis_size(axis))):
         half = block.shape[1] // 2
         upper = ((pos // step) % 2).astype(jnp.int32)
         keep = lax.dynamic_slice_in_dim(block, upper * half, half, 1)
         send = lax.dynamic_slice_in_dim(block, (1 - upper) * half, half, 1)
-        block = keep + swap(send, axis, step)
-        step //= 2
+        block = keep + swap(send, axis, mask)
     return block
 
 
 def all_sum(value, axes):
-    for axis in axes:
-        step = 1
-        while step < lax.axis_size(axis):
-            value = value + swap(value, axis, step)
-            step *= 2
+    for axis, rings in axes:
+        masks = [0]
+        scale = 1
+        for ring in rings:
+            masks += [mask * scale for _, mask in ring_masks(ring)]
+            scale *= ring
+        for mask in masks[1:]:
+            value = value + swap(value, axis, mask)
     return value
 
 
@@ -109,7 +114,7 @@
         ],
         axis=0,
     )
-    summed = all_sum(packed, ("sub", "row"))
+    summed = all_sum(packed, (("sub", (2, 4, lax.axis_size("sub") // 8)), ("row", (row_count,))))
     first, basis_gram, block_gram = lax.optimization_barrier(
         (summed[:count, :vecs], summed[:count, vecs:], summed[count:, :vecs])
     )

time: 114 us -> 110 us (0.965)
  starting transfers between devices: 39.4 us -> 35 us
    ppermute x12, starting transfers between devices: 26.7 us -> 22.2 us  [swap(): lax.ppermute(value, axis, [(source, source ^ mask) for source in range(co...]
  transfers between devices with their start and end apart: 16 -> 16, of which waited for: 14 -> 14; matrix products, arithmetic and copies ran while one was open for 3% -> 4% of each run, Pallas kernels for 0% -> 0%
where the time goes in v3:
time: 110 us
  waiting for transfers between devices  43.4 us (39%)
  starting transfers between devices  35 us (32%)
  matrix products  17.6 us (16%)
  other arithmetic  7.07 us (6%)
  local copies, waits for them, and re-layouts  5.88 us (5%)
    ppermute x12, waiting for transfers between devices, swap(): lax.ppermute(value, axis, [(source, source ^ mask) for source in range(co...  41.3 us
    ppermute x12, starting transfers between devices, swap(): lax.ppermute(value, axis, [(source, source ^ mask) for source in range(co...  22.2 us
    ppermute x4, starting transfers between devices, from_behind(): lax.ppermute(value, axis, [(source, source + steps) for source in range(l...  12.7 us
    dot_general x1, matrix products, per_device(): lax.dot_general(extended, factor_rows, (((1,), (1,)), ((), ())), precisio...  8.59 us
    another operation x3, other arithmetic, per_device(): lower_tri = jnp.linalg.cholesky(gram)  3.6 us
    dot_general x1, matrix products, per_device(): product = jnp.dot(inner, factor_rows, precision=lax.Precision.HIGH)  3.3 us
    another operation x2, other arithmetic, per_device(): solved = jax.scipy.linalg.solve_triangular(lower_tri, twice, lower=True)  3.09 us
    unnamed x9, local copies, waits for them, and re-layouts  2.24 us
  transfers between devices with their start and end apart: 16, of which 14 were waited for; matrix products, arithmetic and copies ran while one was open for 4% of the time, Pallas kernels for 0%

profile of v3, /device:TPU:38, one launch (start us, length us, event | category | flops | bytes accessed | tf_op | source)
XLA Modules:
  0.0 110.0 jit_solution(15459370099198335515)
XLA Ops:
  3.8 1.9 %collective-permute-done = f32[32,512]{1,0:T(8,128)S(1)} collective-permute-done((f32[32,512]{1,0:T(8,128)S(1)}, f32[32,512]{1,0:T(8,128)S(1)}, u32[]{:S(2)}, u32[]{:S(2)}) %collective-permute-start) | collective-permute-done | bytes 65568 | tf_op jit(solution)/shard_map/ppermute | solution.py:17
  5.8 3.1 %collective-permute-start.1 = (f32[32,1024]{1,0:T(8,128)S(1)}, f32[32,1024]{1,0:T(8,128)S(1)}, u32[]{:S(2)}, u32[]{:S(2)}) collective-permute-start(f32[32,1024]{1,0:T(8,128)S(1)} %maximum_select_fusion.1), channel_id=1, source_target_pairs={{0,3},{1,2},{2,1},{3,0},{4,7},{5,6},{6,5},{7,4},{8,11},{9,10},{10,... | collective-permute-start | bytes 393224 | tf_op jit(solution)/shard_map/ppermute | solution.py:17
  8.9 3.1 %collective-permute-done.1 = f32[32,1024]{1,0:T(8,128)S(1)} collective-permute-done((f32[32,1024]{1,0:T(8,128)S(1)}, f32[32,1024]{1,0:T(8,128)S(1)}, u32[]{:S(2)}, u32[]{:S(2)}) %collective-permute-start.1) | collective-permute-done | bytes 131104 | tf_op jit(solution)/shard_map/ppermute | solution.py:17
  13.6 1.9 %collective-permute-start.2 = (f32[32,512]{1,0:T(8,128)S(1)}, f32[32,512]{1,0:T(8,128)S(1)}, u32[]{:S(2)}, u32[]{:S(2)}) collective-permute-start(f32[32,512]{1,0:T(8,128)S(1)} %select_bitcast_fusion.1), channel_id=1, source_target_pairs={{0,4},{4,8},{8,12},{12,16},{16,20},{20,24},{24,28},{28,32},{32,36}... | collective-permute-start | bytes 196616 | tf_op jit(solution)/shard_map/ppermute | solution.py:12
  16.6 3.6 %collective-permute-start.3 = (f32[32,512]{1,0:T(8,128)S(1)}, f32[32,512]{1,0:T(8,128)S(1)}, u32[]{:S(2)}, u32[]{:S(2)}) collective-permute-start(f32[32,512]{1,0:T(8,128)S(1)} %select_bitcast_fusion), channel_id=1, source_target_pairs={{4,0},{8,4},{12,8},{16,12},{20,16},{24,20},{28,24},{32,28},{36,32}... | collective-permute-start | bytes 196616 | tf_op jit(solution)/shard_map/ppermute | solution.py:12
  22.2 8.6 %fusion.2 = f32[32,768]{1,0:T(8,128)S(1)} fusion(f32[1,768,3072]{2,1,0:T(8,128)} %param.7, f32[32,512]{1,0:T(8,128)S(1)} %collective-permute-done.3, f32[32,512]{1,0:T(8,128)S(1)} %collective-permute-done.2, f32[32,2048]{1,0:T(8,128)S(1)} %maximum_select_fusion), kind=kOutput, calls=%fused_computation.4 | convolution fusion | flops 453181440 | bytes 9928704 | tf_op jit(solution)/shard_map/dot_general | solution.py:86
  30.8 3.3 %fusion = f32[32,3072]{1,0:T(8,128)S(1)} fusion(f32[1,768,3072]{2,1,0:T(8,128)S(1)} %copy-done, f32[32,768]{1,0:T(8,128)S(1)} %fusion.2, f32[32,3072]{1,0:T(8,128)S(1)} %pad_maximum_fusion, s32[]{:T(128)S(6)} %select_n.64), kind=kOutput, calls=%fused_computation.2 | convolution fusion | flops 453009408 | bytes 10027012 | tf_op jit(solution)/shard_map/dot_general | solution.py:89
  34.2 5.3 %collective-permute-start.5 = (f32[32,512]{1,0:T(8,128)S(1)}, f32[32,512]{1,0:T(8,128)S(1)}, u32[]{:S(2)}, u32[]{:S(2)}) collective-permute-start(f32[32,512]{1,0:T(8,128)S(1)} %get-tuple-element.14), channel_id=1, source_target_pairs={{0,4},{4,8},{8,12},{12,16},{16,20},{20,24},{24,28},{28,32},{32,36}... | collective-permute-start | bytes 196616 | tf_op jit(solution)/shard_map/ppermute | solution.py:12
  39.5 1.9 %collective-permute-start.4 = (f32[32,512]{1,0:T(8,128)S(1)}, f32[32,512]{1,0:T(8,128)S(1)}, u32[]{:S(2)}, u32[]{:S(2)}) collective-permute-start(f32[32,512]{1,0:T(8,128)S(1)} %get-tuple-element.13), channel_id=1, source_target_pairs={{4,0},{8,4},{12,8},{16,12},{20,16},{24,20},{28,24},{32,28},{36,32}... | collective-permute-start | bytes 196616 | tf_op jit(solution)/shard_map/ppermute | solution.py:12
  45.0 3.1 %collective-permute-start.6 = (f32[32,1024]{1,0:T(8,128)S(1)}, f32[32,1024]{1,0:T(8,128)S(1)}, u32[]{:S(2)}, u32[]{:S(2)}) collective-permute-start(f32[32,1024]{1,0:T(8,128)S(1)} %constant_dynamic-slice_fusion.1), channel_id=1, source_target_pairs={{0,3},{1,2},{2,1},{3,0},{4,7},{5,6},{6,5},{7,4},{8,11},{9,10},{10,... | collective-permute-start | bytes 393224 | tf_op jit(solution)/shard_map/ppermute | solution.py:17
  48.1 3.2 %collective-permute-done.6 = f32[32,1024]{1,0:T(8,128)S(1)} collective-permute-done((f32[32,1024]{1,0:T(8,128)S(1)}, f32[32,1024]{1,0:T(8,128)S(1)}, u32[]{:S(2)}, u32[]{:S(2)}) %collective-permute-start.6) | collective-permute-done | bytes 131104 | tf_op jit(solution)/shard_map/ppermute | solution.py:17
  51.9 3.9 %collective-permute-done.7 = f32[32,512]{1,0:T(8,128)S(1)} collective-permute-done((f32[32,512]{1,0:T(8,128)S(1)}, f32[32,512]{1,0:T(8,128)S(1)}, u32[]{:S(2)}, u32[]{:S(2)}) %collective-permute-start.7) | collective-permute-done | bytes 65568 | tf_op jit(solution)/shard_map/ppermute | solution.py:17
  56.4 2.4 %collective-permute-start.8 = (f32[128,128]{0,1:T(8,128)S(1)}, f32[128,128]{0,1:T(8,128)S(1)}, u32[]{:S(2)}, u32[]{:S(2)}) collective-permute-start(f32[128,128]{0,1:T(8,128)S(1)} %select_maximum_fusion), channel_id=1, source_target_pairs={{0,4},{4,0},{8,12},{12,8},{16,20},{20,16},{24,28},{28,24},{32,36},... | collective-permute-start | bytes 196616 | tf_op jit(solution)/shard_map/ppermute | solution.py:17
  59.9 4.3 %collective-permute-done.9 = f32[128,128]{0,1:T(8,128)S(1)} collective-permute-done((f32[128,128]{0,1:T(8,128)S(1)}, f32[128,128]{0,1:T(8,128)S(1)}, u32[]{:S(2)}, u32[]{:S(2)}) %collective-permute-start.9) | collective-permute-done | bytes 65568 | tf_op jit(solution)/shard_map/ppermute | solution.py:17
  65.3 4.5 %collective-permute-done.10 = f32[128,128]{0,1:T(8,128)S(1)} collective-permute-done((f32[128,128]{0,1:T(8,128)S(1)}, f32[128,128]{0,1:T(8,128)S(1)}, u32[]{:S(2)}, u32[]{:S(2)}) %collective-permute-start.10) | collective-permute-done | bytes 65568 | tf_op jit(solution)/shard_map/ppermute | solution.py:17
  70.0 4.2 %collective-permute-done.11 = f32[128,128]{0,1:T(8,128)S(1)} collective-permute-done((f32[128,128]{0,1:T(8,128)S(1)}, f32[128,128]{0,1:T(8,128)S(1)}, u32[]{:S(2)}, u32[]{:S(2)}) %collective-permute-start.11) | collective-permute-done | bytes 65568 | tf_op jit(solution)/shard_map/ppermute | solution.py:17
  74.2 7.0 %collective-permute-start.12 = (f32[128,128]{0,1:T(8,128)S(1)}, f32[128,128]{0,1:T(8,128)S(1)}, u32[]{:S(2)}, u32[]{:S(2)}) collective-permute-start(f32[128,128]{0,1:T(8,128)S(1)} %add.110), channel_id=1, source_target_pairs={{0,64},{4,68},{8,72},{12,76},{16,80},{20,84},{24,88},{28,92},{32,9... | collective-permute-start | bytes 196616 | tf_op jit(solution)/shard_map/ppermute | solution.py:17
  81.1 2.2 %collective-permute-done.12 = f32[128,128]{0,1:T(8,128)S(1)} collective-permute-done((f32[128,128]{0,1:T(8,128)S(1)}, f32[128,128]{0,1:T(8,128)S(1)}, u32[]{:S(2)}, u32[]{:S(2)}) %collective-permute-start.12) | collective-permute-done | bytes 65568 | tf_op jit(solution)/shard_map/ppermute | solution.py:17
  83.5 6.6 %collective-permute-done.13 = f32[128,128]{0,1:T(8,128)S(1)} collective-permute-done((f32[128,128]{0,1:T(8,128)S(1)}, f32[128,128]{0,1:T(8,128)S(1)}, u32[]{:S(2)}, u32[]{:S(2)}) %collective-permute-start.13) | collective-permute-done | bytes 65568 | tf_op jit(solution)/shard_map/ppermute | solution.py:17
  90.5 4.0 %collective-permute-done.14 = f32[128,128]{0,1:T(8,128)S(1)} collective-permute-done((f32[128,128]{0,1:T(8,128)S(1)}, f32[128,128]{0,1:T(8,128)S(1)}, u32[]{:S(2)}, u32[]{:S(2)}) %collective-permute-start.14) | collective-permute-done | bytes 65568 | tf_op jit(solution)/shard_map/ppermute | solution.py:17
  94.5 3.0 %collective-permute-start.15 = (f32[128,128]{0,1:T(8,128)S(1)}, f32[128,128]{0,1:T(8,128)S(1)}, u32[]{:S(2)}, u32[]{:S(2)}) collective-permute-start(f32[128,128]{0,1:T(8,128)S(1)} %add.113), channel_id=1, source_target_pairs={{0,3},{1,2},{2,1},{3,0},{4,7},{5,6},{6,5},{7,4},{8,11},{9,10},{10,... | collective-permute-start | bytes 196616 | tf_op jit(solution)/shard_map/ppermute | solution.py:17
  97.5 2.5 %collective-permute-done.15 = f32[128,128]{0,1:T(8,128)S(1)} collective-permute-done((f32[128,128]{0,1:T(8,128)S(1)}, f32[128,128]{0,1:T(8,128)S(1)}, u32[]{:S(2)}, u32[]{:S(2)}) %collective-permute-start.15) | collective-permute-done | bytes 65568 | tf_op jit(solution)/shard_map/ppermute | solution.py:17
  101.6 2.9 %cholesky.18 = f32[32,32]{1,0:T(8,128)S(1)} custom-call(f32[32,32]{1,0:T(8,128)S(1)} %fusion.23), custom_call_target="Cholesky" | custom-call | tf_op jit(solution)/shard_map/jit(cholesky)/cholesky | solution.py:129
  105.9 2.4 %custom-call.7 = f32[1,32,32]{1,2,0:T(8,128)S(1)} custom-call(f32[1,32,32]{2,1,0:T(8,128)S(1)} %get-tuple-element.15), custom_call_target="InvertDiagBlocksLowerTriangular" | custom-call | tf_op jit(solution)/shard_map/jit(_solve_triangular)/triangular_solve | solution.py:130
  (72 shorter events, 19.9 us)
Async XLA Ops:
  1.5 4.3 %collective-permute-start = (f32[32,512]{1,0:T(8,128)S(1)}, f32[32,512]{1,0:T(8,128)S(1)}, u32[]{:S(2)}, u32[]{:S(2)}) collective-permute-start(f32[32,512]{1,0:T(8,128)S(1)} %bitcast.58), channel_id=1, source_target_pairs={{0,1},{1,0},{2,3},{3,2},{4,5},{5,4},{6,7},{7,6},{8,9},{9,8},{10,11... | collective-permute-start | bytes 196616 | tf_op jit(solution)/shard_map/ppermute | solution.py:17
  5.8 6.3 %collective-permute-start.1 = (f32[32,1024]{1,0:T(8,128)S(1)}, f32[32,1024]{1,0:T(8,128)S(1)}, u32[]{:S(2)}, u32[]{:S(2)}) collective-permute-start(f32[32,1024]{1,0:T(8,128)S(1)} %maximum_select_fusion.1), channel_id=1, source_target_pairs={{0,3},{1,2},{2,1},{3,0},{4,7},{5,6},{6,5},{7,4},{8,11},{9,10},{10,... | collective-permute-start | bytes 393224 | tf_op jit(solution)/shard_map/ppermute | solution.py:17
  13.6 6.8 %collective-permute-start.2 = (f32[32,512]{1,0:T(8,128)S(1)}, f32[32,512]{1,0:T(8,128)S(1)}, u32[]{:S(2)}, u32[]{:S(2)}) collective-permute-start(f32[32,512]{1,0:T(8,128)S(1)} %select_bitcast_fusion.1), channel_id=1, source_target_pairs={{0,4},{4,8},{8,12},{12,16},{16,20},{20,24},{24,28},{28,32},{32,36}... | collective-permute-start | bytes 196616 | tf_op jit(solution)/shard_map/ppermute | solution.py:12
  16.6 5.5 %collective-permute-start.3 = (f32[32,512]{1,0:T(8,128)S(1)}, f32[32,512]{1,0:T(8,128)S(1)}, u32[]{:S(2)}, u32[]{:S(2)}) collective-permute-start(f32[32,512]{1,0:T(8,128)S(1)} %select_bitcast_fusion), channel_id=1, source_target_pairs={{4,0},{8,4},{12,8},{16,12},{20,16},{24,20},{28,24},{32,28},{36,32}... | collective-permute-start | bytes 196616 | tf_op jit(solution)/shard_map/ppermute | solution.py:12
  20.3 10.5 %copy-start = (f32[1,768,3072]{2,1,0:T(8,128)S(1)}, f32[1,768,3072]{2,1,0:T(8,128)}, u32[]{:S(2)}) copy-start(f32[1,768,3072]{2,1,0:T(8,128)} %param.7) | copy-start | bytes 28311556
  30.8 20.8 %copy-start.1 = (f32[96,1,512]{2,1,0:T(1,128)S(1)}, f32[96,1,512]{2,1,0:T(1,128)}, u32[]{:S(2)}) copy-start(f32[96,1,512]{2,1,0:T(1,128)} %param.8) | copy-start | bytes 589828
  34.2 7.2 %collective-permute-start.5 = (f32[32,512]{1,0:T(8,128)S(1)}, f32[32,512]{1,0:T(8,128)S(1)}, u32[]{:S(2)}, u32[]{:S(2)}) collective-permute-start(f32[32,512]{1,0:T(8,128)S(1)} %get-tuple-element.14), channel_id=1, source_target_pairs={{0,4},{4,8},{8,12},{12,16},{16,20},{20,24},{24,28},{28,32},{32,36}... | collective-permute-start | bytes 196616 | tf_op jit(solution)/shard_map/ppermute | solution.py:12
  39.5 3.8 %collective-permute-start.4 = (f32[32,512]{1,0:T(8,128)S(1)}, f32[32,512]{1,0:T(8,128)S(1)}, u32[]{:S(2)}, u32[]{:S(2)}) collective-permute-start(f32[32,512]{1,0:T(8,128)S(1)} %get-tuple-element.13), channel_id=1, source_target_pairs={{4,0},{8,4},{12,8},{16,12},{20,16},{24,20},{28,24},{32,28},{36,32}... | collective-permute-start | bytes 196616 | tf_op jit(solution)/shard_map/ppermute | solution.py:12
  45.0 6.3 %collective-permute-start.6 = (f32[32,1024]{1,0:T(8,128)S(1)}, f32[32,1024]{1,0:T(8,128)S(1)}, u32[]{:S(2)}, u32[]{:S(2)}) collective-permute-start(f32[32,1024]{1,0:T(8,128)S(1)} %constant_dynamic-slice_fusion.1), channel_id=1, source_target_pairs={{0,3},{1,2},{2,1},{3,0},{4,7},{5,6},{6,5},{7,4},{8,11},{9,10},{10,... | collective-permute-start | bytes 393224 | tf_op jit(solution)/shard_map/ppermute | solution.py:17
  51.3 4.5 %collective-permute-start.7 = (f32[32,512]{1,0:T(8,128)S(1)}, f32[32,512]{1,0:T(8,128)S(1)}, u32[]{:S(2)}, u32[]{:S(2)}) collective-permute-start(f32[32,512]{1,0:T(8,128)S(1)} %constant_dynamic-slice_fusion), channel_id=1, source_target_pairs={{0,1},{1,0},{2,3},{3,2},{4,5},{5,4},{6,7},{7,6},{8,9},{9,8},{10,11... | collective-permute-start | bytes 196616 | tf_op jit(solution)/shard_map/ppermute | solution.py:17
  56.4 3.3 %collective-permute-start.8 = (f32[128,128]{0,1:T(8,128)S(1)}, f32[128,128]{0,1:T(8,128)S(1)}, u32[]{:S(2)}, u32[]{:S(2)}) collective-permute-start(f32[128,128]{0,1:T(8,128)S(1)} %select_maximum_fusion), channel_id=1, source_target_pairs={{0,4},{4,0},{8,12},{12,8},{16,20},{20,16},{24,28},{28,24},{32,36},... | collective-permute-start | bytes 196616 | tf_op jit(solution)/shard_map/ppermute | solution.py:17
  59.8 4.4 %collective-permute-start.9 = (f32[128,128]{0,1:T(8,128)S(1)}, f32[128,128]{0,1:T(8,128)S(1)}, u32[]{:S(2)}, u32[]{:S(2)}) collective-permute-start(f32[128,128]{0,1:T(8,128)S(1)} %fusion.48), channel_id=1, source_target_pairs={{0,8},{4,12},{8,0},{12,4},{16,24},{20,28},{24,16},{28,20},{32,40},... | collective-permute-start | bytes 196616 | tf_op jit(solution)/shard_map/ppermute | solution.py:17
  64.2 5.6 %collective-permute-start.10 = (f32[128,128]{0,1:T(8,128)S(1)}, f32[128,128]{0,1:T(8,128)S(1)}, u32[]{:S(2)}, u32[]{:S(2)}) collective-permute-start(f32[128,128]{0,1:T(8,128)S(1)} %add.108), channel_id=1, source_target_pairs={{0,24},{4,28},{8,16},{12,20},{16,8},{20,12},{24,0},{28,4},{32,56},... | collective-permute-start | bytes 196616 | tf_op jit(solution)/shard_map/ppermute | solution.py:17
  69.8 4.4 %collective-permute-start.11 = (f32[128,128]{0,1:T(8,128)S(1)}, f32[128,128]{0,1:T(8,128)S(1)}, u32[]{:S(2)}, u32[]{:S(2)}) collective-permute-start(f32[128,128]{0,1:T(8,128)S(1)} %add.109), channel_id=1, source_target_pairs={{0,32},{4,36},{8,40},{12,44},{16,48},{20,52},{24,56},{28,60},{32,0... | collective-permute-start | bytes 196616 | tf_op jit(solution)/shard_map/ppermute | solution.py:17
  74.2 9.2 %collective-permute-start.12 = (f32[128,128]{0,1:T(8,128)S(1)}, f32[128,128]{0,1:T(8,128)S(1)}, u32[]{:S(2)}, u32[]{:S(2)}) collective-permute-start(f32[128,128]{0,1:T(8,128)S(1)} %add.110), channel_id=1, source_target_pairs={{0,64},{4,68},{8,72},{12,76},{16,80},{20,84},{24,88},{28,92},{32,9... | collective-permute-start | bytes 196616 | tf_op jit(solution)/shard_map/ppermute | solution.py:17
  83.4 6.7 %collective-permute-start.13 = (f32[128,128]{0,1:T(8,128)S(1)}, f32[128,128]{0,1:T(8,128)S(1)}, u32[]{:S(2)}, u32[]{:S(2)}) collective-permute-start(f32[128,128]{0,1:T(8,128)S(1)} %add.111), channel_id=1, source_target_pairs={{0,192},{4,196},{8,200},{12,204},{16,208},{20,212},{24,216},{28,22... | collective-permute-start | bytes 196616 | tf_op jit(solution)/shard_map/ppermute | solution.py:17
  90.1 4.4 %collective-permute-start.14 = (f32[128,128]{0,1:T(8,128)S(1)}, f32[128,128]{0,1:T(8,128)S(1)}, u32[]{:S(2)}, u32[]{:S(2)}) collective-permute-start(f32[128,128]{0,1:T(8,128)S(1)} %add.112), channel_id=1, source_target_pairs={{0,1},{1,0},{2,3},{3,2},{4,5},{5,4},{6,7},{7,6},{8,9},{9,8},{10,11... | collective-permute-start | bytes 196616 | tf_op jit(solution)/shard_map/ppermute | solution.py:17
  94.5 5.6 %collective-permute-start.15 = (f32[128,128]{0,1:T(8,128)S(1)}, f32[128,128]{0,1:T(8,128)S(1)}, u32[]{:S(2)}, u32[]{:S(2)}) collective-permute-start(f32[128,128]{0,1:T(8,128)S(1)} %add.113), channel_id=1, source_target_pairs={{0,3},{1,2},{2,1},{3,0},{4,7},{5,6},{6,5},{7,4},{8,11},{9,10},{10,... | collective-permute-start | bytes 196616 | tf_op jit(solution)/shard_map/ppermute | solution.py:17
  100.3 9.7 %copy-start.2 = (f32[96,32]{0,1:T(8,128)}, f32[96,32]{0,1:T(8,128)S(1)}, u32[]{:S(2)}) copy-start(f32[96,32]{0,1:T(8,128)S(1)} %get-tuple-element.19) | copy-start | bytes 36868

commit v4 on v3

--- a/solution.py
+++ b/solution.py
@@ -95,10 +95,10 @@
     all_rows = lax.iota(jnp.int32, sub_rows)
     select_upper = (index_rows[1][:, None] == all_rows[None, :]).astype(jnp.float32)
     select_lower = (index_rows[0][:, None] == all_rows[None, :]).astype(jnp.float32)
-    gathered = (
-        partial_value[:, :sub_rows]
-        + jnp.dot(back_upper, select_upper, precision=HIGH)
-        + jnp.dot(back_lower, select_lower, precision=HIGH)
+    gathered = partial_value[:, :sub_rows] + jnp.dot(
+        jnp.concatenate([back_upper, back_lower], axis=1),
+        jnp.concatenate([select_upper, select_lower], axis=0),
+        precision=HIGH,
     )
     block_t = scatter_rows(gathered, "row")
     vectors = basis[:, 0, :]
@@ -107,17 +107,13 @@
     first_part = contract_rows(vectors, block_t)
     basis_gram = contract_rows(vectors, vectors)
     block_gram = contract_rows(block_t, block_t)
-    packed = jnp.concatenate(
-        [
-            jnp.concatenate([first_part, basis_gram], axis=1),
-            jnp.concatenate([block_gram, jnp.zeros((vecs, count), jnp.float32)], axis=1),
-        ],
-        axis=0,
-    )
+    corner = count - vecs
+    packed = jnp.concatenate([first_part, basis_gram.at[corner:, :vecs].set(block_gram)], axis=1)
     summed = all_sum(packed, (("sub", (2, 4, lax.axis_size("sub") // 8)), ("row", (row_count,))))
     first, basis_gram, block_gram = lax.optimization_barrier(
-        (summed[:count, :vecs], summed[:count, vecs:], summed[count:, :vecs])
+        (summed[:, :vecs], summed[:, vecs:], summed[corner:, vecs:vecs + vecs])
     )
+    basis_gram = basis_gram.at[corner:, :vecs].set(basis_gram[:vecs, corner:].T)
     second = first - jnp.dot(basis_gram, first, precision=HIGH)
     coeffs = first + second
     once = block_t - contract_first(first, vectors)

time: 110 us -> 117 us (1.064)
  the two profiles are of different devices: /device:TPU:38 before, /device:TPU:64 now
where the time goes in v4:
time: 117 us
  waiting for transfers between devices  46.1 us (39%)
  starting transfers between devices  37.2 us (32%)
  matrix products  16.2 us (14%)
  other arithmetic  8.5 us (7%)
  local copies, waits for them, and re-layouts  7.81 us (7%)
    ppermute x12, waiting for transfers between devices, swap(): lax.ppermute(value, axis, [(source, source ^ mask) for source in range(co...  40.1 us
    ppermute x12, starting transfers between devices, swap(): lax.ppermute(value, axis, [(source, source ^ mask) for source in range(co...  21.8 us
    ppermute x4, starting transfers between devices, from_behind(): lax.ppermute(value, axis, [(source, source + steps) for source in range(l...  15.4 us
    dot_general x1, matrix products, per_device(): lax.dot_general(extended, factor_rows, (((1,), (1,)), ((), ())), precisio...  7.99 us
    ppermute x4, waiting for transfers between devices, from_behind(): lax.ppermute(value, axis, [(source, source + steps) for source in range(l...  6.02 us
    another operation x3, other arithmetic, per_device(): lower_tri = jnp.linalg.cholesky(gram)  3.6 us
    dot_general x1, matrix products, per_device(): product = jnp.dot(inner, factor_rows, precision=lax.Precision.HIGH)  3.3 us
    another operation x2, other arithmetic, per_device(): solved = jax.scipy.linalg.solve_triangular(lower_tri, twice, lower=True)  3.09 us
  transfers between devices with their start and end apart: 16, of which 14 were waited for; matrix products, arithmetic and copies ran while one was open for 3% of the time, Pallas kernels for 0%

profile of v4, /device:TPU:64, one launch (start us, length us, event | category | flops | bytes accessed | tf_op | source)
XLA Modules:
  0.0 116.9 jit_solution(7982032063472746717)
XLA Ops:
  5.8 3.1 %collective-permute-start.1 = (f32[32,1024]{1,0:T(8,128)S(1)}, f32[32,1024]{1,0:T(8,128)S(1)}, u32[]{:S(2)}, u32[]{:S(2)}) collective-permute-start(f32[32,1024]{1,0:T(8,128)S(1)} %maximum_select_fusion.1), channel_id=1, source_target_pairs={{0,3},{1,2},{2,1},{3,0},{4,7},{5,6},{6,5},{7,4},{8,11},{9,10},{10,... | collective-permute-start | bytes 393224 | tf_op jit(solution)/shard_map/ppermute | solution.py:17
  8.9 3.1 %collective-permute-done.1 = f32[32,1024]{1,0:T(8,128)S(1)} collective-permute-done((f32[32,1024]{1,0:T(8,128)S(1)}, f32[32,1024]{1,0:T(8,128)S(1)}, u32[]{:S(2)}, u32[]{:S(2)}) %collective-permute-start.1) | collective-permute-done | bytes 131104 | tf_op jit(solution)/shard_map/ppermute | solution.py:17
  13.5 1.9 %collective-permute-start.2 = (f32[32,512]{1,0:T(8,128)S(1)}, f32[32,512]{1,0:T(8,128)S(1)}, u32[]{:S(2)}, u32[]{:S(2)}) collective-permute-start(f32[32,512]{1,0:T(8,128)S(1)} %select_bitcast_fusion.1), channel_id=1, source_target_pairs={{0,4},{4,8},{8,12},{12,16},{16,20},{20,24},{24,28},{28,32},{32,36}... | collective-permute-start | bytes 196616 | tf_op jit(solution)/shard_map/ppermute | solution.py:12
  16.6 5.8 %collective-permute-start.3 = (f32[32,512]{1,0:T(8,128)S(1)}, f32[32,512]{1,0:T(8,128)S(1)}, u32[]{:S(2)}, u32[]{:S(2)}) collective-permute-start(f32[32,512]{1,0:T(8,128)S(1)} %select_bitcast_fusion), channel_id=1, source_target_pairs={{4,0},{8,4},{12,8},{16,12},{20,16},{24,20},{28,24},{32,28},{36,32}... | collective-permute-start | bytes 196616 | tf_op jit(solution)/shard_map/ppermute | solution.py:12
  24.3 8.0 %fusion.2 = f32[32,768]{1,0:T(8,128)S(1)} fusion(f32[1,768,3072]{2,1,0:T(8,128)} %param.11, f32[32,512]{1,0:T(8,128)S(1)} %collective-permute-done.3, f32[32,512]{1,0:T(8,128)S(1)} %collective-permute-done.2, f32[32,2048]{1,0:T(8,128)S(1)} %maximum_select_fusion), kind=kOutput, calls=%fused_computation.4 | convolution fusion | flops 453181440 | bytes 9928704 | tf_op jit(solution)/shard_map/dot_general | solution.py:86
  32.3 3.3 %fusion = f32[32,3072]{1,0:T(8,128)S(1)} fusion(f32[1,768,3072]{2,1,0:T(8,128)S(1)} %copy-done, f32[32,768]{1,0:T(8,128)S(1)} %fusion.2, f32[32,3072]{1,0:T(8,128)S(1)} %pad_maximum_fusion, s32[]{:T(128)S(6)} %select_n.64), kind=kOutput, calls=%fused_computation.2 | convolution fusion | flops 453009408 | bytes 10027012 | tf_op jit(solution)/shard_map/dot_general | solution.py:89
  35.7 5.8 %collective-permute-start.4 = (f32[32,512]{1,0:T(8,128)S(1)}, f32[32,512]{1,0:T(8,128)S(1)}, u32[]{:S(2)}, u32[]{:S(2)}) collective-permute-start(f32[32,512]{1,0:T(8,128)S(1)} %get-tuple-element.37), channel_id=1, source_target_pairs={{4,0},{8,4},{12,8},{16,12},{20,16},{24,20},{28,24},{32,28},{36,32}... | collective-permute-start | bytes 196616 | tf_op jit(solution)/shard_map/ppermute | solution.py:12
  45.1 4.1 %collective-permute-done.5 = f32[32,512]{1,0:T(8,128)S(1)} collective-permute-done((f32[32,512]{1,0:T(8,128)S(1)}, f32[32,512]{1,0:T(8,128)S(1)}, u32[]{:S(2)}, u32[]{:S(2)}) %collective-permute-start.5) | collective-permute-done | bytes 65568 | tf_op jit(solution)/shard_map/ppermute | solution.py:12
  49.2 2.5 %fusion.5 = f32[32,2048]{1,0:T(8,128)S(1)} fusion(pred[512,2048]{1,0:T(32,128)(4,1)S(1)} %get-tuple-element.49, pred[512,2048]{1,0:T(32,128)(4,1)S(1)} %get-tuple-element.50, f32[32,3072]{1,0:T(8,128)S(1)} %add_dynamic-update-slice_fusion, f32[32,512]{1,0:T(8,128)S(1)} %collective-permute-done.5, f32[32,512]{1,0:T(8,128)S(1)} %collective-permute-done.4), kind=kOutput, calls=%fused_computation.10 | convolution fusion | flops 807501824 | bytes 2752512 | tf_op jit(solution)/shard_map/dot_general | solution.py:98
  51.8 3.1 %collective-permute-start.6 = (f32[32,1024]{1,0:T(8,128)S(1)}, f32[32,1024]{1,0:T(8,128)S(1)}, u32[]{:S(2)}, u32[]{:S(2)}) collective-permute-start(f32[32,1024]{1,0:T(8,128)S(1)} %constant_dynamic-slice_fusion.1), channel_id=1, source_target_pairs={{0,3},{1,2},{2,1},{3,0},{4,7},{5,6},{6,5},{7,4},{8,11},{9,10},{10,... | collective-permute-start | bytes 393224 | tf_op jit(solution)/shard_map/ppermute | solution.py:17
  54.9 3.2 %collective-permute-done.6 = f32[32,1024]{1,0:T(8,128)S(1)} collective-permute-done((f32[32,1024]{1,0:T(8,128)S(1)}, f32[32,1024]{1,0:T(8,128)S(1)}, u32[]{:S(2)}, u32[]{:S(2)}) %collective-permute-start.6) | collective-permute-done | bytes 131104 | tf_op jit(solution)/shard_map/ppermute | solution.py:17
  58.7 3.9 %collective-permute-done.7 = f32[32,512]{1,0:T(8,128)S(1)} collective-permute-done((f32[32,512]{1,0:T(8,128)S(1)}, f32[32,512]{1,0:T(8,128)S(1)}, u32[]{:S(2)}, u32[]{:S(2)}) %collective-permute-start.7) | collective-permute-done | bytes 65568 | tf_op jit(solution)/shard_map/ppermute | solution.py:17
  65.6 4.3 %collective-permute-done.9 = f32[96,128]{0,1:T(8,128)S(1)} collective-permute-done((f32[96,128]{0,1:T(8,128)S(1)}, f32[96,128]{0,1:T(8,128)S(1)}, u32[]{:S(2)}, u32[]{:S(2)}) %collective-permute-start.9) | collective-permute-done | bytes 49184 | tf_op jit(solution)/shard_map/ppermute | solution.py:17
  69.9 5.5 %collective-permute-done.10 = f32[96,128]{0,1:T(8,128)S(1)} collective-permute-done((f32[96,128]{0,1:T(8,128)S(1)}, f32[96,128]{0,1:T(8,128)S(1)}, u32[]{:S(2)}, u32[]{:S(2)}) %collective-permute-start.10) | collective-permute-done | bytes 49184 | tf_op jit(solution)/shard_map/ppermute | solution.py:17
  75.4 2.0 %collective-permute-start.11 = (f32[96,128]{0,1:T(8,128)S(1)}, f32[96,128]{0,1:T(8,128)S(1)}, u32[]{:S(2)}, u32[]{:S(2)}) collective-permute-start(f32[96,128]{0,1:T(8,128)S(1)} %add.107), channel_id=1, source_target_pairs={{0,32},{4,36},{8,40},{12,44},{16,48},{20,52},{24,56},{28,60},{32,0... | collective-permute-start | bytes 147464 | tf_op jit(solution)/shard_map/ppermute | solution.py:17
  77.4 2.8 %collective-permute-done.11 = f32[96,128]{0,1:T(8,128)S(1)} collective-permute-done((f32[96,128]{0,1:T(8,128)S(1)}, f32[96,128]{0,1:T(8,128)S(1)}, u32[]{:S(2)}, u32[]{:S(2)}) %collective-permute-start.11) | collective-permute-done | bytes 49184 | tf_op jit(solution)/shard_map/ppermute | solution.py:17
  80.3 5.2 %collective-permute-done.12 = f32[96,128]{0,1:T(8,128)S(1)} collective-permute-done((f32[96,128]{0,1:T(8,128)S(1)}, f32[96,128]{0,1:T(8,128)S(1)}, u32[]{:S(2)}, u32[]{:S(2)}) %collective-permute-start.12) | collective-permute-done | bytes 49184 | tf_op jit(solution)/shard_map/ppermute | solution.py:17
  85.5 8.2 %collective-permute-start.13 = (f32[96,128]{0,1:T(8,128)S(1)}, f32[96,128]{0,1:T(8,128)S(1)}, u32[]{:S(2)}, u32[]{:S(2)}) collective-permute-start(f32[96,128]{0,1:T(8,128)S(1)} %add.109), channel_id=1, source_target_pairs={{0,192},{4,196},{8,200},{12,204},{16,208},{20,212},{24,216},{28,22... | collective-permute-start | bytes 147464 | tf_op jit(solution)/shard_map/ppermute | solution.py:17
  93.7 2.3 %collective-permute-done.13 = f32[96,128]{0,1:T(8,128)S(1)} collective-permute-done((f32[96,128]{0,1:T(8,128)S(1)}, f32[96,128]{0,1:T(8,128)S(1)}, u32[]{:S(2)}, u32[]{:S(2)}) %collective-permute-start.13) | collective-permute-done | bytes 49184 | tf_op jit(solution)/shard_map/ppermute | solution.py:17
  96.1 4.3 %collective-permute-done.14 = f32[96,128]{0,1:T(8,128)S(1)} collective-permute-done((f32[96,128]{0,1:T(8,128)S(1)}, f32[96,128]{0,1:T(8,128)S(1)}, u32[]{:S(2)}, u32[]{:S(2)}) %collective-permute-start.14) | collective-permute-done | bytes 49184 | tf_op jit(solution)/shard_map/ppermute | solution.py:17
  100.4 3.1 %collective-permute-start.15 = (f32[96,128]{0,1:T(8,128)S(1)}, f32[96,128]{0,1:T(8,128)S(1)}, u32[]{:S(2)}, u32[]{:S(2)}) collective-permute-start(f32[96,128]{0,1:T(8,128)S(1)} %add.111), channel_id=1, source_target_pairs={{0,3},{1,2},{2,1},{3,0},{4,7},{5,6},{6,5},{7,4},{8,11},{9,10},{10,... | collective-permute-start | bytes 147464 | tf_op jit(solution)/shard_map/ppermute | solution.py:17
  103.5 2.5 %collective-permute-done.15 = f32[96,128]{0,1:T(8,128)S(1)} collective-permute-done((f32[96,128]{0,1:T(8,128)S(1)}, f32[96,128]{0,1:T(8,128)S(1)}, u32[]{:S(2)}, u32[]{:S(2)}) %collective-permute-start.15) | collective-permute-done | bytes 49184 | tf_op jit(solution)/shard_map/ppermute | solution.py:17
  108.6 2.9 %cholesky.18 = f32[32,32]{1,0:T(8,128)S(1)} custom-call(f32[32,32]{1,0:T(8,128)S(1)} %fusion.22), custom_call_target="Cholesky" | custom-call | tf_op jit(solution)/shard_map/jit(cholesky)/cholesky | solution.py:125
  112.8 2.4 %custom-call.7 = f32[1,32,32]{1,2,0:T(8,128)S(1)} custom-call(f32[1,32,32]{2,1,0:T(8,128)S(1)} %get-tuple-element.39), custom_call_target="InvertDiagBlocksLowerTriangular" | custom-call | tf_op jit(solution)/shard_map/jit(_solve_triangular)/triangular_solve | solution.py:126
  (76 shorter events, 22.6 us)
Async XLA Ops:
  1.5 4.3 %collective-permute-start = (f32[32,512]{1,0:T(8,128)S(1)}, f32[32,512]{1,0:T(8,128)S(1)}, u32[]{:S(2)}, u32[]{:S(2)}) collective-permute-start(f32[32,512]{1,0:T(8,128)S(1)} %bitcast.58), channel_id=1, source_target_pairs={{0,1},{1,0},{2,3},{3,2},{4,5},{5,4},{6,7},{7,6},{8,9},{9,8},{10,11... | collective-permute-start | bytes 196616 | tf_op jit(solution)/shard_map/ppermute | solution.py:17
  5.8 6.3 %collective-permute-start.1 = (f32[32,1024]{1,0:T(8,128)S(1)}, f32[32,1024]{1,0:T(8,128)S(1)}, u32[]{:S(2)}, u32[]{:S(2)}) collective-permute-start(f32[32,1024]{1,0:T(8,128)S(1)} %maximum_select_fusion.1), channel_id=1, source_target_pairs={{0,3},{1,2},{2,1},{3,0},{4,7},{5,6},{6,5},{7,4},{8,11},{9,10},{10,... | collective-permute-start | bytes 393224 | tf_op jit(solution)/shard_map/ppermute | solution.py:17
  13.5 8.9 %collective-permute-start.2 = (f32[32,512]{1,0:T(8,128)S(1)}, f32[32,512]{1,0:T(8,128)S(1)}, u32[]{:S(2)}, u32[]{:S(2)}) collective-permute-start(f32[32,512]{1,0:T(8,128)S(1)} %select_bitcast_fusion.1), channel_id=1, source_target_pairs={{0,4},{4,8},{8,12},{12,16},{16,20},{20,24},{24,28},{28,32},{32,36}... | collective-permute-start | bytes 196616 | tf_op jit(solution)/shard_map/ppermute | solution.py:12
  16.6 7.6 %collective-permute-start.3 = (f32[32,512]{1,0:T(8,128)S(1)}, f32[32,512]{1,0:T(8,128)S(1)}, u32[]{:S(2)}, u32[]{:S(2)}) collective-permute-start(f32[32,512]{1,0:T(8,128)S(1)} %select_bitcast_fusion), channel_id=1, source_target_pairs={{4,0},{8,4},{12,8},{16,12},{20,16},{24,20},{28,24},{32,28},{36,32}... | collective-permute-start | bytes 196616 | tf_op jit(solution)/shard_map/ppermute | solution.py:12
  24.3 8.0 %copy-start = (f32[1,768,3072]{2,1,0:T(8,128)S(1)}, f32[1,768,3072]{2,1,0:T(8,128)}, u32[]{:S(2)}) copy-start(f32[1,768,3072]{2,1,0:T(8,128)} %param.11) | copy-start | bytes 28311556
  35.7 9.4 %collective-permute-start.4 = (f32[32,512]{1,0:T(8,128)S(1)}, f32[32,512]{1,0:T(8,128)S(1)}, u32[]{:S(2)}, u32[]{:S(2)}) collective-permute-start(f32[32,512]{1,0:T(8,128)S(1)} %get-tuple-element.37), channel_id=1, source_target_pairs={{4,0},{8,4},{12,8},{16,12},{20,16},{24,20},{28,24},{32,28},{36,32}... | collective-permute-start | bytes 196616 | tf_op jit(solution)/shard_map/ppermute | solution.py:12
  41.5 7.7 %collective-permute-start.5 = (f32[32,512]{1,0:T(8,128)S(1)}, f32[32,512]{1,0:T(8,128)S(1)}, u32[]{:S(2)}, u32[]{:S(2)}) collective-permute-start(f32[32,512]{1,0:T(8,128)S(1)} %get-tuple-element.38), channel_id=1, source_target_pairs={{0,4},{4,8},{8,12},{12,16},{16,20},{20,24},{24,28},{28,32},{32,36}... | collective-permute-start | bytes 196616 | tf_op jit(solution)/shard_map/ppermute | solution.py:12
  45.0 13.4 %copy-start.1 = (f32[96,1,512]{2,1,0:T(1,128)S(1)}, f32[96,1,512]{2,1,0:T(1,128)}, u32[]{:S(2)}) copy-start(f32[96,1,512]{2,1,0:T(1,128)} %param.12) | copy-start | bytes 589828
  51.8 6.3 %collective-permute-start.6 = (f32[32,1024]{1,0:T(8,128)S(1)}, f32[32,1024]{1,0:T(8,128)S(1)}, u32[]{:S(2)}, u32[]{:S(2)}) collective-permute-start(f32[32,1024]{1,0:T(8,128)S(1)} %constant_dynamic-slice_fusion.1), channel_id=1, source_target_pairs={{0,3},{1,2},{2,1},{3,0},{4,7},{5,6},{6,5},{7,4},{8,11},{9,10},{10,... | collective-permute-start | bytes 393224 | tf_op jit(solution)/shard_map/ppermute | solution.py:17
  58.1 4.5 %collective-permute-start.7 = (f32[32,512]{1,0:T(8,128)S(1)}, f32[32,512]{1,0:T(8,128)S(1)}, u32[]{:S(2)}, u32[]{:S(2)}) collective-permute-start(f32[32,512]{1,0:T(8,128)S(1)} %constant_dynamic-slice_fusion), channel_id=1, source_target_pairs={{0,1},{1,0},{2,3},{3,2},{4,5},{5,4},{6,7},{7,6},{8,9},{9,8},{10,11... | collective-permute-start | bytes 196616 | tf_op jit(solution)/shard_map/ppermute | solution.py:17
  64.1 1.3 %collective-permute-start.8 = (f32[96,128]{0,1:T(8,128)S(1)}, f32[96,128]{0,1:T(8,128)S(1)}, u32[]{:S(2)}, u32[]{:S(2)}) collective-permute-start(f32[96,128]{0,1:T(8,128)S(1)} %pad_maximum_fusion.1), channel_id=1, source_target_pairs={{0,4},{4,0},{8,12},{12,8},{16,20},{20,16},{24,28},{28,24},{32,36},... | collective-permute-start | bytes 147464 | tf_op jit(solution)/shard_map/ppermute | solution.py:17
  65.5 4.4 %collective-permute-start.9 = (f32[96,128]{0,1:T(8,128)S(1)}, f32[96,128]{0,1:T(8,128)S(1)}, u32[]{:S(2)}, u32[]{:S(2)}) collective-permute-start(f32[96,128]{0,1:T(8,128)S(1)} %fusion.27), channel_id=1, source_target_pairs={{0,8},{4,12},{8,0},{12,4},{16,24},{20,28},{24,16},{28,20},{32,40},... | collective-permute-start | bytes 147464 | tf_op jit(solution)/shard_map/ppermute | solution.py:17
  69.8 5.6 %collective-permute-start.10 = (f32[96,128]{0,1:T(8,128)S(1)}, f32[96,128]{0,1:T(8,128)S(1)}, u32[]{:S(2)}, u32[]{:S(2)}) collective-permute-start(f32[96,128]{0,1:T(8,128)S(1)} %add.106), channel_id=1, source_target_pairs={{0,24},{4,28},{8,16},{12,20},{16,8},{20,12},{24,0},{28,4},{32,56},... | collective-permute-start | bytes 147464 | tf_op jit(solution)/shard_map/ppermute | solution.py:17
  75.4 4.8 %collective-permute-start.11 = (f32[96,128]{0,1:T(8,128)S(1)}, f32[96,128]{0,1:T(8,128)S(1)}, u32[]{:S(2)}, u32[]{:S(2)}) collective-permute-start(f32[96,128]{0,1:T(8,128)S(1)} %add.107), channel_id=1, source_target_pairs={{0,32},{4,36},{8,40},{12,44},{16,48},{20,52},{24,56},{28,60},{32,0... | collective-permute-start | bytes 147464 | tf_op jit(solution)/shard_map/ppermute | solution.py:17
  80.2 5.3 %collective-permute-start.12 = (f32[96,128]{0,1:T(8,128)S(1)}, f32[96,128]{0,1:T(8,128)S(1)}, u32[]{:S(2)}, u32[]{:S(2)}) collective-permute-start(f32[96,128]{0,1:T(8,128)S(1)} %add.108), channel_id=1, source_target_pairs={{0,64},{4,68},{8,72},{12,76},{16,80},{20,84},{24,88},{28,92},{32,9... | collective-permute-start | bytes 147464 | tf_op jit(solution)/shard_map/ppermute | solution.py:17
  85.5 10.5 %collective-permute-start.13 = (f32[96,128]{0,1:T(8,128)S(1)}, f32[96,128]{0,1:T(8,128)S(1)}, u32[]{:S(2)}, u32[]{:S(2)}) collective-permute-start(f32[96,128]{0,1:T(8,128)S(1)} %add.109), channel_id=1, source_target_pairs={{0,192},{4,196},{8,200},{12,204},{16,208},{20,212},{24,216},{28,22... | collective-permute-start | bytes 147464 | tf_op jit(solution)/shard_map/ppermute | solution.py:17
  96.0 4.4 %collective-permute-start.14 = (f32[96,128]{0,1:T(8,128)S(1)}, f32[96,128]{0,1:T(8,128)S(1)}, u32[]{:S(2)}, u32[]{:S(2)}) collective-permute-start(f32[96,128]{0,1:T(8,128)S(1)} %add.110), channel_id=1, source_target_pairs={{0,1},{1,0},{2,3},{3,2},{4,5},{5,4},{6,7},{7,6},{8,9},{9,8},{10,11... | collective-permute-start | bytes 147464 | tf_op jit(solution)/shard_map/ppermute | solution.py:17
  100.4 5.6 %collective-permute-start.15 = (f32[96,128]{0,1:T(8,128)S(1)}, f32[96,128]{0,1:T(8,128)S(1)}, u32[]{:S(2)}, u32[]{:S(2)}) collective-permute-start(f32[96,128]{0,1:T(8,128)S(1)} %add.111), channel_id=1, source_target_pairs={{0,3},{1,2},{2,1},{3,0},{4,7},{5,6},{6,5},{7,4},{8,11},{9,10},{10,... | collective-permute-start | bytes 147464 | tf_op jit(solution)/shard_map/ppermute | solution.py:17
  107.3 9.7 %copy-start.2 = (f32[96,32]{0,1:T(8,128)}, f32[96,32]{0,1:T(8,128)S(1)}, u32[]{:S(2)}) copy-start(f32[96,32]{0,1:T(8,128)S(1)} %get-tuple-element.43) | copy-start | bytes 36868

commit v5 on v3

--- a/solution.py
+++ b/solution.py
@@ -77,26 +77,31 @@
     to_upper = jnp.take(whole, index_rows[1], axis=1)
     from_lower = from_behind(to_upper, "sub", 1)
     from_upper = from_behind(to_lower, "sub", -1)
-    extended = jnp.concatenate([whole, from_lower, from_upper], axis=1)
     factor_rows = factor[0]
     share = factor_rows.shape[0]
     margin = from_lower.shape[1]
     row_pos = lax.axis_index("row")
+    three = lax.Precision.HIGH
+    by_rows = (((1,), (1,)), ((), ()))
     start = row_pos * share
-    inner = lax.dynamic_slice_in_dim(extended, start, share, 1) + lax.dot_general(
-        extended, factor_rows, (((1,), (1,)), ((), ())), precision=lax.Precision.HIGH
+    inner_own = lax.optimization_barrier(lax.dot_general(whole, factor_rows[:, :sub_rows], by_rows, precision=three))
+    margins = jnp.concatenate([from_lower, from_upper], axis=1)
+    extended = jnp.concatenate([whole, margins], axis=1)
+    inner = (
+        inner_own
+        + lax.dot_general(margins, factor_rows[:, sub_rows:], by_rows, precision=three)
+        + lax.dynamic_slice_in_dim(extended, start, share, 1)
     )
-    product = jnp.dot(inner, factor_rows, precision=lax.Precision.HIGH)
-    partial_value = lax.dynamic_update_slice_in_dim(
-        product, lax.dynamic_slice_in_dim(product, start, share, 1) + inner, start, 1
-    )
-    back_upper = from_behind(partial_value[:, sub_rows:sub_rows + margin], "sub", -1)
-    back_lower = from_behind(partial_value[:, sub_rows + margin:], "sub", 1)
+    placed = lax.dynamic_update_slice_in_dim(jnp.zeros(extended.shape, jnp.float32), inner, start, 1)
+    margin_value = jnp.dot(inner, factor_rows[:, sub_rows:], precision=three) + placed[:, sub_rows:]
+    back_upper = from_behind(margin_value[:, :margin], "sub", -1)
+    back_lower = from_behind(margin_value[:, margin:], "sub", 1)
+    own_value = jnp.dot(inner, factor_rows[:, :sub_rows], precision=three) + placed[:, :sub_rows]
     all_rows = lax.iota(jnp.int32, sub_rows)
     select_upper = (index_rows[1][:, None] == all_rows[None, :]).astype(jnp.float32)
     select_lower = (index_rows[0][:, None] == all_rows[None, :]).astype(jnp.float32)
     gathered = (
-        partial_value[:, :sub_rows]
+        own_value
         + jnp.dot(back_upper, select_upper, precision=HIGH)
         + jnp.dot(back_lower, select_lower, precision=HIGH)
     )

time: 110 us -> 109 us (level)
    ppermute x4, starting transfers between devices: 12.7 us -> 11.4 us  [from_behind(): lax.ppermute(value, axis, [(source, source + steps) for source in range(l...]
    dot_general x2 -> x4, matrix products: 11.9 us -> 12.3 us  [the longest x1 5.6 us: per_device(): lax.dot_general(whole, factor_rows[:, :sub_rows], by_rows, precision=three)]
  transfers between devices with their start and end apart: 16 -> 16, of which waited for: 14 -> 13; matrix products, arithmetic and copies ran while one was open for 4% -> 11% of each run, Pallas kernels for 0% -> 0%
where the time goes in v5:
time: 109 us
  waiting for transfers between devices  42.7 us (39%)
  starting transfers between devices  34.1 us (31%)
  matrix products  18 us (17%)
  other arithmetic  7.07 us (6%)
  local copies, waits for them, and re-layouts  5.9 us (5%)
    ppermute x12, waiting for transfers between devices, swap(): lax.ppermute(value, axis, [(source, source ^ mask) for source in range(co...  41.3 us
    ppermute x12, starting transfers between devices, swap(): lax.ppermute(value, axis, [(source, source ^ mask) for source in range(co...  22.7 us
    ppermute x4, starting transfers between devices, from_behind(): lax.ppermute(value, axis, [(source, source + steps) for source in range(l...  11.4 us
    dot_general x1, matrix products, per_device(): lax.dot_general(whole, factor_rows[:, :sub_rows], by_rows, precision=three)  5.6 us
    another operation x3, other arithmetic, per_device(): lower_tri = jnp.linalg.cholesky(gram)  3.6 us
    dot_general x1, matrix products, per_device(): lax.dot_general(margins, factor_rows[:, sub_rows:], by_rows, precision=th...  3.35 us
    another operation x2, other arithmetic, per_device(): solved = jax.scipy.linalg.solve_triangular(lower_tri, twice, lower=True)  3.09 us
    unnamed x9, local copies, waits for them, and re-layouts  2.24 us
  transfers between devices with their start and end apart: 16, of which 13 were waited for; matrix products, arithmetic and copies ran while one was open for 11% of the time, Pallas kernels for 0%

profile of v5, /device:TPU:38, one launch (start us, length us, event | category | flops | bytes accessed | tf_op | source)
XLA Modules:
  0.0 108.8 jit_solution(13630057053680531675)
XLA Ops:
  5.8 3.1 %collective-permute-start.1 = (f32[32,1024]{1,0:T(8,128)S(1)}, f32[32,1024]{1,0:T(8,128)S(1)}, u32[]{:S(2)}, u32[]{:S(2)}) collective-permute-start(f32[32,1024]{1,0:T(8,128)S(1)} %maximum_select_fusion.1), channel_id=1, source_target_pairs={{0,3},{1,2},{2,1},{3,0},{4,7},{5,6},{6,5},{7,4},{8,11},{9,10},{10,... | collective-permute-start | bytes 393224 | tf_op jit(solution)/shard_map/ppermute | solution.py:17
  8.9 3.1 %collective-permute-done.1 = f32[32,1024]{1,0:T(8,128)S(1)} collective-permute-done((f32[32,1024]{1,0:T(8,128)S(1)}, f32[32,1024]{1,0:T(8,128)S(1)}, u32[]{:S(2)}, u32[]{:S(2)}) %collective-permute-start.1) | collective-permute-done | bytes 131104 | tf_op jit(solution)/shard_map/ppermute | solution.py:17
  13.5 1.9 %collective-permute-start.2 = (f32[32,512]{1,0:T(8,128)S(1)}, f32[32,512]{1,0:T(8,128)S(1)}, u32[]{:S(2)}, u32[]{:S(2)}) collective-permute-start(f32[32,512]{1,0:T(8,128)S(1)} %select_bitcast_fusion.1), channel_id=1, source_target_pairs={{0,4},{4,8},{8,12},{12,16},{16,20},{20,24},{24,28},{28,32},{32,36}... | collective-permute-start | bytes 196616 | tf_op jit(solution)/shard_map/ppermute | solution.py:12
  16.6 3.9 %collective-permute-start.3 = (f32[32,512]{1,0:T(8,128)S(1)}, f32[32,512]{1,0:T(8,128)S(1)}, u32[]{:S(2)}, u32[]{:S(2)}) collective-permute-start(f32[32,512]{1,0:T(8,128)S(1)} %select_bitcast_fusion), channel_id=1, source_target_pairs={{4,0},{8,4},{12,8},{16,12},{20,16},{24,20},{28,24},{32,28},{36,32}... | collective-permute-start | bytes 196616 | tf_op jit(solution)/shard_map/ppermute | solution.py:12
  20.6 5.6 %fusion.2 = f32[32,768]{1,0:T(8,128)S(1)} fusion(f32[32,2048]{1,0:T(8,128)S(1)} %maximum_select_fusion, f32[768,3072]{1,0:T(8,128)} %bitcast.57), kind=kOutput, calls=%fused_computation.4 | convolution fusion | flops 301989888 | bytes 6651904 | tf_op jit(solution)/shard_map/dot_general | solution.py:87
  26.2 3.4 %fusion.8 = f32[32,768]{1,0:T(8,128)S(1)} fusion(f32[768,3072]{1,0:T(8,128)} %bitcast.58, f32[32,512]{1,0:T(8,128)S(1)} %collective-permute-done.3, f32[32,512]{1,0:T(8,128)S(1)} %collective-permute-done.2), kind=kOutput, calls=%fused_computation.12 | convolution fusion | flops 151027712 | bytes 3375104 | tf_op jit(solution)/shard_map/dot_general | solution.py:92
  30.8 2.6 %collective-permute-start.5 = (f32[32,512]{1,0:T(8,128)S(1)}, f32[32,512]{1,0:T(8,128)S(1)}, u32[]{:S(2)}, u32[]{:S(2)}) collective-permute-start(f32[32,512]{1,0:T(8,128)S(1)} %get-tuple-element.16), channel_id=1, source_target_pairs={{0,4},{4,8},{8,12},{12,16},{16,20},{20,24},{24,28},{28,32},{32,36}... | collective-permute-start | bytes 196616 | tf_op jit(solution)/shard_map/ppermute | solution.py:12
  33.4 2.2 %fusion.12 = f32[32,2048]{1,0:T(8,128)S(1)} fusion(f32[32,768]{1,0:T(8,128)S(1)} %get-tuple-element.14, f32[768,3072]{1,0:T(8,128)S(1)} %bitcast.60, f32[32,3072]{1,0:T(8,128)S(1)} %get-tuple-element.13), kind=kOutput, calls=%fused_computation.16 | convolution fusion | flops 302055424 | bytes 6914048 | tf_op jit(solution)/shard_map/dot_general | solution.py:99
  35.7 3.0 %collective-permute-start.4 = (f32[32,512]{1,0:T(8,128)S(1)}, f32[32,512]{1,0:T(8,128)S(1)}, u32[]{:S(2)}, u32[]{:S(2)}) collective-permute-start(f32[32,512]{1,0:T(8,128)S(1)} %get-tuple-element.15), channel_id=1, source_target_pairs={{4,0},{8,4},{12,8},{16,12},{20,16},{24,20},{28,24},{32,28},{36,32}... | collective-permute-start | bytes 196616 | tf_op jit(solution)/shard_map/ppermute | solution.py:12
  43.4 3.1 %collective-permute-start.6 = (f32[32,1024]{1,0:T(8,128)S(1)}, f32[32,1024]{1,0:T(8,128)S(1)}, u32[]{:S(2)}, u32[]{:S(2)}) collective-permute-start(f32[32,1024]{1,0:T(8,128)S(1)} %constant_dynamic-slice_fusion.1), channel_id=1, source_target_pairs={{0,3},{1,2},{2,1},{3,0},{4,7},{5,6},{6,5},{7,4},{8,11},{9,10},{10,... | collective-permute-start | bytes 393224 | tf_op jit(solution)/shard_map/ppermute | solution.py:17
  46.5 3.2 %collective-permute-done.6 = f32[32,1024]{1,0:T(8,128)S(1)} collective-permute-done((f32[32,1024]{1,0:T(8,128)S(1)}, f32[32,1024]{1,0:T(8,128)S(1)}, u32[]{:S(2)}, u32[]{:S(2)}) %collective-permute-start.6) | collective-permute-done | bytes 131104 | tf_op jit(solution)/shard_map/ppermute | solution.py:17
  50.3 3.9 %collective-permute-done.7 = f32[32,512]{1,0:T(8,128)S(1)} collective-permute-done((f32[32,512]{1,0:T(8,128)S(1)}, f32[32,512]{1,0:T(8,128)S(1)}, u32[]{:S(2)}, u32[]{:S(2)}) %collective-permute-start.7) | collective-permute-done | bytes 65568 | tf_op jit(solution)/shard_map/ppermute | solution.py:17
  54.8 2.8 %collective-permute-start.8 = (f32[128,128]{0,1:T(8,128)S(1)}, f32[128,128]{0,1:T(8,128)S(1)}, u32[]{:S(2)}, u32[]{:S(2)}) collective-permute-start(f32[128,128]{0,1:T(8,128)S(1)} %select_maximum_fusion), channel_id=1, source_target_pairs={{0,4},{4,0},{8,12},{12,8},{16,20},{20,16},{24,28},{28,24},{32,36},... | collective-permute-start | bytes 196616 | tf_op jit(solution)/shard_map/ppermute | solution.py:17
  58.7 4.3 %collective-permute-done.9 = f32[128,128]{0,1:T(8,128)S(1)} collective-permute-done((f32[128,128]{0,1:T(8,128)S(1)}, f32[128,128]{0,1:T(8,128)S(1)}, u32[]{:S(2)}, u32[]{:S(2)}) %collective-permute-start.9) | collective-permute-done | bytes 65568 | tf_op jit(solution)/shard_map/ppermute | solution.py:17
  64.1 4.5 %collective-permute-done.10 = f32[128,128]{0,1:T(8,128)S(1)} collective-permute-done((f32[128,128]{0,1:T(8,128)S(1)}, f32[128,128]{0,1:T(8,128)S(1)}, u32[]{:S(2)}, u32[]{:S(2)}) %collective-permute-start.10) | collective-permute-done | bytes 65568 | tf_op jit(solution)/shard_map/ppermute | solution.py:17
  68.8 4.2 %collective-permute-done.11 = f32[128,128]{0,1:T(8,128)S(1)} collective-permute-done((f32[128,128]{0,1:T(8,128)S(1)}, f32[128,128]{0,1:T(8,128)S(1)}, u32[]{:S(2)}, u32[]{:S(2)}) %collective-permute-start.11) | collective-permute-done | bytes 65568 | tf_op jit(solution)/shard_map/ppermute | solution.py:17
  73.0 7.0 %collective-permute-start.12 = (f32[128,128]{0,1:T(8,128)S(1)}, f32[128,128]{0,1:T(8,128)S(1)}, u32[]{:S(2)}, u32[]{:S(2)}) collective-permute-start(f32[128,128]{0,1:T(8,128)S(1)} %add.117), channel_id=1, source_target_pairs={{0,64},{4,68},{8,72},{12,76},{16,80},{20,84},{24,88},{28,92},{32,9... | collective-permute-start | bytes 196616 | tf_op jit(solution)/shard_map/ppermute | solution.py:17
  80.0 2.2 %collective-permute-done.12 = f32[128,128]{0,1:T(8,128)S(1)} collective-permute-done((f32[128,128]{0,1:T(8,128)S(1)}, f32[128,128]{0,1:T(8,128)S(1)}, u32[]{:S(2)}, u32[]{:S(2)}) %collective-permute-start.12) | collective-permute-done | bytes 65568 | tf_op jit(solution)/shard_map/ppermute | solution.py:17
  82.3 6.6 %collective-permute-done.13 = f32[128,128]{0,1:T(8,128)S(1)} collective-permute-done((f32[128,128]{0,1:T(8,128)S(1)}, f32[128,128]{0,1:T(8,128)S(1)}, u32[]{:S(2)}, u32[]{:S(2)}) %collective-permute-start.13) | collective-permute-done | bytes 65568 | tf_op jit(solution)/shard_map/ppermute | solution.py:17
  89.3 4.0 %collective-permute-done.14 = f32[128,128]{0,1:T(8,128)S(1)} collective-permute-done((f32[128,128]{0,1:T(8,128)S(1)}, f32[128,128]{0,1:T(8,128)S(1)}, u32[]{:S(2)}, u32[]{:S(2)}) %collective-permute-start.14) | collective-permute-done | bytes 65568 | tf_op jit(solution)/shard_map/ppermute | solution.py:17
  93.3 3.0 %collective-permute-start.15 = (f32[128,128]{0,1:T(8,128)S(1)}, f32[128,128]{0,1:T(8,128)S(1)}, u32[]{:S(2)}, u32[]{:S(2)}) collective-permute-start(f32[128,128]{0,1:T(8,128)S(1)} %add.120), channel_id=1, source_target_pairs={{0,3},{1,2},{2,1},{3,0},{4,7},{5,6},{6,5},{7,4},{8,11},{9,10},{10,... | collective-permute-start | bytes 196616 | tf_op jit(solution)/shard_map/ppermute | solution.py:17
  96.3 2.5 %collective-permute-done.15 = f32[128,128]{0,1:T(8,128)S(1)} collective-permute-done((f32[128,128]{0,1:T(8,128)S(1)}, f32[128,128]{0,1:T(8,128)S(1)}, u32[]{:S(2)}, u32[]{:S(2)}) %collective-permute-start.15) | collective-permute-done | bytes 65568 | tf_op jit(solution)/shard_map/ppermute | solution.py:17
  100.4 2.9 %cholesky.18 = f32[32,32]{1,0:T(8,128)S(1)} custom-call(f32[32,32]{1,0:T(8,128)S(1)} %fusion.39), custom_call_target="Cholesky" | custom-call | tf_op jit(solution)/shard_map/jit(cholesky)/cholesky | solution.py:134
  104.7 2.4 %custom-call.7 = f32[1,32,32]{1,2,0:T(8,128)S(1)} custom-call(f32[1,32,32]{2,1,0:T(8,128)S(1)} %get-tuple-element.17), custom_call_target="InvertDiagBlocksLowerTriangular" | custom-call | tf_op jit(solution)/shard_map/jit(_solve_triangular)/triangular_solve | solution.py:135
  (74 shorter events, 22.2 us)
Async XLA Ops:
  1.5 4.3 %collective-permute-start = (f32[32,512]{1,0:T(8,128)S(1)}, f32[32,512]{1,0:T(8,128)S(1)}, u32[]{:S(2)}, u32[]{:S(2)}) collective-permute-start(f32[32,512]{1,0:T(8,128)S(1)} %bitcast.61), channel_id=1, source_target_pairs={{0,1},{1,0},{2,3},{3,2},{4,5},{5,4},{6,7},{7,6},{8,9},{9,8},{10,11... | collective-permute-start | bytes 196616 | tf_op jit(solution)/shard_map/ppermute | solution.py:17
  5.8 6.3 %collective-permute-start.1 = (f32[32,1024]{1,0:T(8,128)S(1)}, f32[32,1024]{1,0:T(8,128)S(1)}, u32[]{:S(2)}, u32[]{:S(2)}) collective-permute-start(f32[32,1024]{1,0:T(8,128)S(1)} %maximum_select_fusion.1), channel_id=1, source_target_pairs={{0,3},{1,2},{2,1},{3,0},{4,7},{5,6},{6,5},{7,4},{8,11},{9,10},{10,... | collective-permute-start | bytes 393224 | tf_op jit(solution)/shard_map/ppermute | solution.py:17
  13.5 12.6 %collective-permute-start.2 = (f32[32,512]{1,0:T(8,128)S(1)}, f32[32,512]{1,0:T(8,128)S(1)}, u32[]{:S(2)}, u32[]{:S(2)}) collective-permute-start(f32[32,512]{1,0:T(8,128)S(1)} %select_bitcast_fusion.1), channel_id=1, source_target_pairs={{0,4},{4,8},{8,12},{12,16},{16,20},{20,24},{24,28},{28,32},{32,36}... | collective-permute-start | bytes 196616 | tf_op jit(solution)/shard_map/ppermute | solution.py:12
  16.6 13.0 %copy-start = (f32[1,768,3072]{2,1,0:T(8,128)S(1)}, f32[1,768,3072]{2,1,0:T(8,128)}, u32[]{:S(2)}) copy-start(f32[1,768,3072]{2,1,0:T(8,128)} %param.7) | copy-start | bytes 28311556
  16.6 9.5 %collective-permute-start.3 = (f32[32,512]{1,0:T(8,128)S(1)}, f32[32,512]{1,0:T(8,128)S(1)}, u32[]{:S(2)}, u32[]{:S(2)}) collective-permute-start(f32[32,512]{1,0:T(8,128)S(1)} %select_bitcast_fusion), channel_id=1, source_target_pairs={{4,0},{8,4},{12,8},{16,12},{20,16},{24,20},{28,24},{32,28},{36,32}... | collective-permute-start | bytes 196616 | tf_op jit(solution)/shard_map/ppermute | solution.py:12
  29.7 20.3 %copy-start.1 = (f32[96,1,512]{2,1,0:T(1,128)S(1)}, f32[96,1,512]{2,1,0:T(1,128)}, u32[]{:S(2)}) copy-start(f32[96,1,512]{2,1,0:T(1,128)} %param.8) | copy-start | bytes 589828
  30.8 7.8 %collective-permute-start.5 = (f32[32,512]{1,0:T(8,128)S(1)}, f32[32,512]{1,0:T(8,128)S(1)}, u32[]{:S(2)}, u32[]{:S(2)}) collective-permute-start(f32[32,512]{1,0:T(8,128)S(1)} %get-tuple-element.16), channel_id=1, source_target_pairs={{0,4},{4,8},{8,12},{12,16},{16,20},{20,24},{24,28},{28,32},{32,36}... | collective-permute-start | bytes 196616 | tf_op jit(solution)/shard_map/ppermute | solution.py:12
  35.7 6.0 %collective-permute-start.4 = (f32[32,512]{1,0:T(8,128)S(1)}, f32[32,512]{1,0:T(8,128)S(1)}, u32[]{:S(2)}, u32[]{:S(2)}) collective-permute-start(f32[32,512]{1,0:T(8,128)S(1)} %get-tuple-element.15), channel_id=1, source_target_pairs={{4,0},{8,4},{12,8},{16,12},{20,16},{24,20},{28,24},{32,28},{36,32}... | collective-permute-start | bytes 196616 | tf_op jit(solution)/shard_map/ppermute | solution.py:12
  43.4 6.3 %collective-permute-start.6 = (f32[32,1024]{1,0:T(8,128)S(1)}, f32[32,1024]{1,0:T(8,128)S(1)}, u32[]{:S(2)}, u32[]{:S(2)}) collective-permute-start(f32[32,1024]{1,0:T(8,128)S(1)} %constant_dynamic-slice_fusion.1), channel_id=1, source_target_pairs={{0,3},{1,2},{2,1},{3,0},{4,7},{5,6},{6,5},{7,4},{8,11},{9,10},{10,... | collective-permute-start | bytes 393224 | tf_op jit(solution)/shard_map/ppermute | solution.py:17
  49.7 4.5 %collective-permute-start.7 = (f32[32,512]{1,0:T(8,128)S(1)}, f32[32,512]{1,0:T(8,128)S(1)}, u32[]{:S(2)}, u32[]{:S(2)}) collective-permute-start(f32[32,512]{1,0:T(8,128)S(1)} %constant_dynamic-slice_fusion), channel_id=1, source_target_pairs={{0,1},{1,0},{2,3},{3,2},{4,5},{5,4},{6,7},{7,6},{8,9},{9,8},{10,11... | collective-permute-start | bytes 196616 | tf_op jit(solution)/shard_map/ppermute | solution.py:17
  54.8 3.7 %collective-permute-start.8 = (f32[128,128]{0,1:T(8,128)S(1)}, f32[128,128]{0,1:T(8,128)S(1)}, u32[]{:S(2)}, u32[]{:S(2)}) collective-permute-start(f32[128,128]{0,1:T(8,128)S(1)} %select_maximum_fusion), channel_id=1, source_target_pairs={{0,4},{4,0},{8,12},{12,8},{16,20},{20,16},{24,28},{28,24},{32,36},... | collective-permute-start | bytes 196616 | tf_op jit(solution)/shard_map/ppermute | solution.py:17
  58.7 4.4 %collective-permute-start.9 = (f32[128,128]{0,1:T(8,128)S(1)}, f32[128,128]{0,1:T(8,128)S(1)}, u32[]{:S(2)}, u32[]{:S(2)}) collective-permute-start(f32[128,128]{0,1:T(8,128)S(1)} %fusion.68), channel_id=1, source_target_pairs={{0,8},{4,12},{8,0},{12,4},{16,24},{20,28},{24,16},{28,20},{32,40},... | collective-permute-start | bytes 196616 | tf_op jit(solution)/shard_map/ppermute | solution.py:17
  63.0 5.6 %collective-permute-start.10 = (f32[128,128]{0,1:T(8,128)S(1)}, f32[128,128]{0,1:T(8,128)S(1)}, u32[]{:S(2)}, u32[]{:S(2)}) collective-permute-start(f32[128,128]{0,1:T(8,128)S(1)} %add.115), channel_id=1, source_target_pairs={{0,24},{4,28},{8,16},{12,20},{16,8},{20,12},{24,0},{28,4},{32,56},... | collective-permute-start | bytes 196616 | tf_op jit(solution)/shard_map/ppermute | solution.py:17
  68.6 4.4 %collective-permute-start.11 = (f32[128,128]{0,1:T(8,128)S(1)}, f32[128,128]{0,1:T(8,128)S(1)}, u32[]{:S(2)}, u32[]{:S(2)}) collective-permute-start(f32[128,128]{0,1:T(8,128)S(1)} %add.116), channel_id=1, source_target_pairs={{0,32},{4,36},{8,40},{12,44},{16,48},{20,52},{24,56},{28,60},{32,0... | collective-permute-start | bytes 196616 | tf_op jit(solution)/shard_map/ppermute | solution.py:17
  73.0 9.2 %collective-permute-start.12 = (f32[128,128]{0,1:T(8,128)S(1)}, f32[128,128]{0,1:T(8,128)S(1)}, u32[]{:S(2)}, u32[]{:S(2)}) collective-permute-start(f32[128,128]{0,1:T(8,128)S(1)} %add.117), channel_id=1, source_target_pairs={{0,64},{4,68},{8,72},{12,76},{16,80},{20,84},{24,88},{28,92},{32,9... | collective-permute-start | bytes 196616 | tf_op jit(solution)/shard_map/ppermute | solution.py:17
  82.2 6.7 %collective-permute-start.13 = (f32[128,128]{0,1:T(8,128)S(1)}, f32[128,128]{0,1:T(8,128)S(1)}, u32[]{:S(2)}, u32[]{:S(2)}) collective-permute-start(f32[128,128]{0,1:T(8,128)S(1)} %add.118), channel_id=1, source_target_pairs={{0,192},{4,196},{8,200},{12,204},{16,208},{20,212},{24,216},{28,22... | collective-permute-start | bytes 196616 | tf_op jit(solution)/shard_map/ppermute | solution.py:17
  88.9 4.4 %collective-permute-start.14 = (f32[128,128]{0,1:T(8,128)S(1)}, f32[128,128]{0,1:T(8,128)S(1)}, u32[]{:S(2)}, u32[]{:S(2)}) collective-permute-start(f32[128,128]{0,1:T(8,128)S(1)} %add.119), channel_id=1, source_target_pairs={{0,1},{1,0},{2,3},{3,2},{4,5},{5,4},{6,7},{7,6},{8,9},{9,8},{10,11... | collective-permute-start | bytes 196616 | tf_op jit(solution)/shard_map/ppermute | solution.py:17
  93.3 5.6 %collective-permute-start.15 = (f32[128,128]{0,1:T(8,128)S(1)}, f32[128,128]{0,1:T(8,128)S(1)}, u32[]{:S(2)}, u32[]{:S(2)}) collective-permute-start(f32[128,128]{0,1:T(8,128)S(1)} %add.120), channel_id=1, source_target_pairs={{0,3},{1,2},{2,1},{3,0},{4,7},{5,6},{6,5},{7,4},{8,11},{9,10},{10,... | collective-permute-start | bytes 196616 | tf_op jit(solution)/shard_map/ppermute | solution.py:17
  99.1 9.7 %copy-start.2 = (f32[96,32]{0,1:T(8,128)}, f32[96,32]{0,1:T(8,128)S(1)}, u32[]{:S(2)}) copy-start(f32[96,32]{0,1:T(8,128)S(1)} %get-tuple-element.21) | copy-start | bytes 36868

commit v6 on v5

--- a/solution.py
+++ b/solution.py
@@ -1,6 +1,7 @@
 import jax
 import jax.numpy as jnp
 from jax import lax
+from jax.experimental import pallas as pl
 from jax.sharding import PartitionSpec as P
 
 HIGH = lax.Precision.HIGHEST
@@ -63,6 +64,32 @@
         for mask in masks[1:]:
             value = value + swap(value, axis, mask)
     return value
+
+
+def factor_kernel(gram_ref, upper_ref, inverse_ref):
+    size = gram_ref.shape[0]
+    mat = gram_ref[...]
+    rows = lax.broadcasted_iota(jnp.int32, (size, size), 0)
+    cols = lax.broadcasted_iota(jnp.int32, (size, size), 1)
+    inv = (rows == cols).astype(jnp.float32)
+    for j in range(size):
+        col = jnp.sum(jnp.where(cols == j, mat, 0.0), axis=1, keepdims=True)
+        row = jnp.sum(jnp.where(rows == j, mat, 0.0), axis=0, keepdims=True)
+        inv_row = jnp.sum(jnp.where(rows == j, inv, 0.0), axis=0, keepdims=True)
+        pivot = jnp.sum(jnp.where(rows[:, :1] == j, col, 0.0), axis=0, keepdims=True)
+        scale = 1.0 / jnp.sqrt(pivot)
+        ratio = jnp.where(rows[:, :1] > j, col / pivot, 0.0)
+        here = rows == j
+        mat = jnp.where(here, row * scale, mat - ratio * row)
+        inv = jnp.where(here, inv_row * scale, inv - ratio * inv_row)
+    upper_ref[...] = jnp.where(rows <= cols, mat, 0.0)
+    inverse_ref[...] = jnp.where(rows >= cols, inv, 0.0)
+
+
+def cholesky_parts(gram):
+    size = gram.shape[0]
+    shape = jax.ShapeDtypeStruct((size, size), jnp.float32)
+    return pl.pallas_call(factor_kernel, out_shape=(shape, shape))((gram + gram.T) * 0.5)
 
 
 def per_device(residual, factor, basis, send_rows):
@@ -131,9 +158,9 @@
     gram = (
         block_gram - cross - cross.T + contract_first(coeffs, jnp.dot(basis_gram, coeffs, precision=HIGH))
     ) / total_rows
-    lower_tri = jnp.linalg.cholesky(gram)
-    solved = jax.scipy.linalg.solve_triangular(lower_tri, twice, lower=True)
-    return (coeffs, lower_tri.T, solved[:, None, :])
+    upper_tri, lower_inverse = cholesky_parts(gram)
+    solved = jnp.dot(lower_inverse, twice, precision=HIGH)
+    return (coeffs, upper_tri, solved[:, None, :])
 
 
 def solution(mesh):

time: 109 us -> 108 us (level)
  other arithmetic: 7.07 us -> 1 us
  Pallas kernels: 0 us -> 4.68 us
    another operation x5 -> x0, other arithmetic: 6.68 us -> none  [the longest x3 3.6 us: per_device(): lower_tri = jnp.linalg.cholesky(gram)]
    pallas_call x0 -> x1, Pallas kernels: none -> 4.68 us  [cholesky_parts(): pl.pallas_call(factor_kernel, out_shape=(shape, shape))]
    unnamed x9 -> x8, local copies, waits for them, and re-layouts: 2.24 us -> 1.56 us
where the time goes in v6:
time: 108 us; the launch traced here: 107 us
  waiting for transfers between devices  42.7 us (40%)
  starting transfers between devices  34.1 us (32%)
  matrix products  18.6 us (17%)
  local copies, waits for them, and re-layouts  5.23 us (5%)
  Pallas kernels  4.68 us (4%)
    ppermute x12, waiting for transfers between devices, swap(): lax.ppermute(value, axis, [(source, source ^ mask) for source in range(co...  41.3 us
    ppermute x12, starting transfers between devices, swap(): lax.ppermute(value, axis, [(source, source ^ mask) for source in range(co...  22.7 us
    ppermute x4, starting transfers between devices, from_behind(): lax.ppermute(value, axis, [(source, source + steps) for source in range(l...  11.4 us
    dot_general x1, matrix products, per_device(): lax.dot_general(whole, factor_rows[:, :sub_rows], by_rows, precision=three)  5.6 us
    pallas_call x1, Pallas kernels, cholesky_parts(): pl.pallas_call(factor_kernel, out_shape=(shape, shape))  4.68 us
    dot_general x1, matrix products, per_device(): lax.dot_general(margins, factor_rows[:, sub_rows:], by_rows, precision=th...  3.35 us
    dot_general x1, matrix products, per_device(): jnp.dot(inner, factor_rows[:, :sub_rows], precision=three)  2.22 us
  transfers between devices with their start and end apart: 16, of which 13 were waited for; matrix products, arithmetic and copies ran while one was open for 11% of the time, Pallas kernels for 0%

profile of v6, /device:TPU:38, one launch (start us, length us, event | category | flops | bytes accessed | tf_op | source)
XLA Modules:
  0.0 107.3 jit_solution(14495688992748978220)
XLA Ops:
  3.8 1.9 %collective-permute-done = f32[32,512]{1,0:T(8,128)S(1)} collective-permute-done((f32[32,512]{1,0:T(8,128)S(1)}, f32[32,512]{1,0:T(8,128)S(1)}, u32[]{:S(2)}, u32[]{:S(2)}) %collective-permute-start) | collective-permute-done | bytes 65568 | tf_op jit(solution)/shard_map/ppermute | solution.py:18
  5.8 3.1 %collective-permute-start.1 = (f32[32,1024]{1,0:T(8,128)S(1)}, f32[32,1024]{1,0:T(8,128)S(1)}, u32[]{:S(2)}, u32[]{:S(2)}) collective-permute-start(f32[32,1024]{1,0:T(8,128)S(1)} %maximum_select_fusion.1), channel_id=1, source_target_pairs={{0,3},{1,2},{2,1},{3,0},{4,7},{5,6},{6,5},{7,4},{8,11},{9,10},{10,... | collective-permute-start | bytes 393224 | tf_op jit(solution)/shard_map/ppermute | solution.py:18
  8.9 3.1 %collective-permute-done.1 = f32[32,1024]{1,0:T(8,128)S(1)} collective-permute-done((f32[32,1024]{1,0:T(8,128)S(1)}, f32[32,1024]{1,0:T(8,128)S(1)}, u32[]{:S(2)}, u32[]{:S(2)}) %collective-permute-start.1) | collective-permute-done | bytes 131104 | tf_op jit(solution)/shard_map/ppermute | solution.py:18
  13.5 1.9 %collective-permute-start.2 = (f32[32,512]{1,0:T(8,128)S(1)}, f32[32,512]{1,0:T(8,128)S(1)}, u32[]{:S(2)}, u32[]{:S(2)}) collective-permute-start(f32[32,512]{1,0:T(8,128)S(1)} %select_bitcast_fusion.1), channel_id=1, source_target_pairs={{0,4},{4,8},{8,12},{12,16},{16,20},{20,24},{24,28},{28,32},{32,36}... | collective-permute-start | bytes 196616 | tf_op jit(solution)/shard_map/ppermute | solution.py:13
  16.6 3.9 %collective-permute-start.3 = (f32[32,512]{1,0:T(8,128)S(1)}, f32[32,512]{1,0:T(8,128)S(1)}, u32[]{:S(2)}, u32[]{:S(2)}) collective-permute-start(f32[32,512]{1,0:T(8,128)S(1)} %select_bitcast_fusion), channel_id=1, source_target_pairs={{4,0},{8,4},{12,8},{16,12},{20,16},{24,20},{28,24},{32,28},{36,32}... | collective-permute-start | bytes 196616 | tf_op jit(solution)/shard_map/ppermute | solution.py:13
  20.6 5.6 %fusion.2 = f32[32,768]{1,0:T(8,128)S(1)} fusion(f32[32,2048]{1,0:T(8,128)S(1)} %maximum_select_fusion, f32[768,3072]{1,0:T(8,128)} %bitcast.51), kind=kOutput, calls=%fused_computation.4 | convolution fusion | flops 301989888 | bytes 6651904 | tf_op jit(solution)/shard_map/dot_general | solution.py:114
  26.2 3.4 %fusion.8 = f32[32,768]{1,0:T(8,128)S(1)} fusion(f32[768,3072]{1,0:T(8,128)} %bitcast.52, f32[32,512]{1,0:T(8,128)S(1)} %collective-permute-done.3, f32[32,512]{1,0:T(8,128)S(1)} %collective-permute-done.2), kind=kOutput, calls=%fused_computation.12 | convolution fusion | flops 151027712 | bytes 3375104 | tf_op jit(solution)/shard_map/dot_general | solution.py:119
  30.8 2.6 %collective-permute-start.5 = (f32[32,512]{1,0:T(8,128)S(1)}, f32[32,512]{1,0:T(8,128)S(1)}, u32[]{:S(2)}, u32[]{:S(2)}) collective-permute-start(f32[32,512]{1,0:T(8,128)S(1)} %get-tuple-element.20), channel_id=1, source_target_pairs={{0,4},{4,8},{8,12},{12,16},{16,20},{20,24},{24,28},{28,32},{32,36}... | collective-permute-start | bytes 196616 | tf_op jit(solution)/shard_map/ppermute | solution.py:13
  33.4 2.2 %fusion.12 = f32[32,2048]{1,0:T(8,128)S(1)} fusion(f32[32,768]{1,0:T(8,128)S(1)} %get-tuple-element.18, f32[768,3072]{1,0:T(8,128)S(1)} %bitcast.54, f32[32,3072]{1,0:T(8,128)S(1)} %get-tuple-element.17), kind=kOutput, calls=%fused_computation.16 | convolution fusion | flops 302055424 | bytes 6914048 | tf_op jit(solution)/shard_map/dot_general | solution.py:126
  35.7 3.0 %collective-permute-start.4 = (f32[32,512]{1,0:T(8,128)S(1)}, f32[32,512]{1,0:T(8,128)S(1)}, u32[]{:S(2)}, u32[]{:S(2)}) collective-permute-start(f32[32,512]{1,0:T(8,128)S(1)} %get-tuple-element.19), channel_id=1, source_target_pairs={{4,0},{8,4},{12,8},{16,12},{20,16},{24,20},{28,24},{32,28},{36,32}... | collective-permute-start | bytes 196616 | tf_op jit(solution)/shard_map/ppermute | solution.py:13
  43.4 3.1 %collective-permute-start.6 = (f32[32,1024]{1,0:T(8,128)S(1)}, f32[32,1024]{1,0:T(8,128)S(1)}, u32[]{:S(2)}, u32[]{:S(2)}) collective-permute-start(f32[32,1024]{1,0:T(8,128)S(1)} %constant_dynamic-slice_fusion.1), channel_id=1, source_target_pairs={{0,3},{1,2},{2,1},{3,0},{4,7},{5,6},{6,5},{7,4},{8,11},{9,10},{10,... | collective-permute-start | bytes 393224 | tf_op jit(solution)/shard_map/ppermute | solution.py:18
  46.5 3.2 %collective-permute-done.6 = f32[32,1024]{1,0:T(8,128)S(1)} collective-permute-done((f32[32,1024]{1,0:T(8,128)S(1)}, f32[32,1024]{1,0:T(8,128)S(1)}, u32[]{:S(2)}, u32[]{:S(2)}) %collective-permute-start.6) | collective-permute-done | bytes 131104 | tf_op jit(solution)/shard_map/ppermute | solution.py:18
  50.3 3.9 %collective-permute-done.7 = f32[32,512]{1,0:T(8,128)S(1)} collective-permute-done((f32[32,512]{1,0:T(8,128)S(1)}, f32[32,512]{1,0:T(8,128)S(1)}, u32[]{:S(2)}, u32[]{:S(2)}) %collective-permute-start.7) | collective-permute-done | bytes 65568 | tf_op jit(solution)/shard_map/ppermute | solution.py:18
  54.8 2.8 %collective-permute-start.8 = (f32[128,128]{0,1:T(8,128)S(1)}, f32[128,128]{0,1:T(8,128)S(1)}, u32[]{:S(2)}, u32[]{:S(2)}) collective-permute-start(f32[128,128]{0,1:T(8,128)S(1)} %select_maximum_fusion), channel_id=1, source_target_pairs={{0,4},{4,0},{8,12},{12,8},{16,20},{20,16},{24,28},{28,24},{32,36},... | collective-permute-start | bytes 196616 | tf_op jit(solution)/shard_map/ppermute | solution.py:18
  58.7 4.3 %collective-permute-done.9 = f32[128,128]{0,1:T(8,128)S(1)} collective-permute-done((f32[128,128]{0,1:T(8,128)S(1)}, f32[128,128]{0,1:T(8,128)S(1)}, u32[]{:S(2)}, u32[]{:S(2)}) %collective-permute-start.9) | collective-permute-done | bytes 65568 | tf_op jit(solution)/shard_map/ppermute | solution.py:18
  64.1 4.5 %collective-permute-done.10 = f32[128,128]{0,1:T(8,128)S(1)} collective-permute-done((f32[128,128]{0,1:T(8,128)S(1)}, f32[128,128]{0,1:T(8,128)S(1)}, u32[]{:S(2)}, u32[]{:S(2)}) %collective-permute-start.10) | collective-permute-done | bytes 65568 | tf_op jit(solution)/shard_map/ppermute | solution.py:18
  68.8 4.2 %collective-permute-done.11 = f32[128,128]{0,1:T(8,128)S(1)} collective-permute-done((f32[128,128]{0,1:T(8,128)S(1)}, f32[128,128]{0,1:T(8,128)S(1)}, u32[]{:S(2)}, u32[]{:S(2)}) %collective-permute-start.11) | collective-permute-done | bytes 65568 | tf_op jit(solution)/shard_map/ppermute | solution.py:18
  73.0 7.0 %collective-permute-start.12 = (f32[128,128]{0,1:T(8,128)S(1)}, f32[128,128]{0,1:T(8,128)S(1)}, u32[]{:S(2)}, u32[]{:S(2)}) collective-permute-start(f32[128,128]{0,1:T(8,128)S(1)} %add.108), channel_id=1, source_target_pairs={{0,64},{4,68},{8,72},{12,76},{16,80},{20,84},{24,88},{28,92},{32,9... | collective-permute-start | bytes 196616 | tf_op jit(solution)/shard_map/ppermute | solution.py:18
  80.0 2.2 %collective-permute-done.12 = f32[128,128]{0,1:T(8,128)S(1)} collective-permute-done((f32[128,128]{0,1:T(8,128)S(1)}, f32[128,128]{0,1:T(8,128)S(1)}, u32[]{:S(2)}, u32[]{:S(2)}) %collective-permute-start.12) | collective-permute-done | bytes 65568 | tf_op jit(solution)/shard_map/ppermute | solution.py:18
  82.3 6.6 %collective-permute-done.13 = f32[128,128]{0,1:T(8,128)S(1)} collective-permute-done((f32[128,128]{0,1:T(8,128)S(1)}, f32[128,128]{0,1:T(8,128)S(1)}, u32[]{:S(2)}, u32[]{:S(2)}) %collective-permute-start.13) | collective-permute-done | bytes 65568 | tf_op jit(solution)/shard_map/ppermute | solution.py:18
  89.3 4.0 %collective-permute-done.14 = f32[128,128]{0,1:T(8,128)S(1)} collective-permute-done((f32[128,128]{0,1:T(8,128)S(1)}, f32[128,128]{0,1:T(8,128)S(1)}, u32[]{:S(2)}, u32[]{:S(2)}) %collective-permute-start.14) | collective-permute-done | bytes 65568 | tf_op jit(solution)/shard_map/ppermute | solution.py:18
  93.3 3.0 %collective-permute-start.15 = (f32[128,128]{0,1:T(8,128)S(1)}, f32[128,128]{0,1:T(8,128)S(1)}, u32[]{:S(2)}, u32[]{:S(2)}) collective-permute-start(f32[128,128]{0,1:T(8,128)S(1)} %add.111), channel_id=1, source_target_pairs={{0,3},{1,2},{2,1},{3,0},{4,7},{5,6},{6,5},{7,4},{8,11},{9,10},{10,... | collective-permute-start | bytes 196616 | tf_op jit(solution)/shard_map/ppermute | solution.py:18
  96.3 2.5 %collective-permute-done.15 = f32[128,128]{0,1:T(8,128)S(1)} collective-permute-done((f32[128,128]{0,1:T(8,128)S(1)}, f32[128,128]{0,1:T(8,128)S(1)}, u32[]{:S(2)}, u32[]{:S(2)}) %collective-permute-start.15) | collective-permute-done | bytes 65568 | tf_op jit(solution)/shard_map/ppermute | solution.py:18
  101.1 4.7 %shard_map.67 = (f32[32,32]{1,0:T(8,128)}, f32[32,32]{1,0:T(8,128)}) custom-call(f32[32,32]{1,0:T(8,128)} %fusion.38.gram_ref), custom_call_target="tpu_custom_call" | custom-call | tf_op jit(solution)/shard_map/pallas_call | solution.py:92
  (69 shorter events, 19.6 us)
Async XLA Ops:
  1.5 4.3 %collective-permute-start = (f32[32,512]{1,0:T(8,128)S(1)}, f32[32,512]{1,0:T(8,128)S(1)}, u32[]{:S(2)}, u32[]{:S(2)}) collective-permute-start(f32[32,512]{1,0:T(8,128)S(1)} %bitcast.55), channel_id=1, source_target_pairs={{0,1},{1,0},{2,3},{3,2},{4,5},{5,4},{6,7},{7,6},{8,9},{9,8},{10,11... | collective-permute-start | bytes 196616 | tf_op jit(solution)/shard_map/ppermute | solution.py:18
  5.8 6.3 %collective-permute-start.1 = (f32[32,1024]{1,0:T(8,128)S(1)}, f32[32,1024]{1,0:T(8,128)S(1)}, u32[]{:S(2)}, u32[]{:S(2)}) collective-permute-start(f32[32,1024]{1,0:T(8,128)S(1)} %maximum_select_fusion.1), channel_id=1, source_target_pairs={{0,3},{1,2},{2,1},{3,0},{4,7},{5,6},{6,5},{7,4},{8,11},{9,10},{10,... | collective-permute-start | bytes 393224 | tf_op jit(solution)/shard_map/ppermute | solution.py:18
  13.5 12.6 %collective-permute-start.2 = (f32[32,512]{1,0:T(8,128)S(1)}, f32[32,512]{1,0:T(8,128)S(1)}, u32[]{:S(2)}, u32[]{:S(2)}) collective-permute-start(f32[32,512]{1,0:T(8,128)S(1)} %select_bitcast_fusion.1), channel_id=1, source_target_pairs={{0,4},{4,8},{8,12},{12,16},{16,20},{20,24},{24,28},{28,32},{32,36}... | collective-permute-start | bytes 196616 | tf_op jit(solution)/shard_map/ppermute | solution.py:13
  16.6 13.0 %copy-start = (f32[1,768,3072]{2,1,0:T(8,128)S(1)}, f32[1,768,3072]{2,1,0:T(8,128)}, u32[]{:S(2)}) copy-start(f32[1,768,3072]{2,1,0:T(8,128)} %param.7) | copy-start | bytes 28311556
  16.6 9.5 %collective-permute-start.3 = (f32[32,512]{1,0:T(8,128)S(1)}, f32[32,512]{1,0:T(8,128)S(1)}, u32[]{:S(2)}, u32[]{:S(2)}) collective-permute-start(f32[32,512]{1,0:T(8,128)S(1)} %select_bitcast_fusion), channel_id=1, source_target_pairs={{4,0},{8,4},{12,8},{16,12},{20,16},{24,20},{28,24},{32,28},{36,32}... | collective-permute-start | bytes 196616 | tf_op jit(solution)/shard_map/ppermute | solution.py:13
  29.7 20.3 %copy-start.1 = (f32[96,1,512]{2,1,0:T(1,128)S(1)}, f32[96,1,512]{2,1,0:T(1,128)}, u32[]{:S(2)}) copy-start(f32[96,1,512]{2,1,0:T(1,128)} %param.8) | copy-start | bytes 589828
  30.8 7.8 %collective-permute-start.5 = (f32[32,512]{1,0:T(8,128)S(1)}, f32[32,512]{1,0:T(8,128)S(1)}, u32[]{:S(2)}, u32[]{:S(2)}) collective-permute-start(f32[32,512]{1,0:T(8,128)S(1)} %get-tuple-element.20), channel_id=1, source_target_pairs={{0,4},{4,8},{8,12},{12,16},{16,20},{20,24},{24,28},{28,32},{32,36}... | collective-permute-start | bytes 196616 | tf_op jit(solution)/shard_map/ppermute | solution.py:13
  35.7 6.0 %collective-permute-start.4 = (f32[32,512]{1,0:T(8,128)S(1)}, f32[32,512]{1,0:T(8,128)S(1)}, u32[]{:S(2)}, u32[]{:S(2)}) collective-permute-start(f32[32,512]{1,0:T(8,128)S(1)} %get-tuple-element.19), channel_id=1, source_target_pairs={{4,0},{8,4},{12,8},{16,12},{20,16},{24,20},{28,24},{32,28},{36,32}... | collective-permute-start | bytes 196616 | tf_op jit(solution)/shard_map/ppermute | solution.py:13
  43.4 6.3 %collective-permute-start.6 = (f32[32,1024]{1,0:T(8,128)S(1)}, f32[32,1024]{1,0:T(8,128)S(1)}, u32[]{:S(2)}, u32[]{:S(2)}) collective-permute-start(f32[32,1024]{1,0:T(8,128)S(1)} %constant_dynamic-slice_fusion.1), channel_id=1, source_target_pairs={{0,3},{1,2},{2,1},{3,0},{4,7},{5,6},{6,5},{7,4},{8,11},{9,10},{10,... | collective-permute-start | bytes 393224 | tf_op jit(solution)/shard_map/ppermute | solution.py:18
  49.7 4.5 %collective-permute-start.7 = (f32[32,512]{1,0:T(8,128)S(1)}, f32[32,512]{1,0:T(8,128)S(1)}, u32[]{:S(2)}, u32[]{:S(2)}) collective-permute-start(f32[32,512]{1,0:T(8,128)S(1)} %constant_dynamic-slice_fusion), channel_id=1, source_target_pairs={{0,1},{1,0},{2,3},{3,2},{4,5},{5,4},{6,7},{7,6},{8,9},{9,8},{10,11... | collective-permute-start | bytes 196616 | tf_op jit(solution)/shard_map/ppermute | solution.py:18
  54.8 3.7 %collective-permute-start.8 = (f32[128,128]{0,1:T(8,128)S(1)}, f32[128,128]{0,1:T(8,128)S(1)}, u32[]{:S(2)}, u32[]{:S(2)}) collective-permute-start(f32[128,128]{0,1:T(8,128)S(1)} %select_maximum_fusion), channel_id=1, source_target_pairs={{0,4},{4,0},{8,12},{12,8},{16,20},{20,16},{24,28},{28,24},{32,36},... | collective-permute-start | bytes 196616 | tf_op jit(solution)/shard_map/ppermute | solution.py:18
  58.7 4.4 %collective-permute-start.9 = (f32[128,128]{0,1:T(8,128)S(1)}, f32[128,128]{0,1:T(8,128)S(1)}, u32[]{:S(2)}, u32[]{:S(2)}) collective-permute-start(f32[128,128]{0,1:T(8,128)S(1)} %fusion.67), channel_id=1, source_target_pairs={{0,8},{4,12},{8,0},{12,4},{16,24},{20,28},{24,16},{28,20},{32,40},... | collective-permute-start | bytes 196616 | tf_op jit(solution)/shard_map/ppermute | solution.py:18
  63.0 5.6 %collective-permute-start.10 = (f32[128,128]{0,1:T(8,128)S(1)}, f32[128,128]{0,1:T(8,128)S(1)}, u32[]{:S(2)}, u32[]{:S(2)}) collective-permute-start(f32[128,128]{0,1:T(8,128)S(1)} %add.106), channel_id=1, source_target_pairs={{0,24},{4,28},{8,16},{12,20},{16,8},{20,12},{24,0},{28,4},{32,56},... | collective-permute-start | bytes 196616 | tf_op jit(solution)/shard_map/ppermute | solution.py:18
  68.6 4.4 %collective-permute-start.11 = (f32[128,128]{0,1:T(8,128)S(1)}, f32[128,128]{0,1:T(8,128)S(1)}, u32[]{:S(2)}, u32[]{:S(2)}) collective-permute-start(f32[128,128]{0,1:T(8,128)S(1)} %add.107), channel_id=1, source_target_pairs={{0,32},{4,36},{8,40},{12,44},{16,48},{20,52},{24,56},{28,60},{32,0... | collective-permute-start | bytes 196616 | tf_op jit(solution)/shard_map/ppermute | solution.py:18
  73.0 9.2 %collective-permute-start.12 = (f32[128,128]{0,1:T(8,128)S(1)}, f32[128,128]{0,1:T(8,128)S(1)}, u32[]{:S(2)}, u32[]{:S(2)}) collective-permute-start(f32[128,128]{0,1:T(8,128)S(1)} %add.108), channel_id=1, source_target_pairs={{0,64},{4,68},{8,72},{12,76},{16,80},{20,84},{24,88},{28,92},{32,9... | collective-permute-start | bytes 196616 | tf_op jit(solution)/shard_map/ppermute | solution.py:18
  82.2 6.7 %collective-permute-start.13 = (f32[128,128]{0,1:T(8,128)S(1)}, f32[128,128]{0,1:T(8,128)S(1)}, u32[]{:S(2)}, u32[]{:S(2)}) collective-permute-start(f32[128,128]{0,1:T(8,128)S(1)} %add.109), channel_id=1, source_target_pairs={{0,192},{4,196},{8,200},{12,204},{16,208},{20,212},{24,216},{28,22... | collective-permute-start | bytes 196616 | tf_op jit(solution)/shard_map/ppermute | solution.py:18
  88.9 4.4 %collective-permute-start.14 = (f32[128,128]{0,1:T(8,128)S(1)}, f32[128,128]{0,1:T(8,128)S(1)}, u32[]{:S(2)}, u32[]{:S(2)}) collective-permute-start(f32[128,128]{0,1:T(8,128)S(1)} %add.110), channel_id=1, source_target_pairs={{0,1},{1,0},{2,3},{3,2},{4,5},{5,4},{6,7},{7,6},{8,9},{9,8},{10,11... | collective-permute-start | bytes 196616 | tf_op jit(solution)/shard_map/ppermute | solution.py:18
  93.3 5.6 %collective-permute-start.15 = (f32[128,128]{0,1:T(8,128)S(1)}, f32[128,128]{0,1:T(8,128)S(1)}, u32[]{:S(2)}, u32[]{:S(2)}) collective-permute-start(f32[128,128]{0,1:T(8,128)S(1)} %add.111), channel_id=1, source_target_pairs={{0,3},{1,2},{2,1},{3,0},{4,7},{5,6},{6,5},{7,4},{8,11},{9,10},{10,... | collective-permute-start | bytes 196616 | tf_op jit(solution)/shard_map/ppermute | solution.py:18
  99.1 8.2 %copy-start.2 = (f32[96,32]{0,1:T(8,128)}, f32[96,32]{0,1:T(8,128)S(1)}, u32[]{:S(2)}) copy-start(f32[96,32]{0,1:T(8,128)S(1)} %get-tuple-element.23) | copy-start | bytes 36868

commit v7 on v5

--- a/solution.py
+++ b/solution.py
@@ -1,6 +1,7 @@
 import jax
 import jax.numpy as jnp
 from jax import lax
+from jax.experimental import pallas as pl
 from jax.sharding import PartitionSpec as P
 
 HIGH = lax.Precision.HIGHEST
@@ -65,6 +66,27 @@
     return value
 
 
+def factor_kernel(aug_ref, out_ref):
+    size, width = aug_ref.shape
+    aug = aug_ref[...]
+    rows = lax.broadcasted_iota(jnp.int32, (size, width), 0)
+    cols = lax.broadcasted_iota(jnp.int32, (size, width), 1)
+    first_col = rows[:, :1]
+    for j in range(size):
+        col = jnp.sum(jnp.where(cols == j, aug, 0.0), axis=1, keepdims=True)
+        row = jnp.sum(jnp.where(rows == j, aug, 0.0), axis=0, keepdims=True)
+        pivot = jnp.sum(jnp.where(first_col == j, col, 0.0), axis=0, keepdims=True)
+        ratio = jnp.where(first_col > j, col / pivot, 0.0)
+        aug = jnp.where(rows == j, row * (1.0 / jnp.sqrt(pivot)), aug - ratio * row)
+    out_ref[...] = jnp.where((rows <= cols) | (cols >= size), aug, 0.0)
+
+
+def cholesky_parts(gram):
+    size = gram.shape[0]
+    aug = jnp.concatenate([(gram + gram.T) * 0.5, jnp.eye(size, dtype=jnp.float32)], axis=1)
+    out = pl.pallas_call(factor_kernel, out_shape=jax.ShapeDtypeStruct(aug.shape, jnp.float32))(aug)
+    return out[:, :size], out[:, size:]
+
 def per_device(residual, factor, basis, send_rows):
     slab = residual.shape[2]
     row_count = lax.axis_size("row")
@@ -73,8 +95,9 @@
     own_rows = residual[:, 0, :]
     whole = gather_rows(own_rows, "row")
     index_rows = send_rows[0]
-    to_lower = jnp.take(whole, index_rows[0], axis=1)
-    to_upper = jnp.take(whole, index_rows[1], axis=1)
+    both_sides = jnp.take(whole, index_rows.reshape(-1), axis=1)
+    to_lower = both_sides[:, :index_rows.shape[1]]
+    to_upper = both_sides[:, index_rows.shape[1]:]
     from_lower = from_behind(to_upper, "sub", 1)
     from_upper = from_behind(to_lower, "sub", -1)
     factor_rows = factor[0]
@@ -131,9 +154,9 @@
     gram = (
         block_gram - cross - cross.T + contract_first(coeffs, jnp.dot(basis_gram, coeffs, precision=HIGH))
     ) / total_rows
-    lower_tri = jnp.linalg.cholesky(gram)
-    solved = jax.scipy.linalg.solve_triangular(lower_tri, twice, lower=True)
-    return (coeffs, lower_tri.T, solved[:, None, :])
+    upper_tri, lower_inverse = cholesky_parts(gram)
+    solved = jnp.dot(lower_inverse, twice, precision=HIGH)
+    return (coeffs, upper_tri, solved[:, None, :])
 
 
 def solution(mesh):

time: 109 us -> 109 us (level)
  other arithmetic: 7.07 us -> 1.07 us
  Pallas kernels: 0 us -> 4.68 us
  local copies, waits for them, and re-layouts: 5.9 us -> 7.32 us
  waiting for transfers between devices: 42.7 us -> 41.3 us
    another operation x5 -> x0, other arithmetic: 6.68 us -> none  [the longest x3 3.6 us: per_device(): lower_tri = jnp.linalg.cholesky(gram)]
    pallas_call x0 -> x1, Pallas kernels: none -> 4.68 us  [cholesky_parts(): pl.pallas_call(factor_kernel, out_shape=jax.ShapeDtypeStruct(aug.shape, j...]
    ppermute x12, waiting for transfers between devices: 41.3 us -> 39.9 us  [swap(): lax.ppermute(value, axis, [(source, source ^ mask) for source in range(co...]
    gather x4 -> x2, local copies, waits for them, and re-layouts: 2.27 us -> 2.98 us  [per_device(): both_sides = jnp.take(whole, index_rows.reshape(-1), axis=1)]
    unnamed x9 -> x10, local copies, waits for them, and re-layouts: 2.24 us -> 2.94 us
where the time goes in v7:
time: 109 us; the launch traced here: 108 us
  waiting for transfers between devices  41.3 us (38%)
  starting transfers between devices  34.1 us (31%)
  matrix products  18.7 us (17%)
  local copies, waits for them, and re-layouts  7.32 us (7%)
  Pallas kernels  4.68 us (4%)
    ppermute x12, waiting for transfers between devices, swap(): lax.ppermute(value, axis, [(source, source ^ mask) for source in range(co...  39.9 us
    ppermute x12, starting transfers between devices, swap(): lax.ppermute(value, axis, [(source, source ^ mask) for source in range(co...  22.7 us
    ppermute x4, starting transfers between devices, from_behind(): lax.ppermute(value, axis, [(source, source + steps) for source in range(l...  11.4 us
    dot_general x1, matrix products, per_device(): lax.dot_general(whole, factor_rows[:, :sub_rows], by_rows, precision=three)  5.6 us
    pallas_call x1, Pallas kernels, cholesky_parts(): pl.pallas_call(factor_kernel, out_shape=jax.ShapeDtypeStruct(aug.shape, j...  4.68 us
    dot_general x1, matrix products, per_device(): lax.dot_general(margins, factor_rows[:, sub_rows:], by_rows, precision=th...  3.35 us
    gather x2, local copies, waits for them, and re-layouts, per_device(): both_sides = jnp.take(whole, index_rows.reshape(-1), axis=1)  2.98 us
    unnamed x10, local copies, waits for them, and re-layouts  2.94 us
  transfers between devices with their start and end apart: 16, of which 13 were waited for; matrix products, arithmetic and copies ran while one was open for 11% of the time, Pallas kernels for 0%

profile of v7, /device:TPU:38, one launch (start us, length us, event | category | flops | bytes accessed | tf_op | source)
XLA Modules:
  0.0 108.2 jit_solution(3119403628697655080)
XLA Ops:
  5.8 3.1 %collective-permute-start.1 = (f32[32,1024]{1,0:T(8,128)S(1)}, f32[32,1024]{1,0:T(8,128)S(1)}, u32[]{:S(2)}, u32[]{:S(2)}) collective-permute-start(f32[32,1024]{1,0:T(8,128)S(1)} %maximum_select_fusion.1), channel_id=1, source_target_pairs={{0,3},{1,2},{2,1},{3,0},{4,7},{5,6},{6,5},{7,4},{8,11},{9,10},{10,... | collective-permute-start | bytes 393224 | tf_op jit(solution)/shard_map/ppermute | solution.py:18
  8.9 3.2 %collective-permute-done.1 = f32[32,1024]{1,0:T(8,128)S(1)} collective-permute-done((f32[32,1024]{1,0:T(8,128)S(1)}, f32[32,1024]{1,0:T(8,128)S(1)}, u32[]{:S(2)}, u32[]{:S(2)}) %collective-permute-start.1) | collective-permute-done | bytes 131104 | tf_op jit(solution)/shard_map/ppermute | solution.py:18
  12.4 2.8 %gather_fusion = f32[1024,32]{1,0:T(8,128)S(1)} fusion(f32[32,2048]{0,1:T(8,128)S(1)} %copy.7, s32[1024]{0:T(1024)S(1)} %broadcast_clamp_fusion), kind=kCustom, calls=%fused_computation | custom fusion | bytes 266240 | tf_op jit(solution)/shard_map/jit(_take)/gather | solution.py:98
  15.4 2.3 %collective-permute-start.2 = (f32[32,512]{1,0:T(8,128)S(1)}, f32[32,512]{1,0:T(8,128)S(1)}, u32[]{:S(2)}, u32[]{:S(2)}) collective-permute-start(f32[32,512]{1,0:T(8,128)S(1)} %get-tuple-element.16), channel_id=1, source_target_pairs={{0,4},{4,8},{8,12},{12,16},{16,20},{20,24},{24,28},{28,32},{32,36}... | collective-permute-start | bytes 196616 | tf_op jit(solution)/shard_map/ppermute | solution.py:13
  17.7 3.5 %collective-permute-start.3 = (f32[32,512]{1,0:T(8,128)S(1)}, f32[32,512]{1,0:T(8,128)S(1)}, u32[]{:S(2)}, u32[]{:S(2)}) collective-permute-start(f32[32,512]{1,0:T(8,128)S(1)} %get-tuple-element.17), channel_id=1, source_target_pairs={{4,0},{8,4},{12,8},{16,12},{20,16},{24,20},{28,24},{32,28},{36,32}... | collective-permute-start | bytes 196616 | tf_op jit(solution)/shard_map/ppermute | solution.py:13
  21.3 5.6 %fusion.2 = f32[32,768]{1,0:T(8,128)S(1)} fusion(f32[32,2048]{1,0:T(8,128)S(1)} %maximum_select_fusion, f32[768,3072]{1,0:T(8,128)} %bitcast.55), kind=kOutput, calls=%fused_computation.3 | convolution fusion | flops 301989888 | bytes 6651904 | tf_op jit(solution)/shard_map/dot_general | solution.py:110
  26.9 3.4 %fusion.8 = f32[32,768]{1,0:T(8,128)S(1)} fusion(f32[768,3072]{1,0:T(8,128)} %bitcast.56, f32[32,512]{1,0:T(8,128)S(1)} %collective-permute-done.3, f32[32,512]{1,0:T(8,128)S(1)} %collective-permute-done.2), kind=kOutput, calls=%fused_computation.11 | convolution fusion | flops 151027712 | bytes 3375104 | tf_op jit(solution)/shard_map/dot_general | solution.py:115
  31.5 2.3 %collective-permute-start.5 = (f32[32,512]{1,0:T(8,128)S(1)}, f32[32,512]{1,0:T(8,128)S(1)}, u32[]{:S(2)}, u32[]{:S(2)}) collective-permute-start(f32[32,512]{1,0:T(8,128)S(1)} %get-tuple-element.15), channel_id=1, source_target_pairs={{0,4},{4,8},{8,12},{12,16},{16,20},{20,24},{24,28},{28,32},{32,36}... | collective-permute-start | bytes 196616 | tf_op jit(solution)/shard_map/ppermute | solution.py:13
  33.8 2.2 %fusion.12 = f32[32,2048]{1,0:T(8,128)S(1)} fusion(f32[32,768]{1,0:T(8,128)S(1)} %get-tuple-element.13, f32[768,3072]{1,0:T(8,128)S(1)} %bitcast.58, f32[32,3072]{1,0:T(8,128)S(1)} %get-tuple-element.12), kind=kOutput, calls=%fused_computation.15 | convolution fusion | flops 302055424 | bytes 6914048 | tf_op jit(solution)/shard_map/dot_general | solution.py:122
  36.0 3.3 %collective-permute-start.4 = (f32[32,512]{1,0:T(8,128)S(1)}, f32[32,512]{1,0:T(8,128)S(1)}, u32[]{:S(2)}, u32[]{:S(2)}) collective-permute-start(f32[32,512]{1,0:T(8,128)S(1)} %get-tuple-element.14), channel_id=1, source_target_pairs={{4,0},{8,4},{12,8},{16,12},{20,16},{24,20},{28,24},{32,28},{36,32}... | collective-permute-start | bytes 196616 | tf_op jit(solution)/shard_map/ppermute | solution.py:13
  44.1 3.1 %collective-permute-start.6 = (f32[32,1024]{1,0:T(8,128)S(1)}, f32[32,1024]{1,0:T(8,128)S(1)}, u32[]{:S(2)}, u32[]{:S(2)}) collective-permute-start(f32[32,1024]{1,0:T(8,128)S(1)} %constant_dynamic-slice_fusion.1), channel_id=1, source_target_pairs={{0,3},{1,2},{2,1},{3,0},{4,7},{5,6},{6,5},{7,4},{8,11},{9,10},{10,... | collective-permute-start | bytes 393224 | tf_op jit(solution)/shard_map/ppermute | solution.py:18
  47.2 3.2 %collective-permute-done.6 = f32[32,1024]{1,0:T(8,128)S(1)} collective-permute-done((f32[32,1024]{1,0:T(8,128)S(1)}, f32[32,1024]{1,0:T(8,128)S(1)}, u32[]{:S(2)}, u32[]{:S(2)}) %collective-permute-start.6) | collective-permute-done | bytes 131104 | tf_op jit(solution)/shard_map/ppermute | solution.py:18
  51.0 3.9 %collective-permute-done.7 = f32[32,512]{1,0:T(8,128)S(1)} collective-permute-done((f32[32,512]{1,0:T(8,128)S(1)}, f32[32,512]{1,0:T(8,128)S(1)}, u32[]{:S(2)}, u32[]{:S(2)}) %collective-permute-start.7) | collective-permute-done | bytes 65568 | tf_op jit(solution)/shard_map/ppermute | solution.py:18
  55.5 2.8 %collective-permute-start.8 = (f32[128,128]{0,1:T(8,128)S(1)}, f32[128,128]{0,1:T(8,128)S(1)}, u32[]{:S(2)}, u32[]{:S(2)}) collective-permute-start(f32[128,128]{0,1:T(8,128)S(1)} %select_maximum_fusion), channel_id=1, source_target_pairs={{0,4},{4,0},{8,12},{12,8},{16,20},{20,16},{24,28},{28,24},{32,36},... | collective-permute-start | bytes 196616 | tf_op jit(solution)/shard_map/ppermute | solution.py:18
  59.4 4.3 %collective-permute-done.9 = f32[128,128]{0,1:T(8,128)S(1)} collective-permute-done((f32[128,128]{0,1:T(8,128)S(1)}, f32[128,128]{0,1:T(8,128)S(1)}, u32[]{:S(2)}, u32[]{:S(2)}) %collective-permute-start.9) | collective-permute-done | bytes 65568 | tf_op jit(solution)/shard_map/ppermute | solution.py:18
  64.8 4.5 %collective-permute-done.10 = f32[128,128]{0,1:T(8,128)S(1)} collective-permute-done((f32[128,128]{0,1:T(8,128)S(1)}, f32[128,128]{0,1:T(8,128)S(1)}, u32[]{:S(2)}, u32[]{:S(2)}) %collective-permute-start.10) | collective-permute-done | bytes 65568 | tf_op jit(solution)/shard_map/ppermute | solution.py:18
  69.5 4.2 %collective-permute-done.11 = f32[128,128]{0,1:T(8,128)S(1)} collective-permute-done((f32[128,128]{0,1:T(8,128)S(1)}, f32[128,128]{0,1:T(8,128)S(1)}, u32[]{:S(2)}, u32[]{:S(2)}) %collective-permute-start.11) | collective-permute-done | bytes 65568 | tf_op jit(solution)/shard_map/ppermute | solution.py:18
  73.7 7.0 %collective-permute-start.12 = (f32[128,128]{0,1:T(8,128)S(1)}, f32[128,128]{0,1:T(8,128)S(1)}, u32[]{:S(2)}, u32[]{:S(2)}) collective-permute-start(f32[128,128]{0,1:T(8,128)S(1)} %add.127), channel_id=1, source_target_pairs={{0,64},{4,68},{8,72},{12,76},{16,80},{20,84},{24,88},{28,92},{32,9... | collective-permute-start | bytes 196616 | tf_op jit(solution)/shard_map/ppermute | solution.py:18
  80.7 2.2 %collective-permute-done.12 = f32[128,128]{0,1:T(8,128)S(1)} collective-permute-done((f32[128,128]{0,1:T(8,128)S(1)}, f32[128,128]{0,1:T(8,128)S(1)}, u32[]{:S(2)}, u32[]{:S(2)}) %collective-permute-start.12) | collective-permute-done | bytes 65568 | tf_op jit(solution)/shard_map/ppermute | solution.py:18
  83.0 6.6 %collective-permute-done.13 = f32[128,128]{0,1:T(8,128)S(1)} collective-permute-done((f32[128,128]{0,1:T(8,128)S(1)}, f32[128,128]{0,1:T(8,128)S(1)}, u32[]{:S(2)}, u32[]{:S(2)}) %collective-permute-start.13) | collective-permute-done | bytes 65568 | tf_op jit(solution)/shard_map/ppermute | solution.py:18
  90.0 4.0 %collective-permute-done.14 = f32[128,128]{0,1:T(8,128)S(1)} collective-permute-done((f32[128,128]{0,1:T(8,128)S(1)}, f32[128,128]{0,1:T(8,128)S(1)}, u32[]{:S(2)}, u32[]{:S(2)}) %collective-permute-start.14) | collective-permute-done | bytes 65568 | tf_op jit(solution)/shard_map/ppermute | solution.py:18
  94.0 3.0 %collective-permute-start.15 = (f32[128,128]{0,1:T(8,128)S(1)}, f32[128,128]{0,1:T(8,128)S(1)}, u32[]{:S(2)}, u32[]{:S(2)}) collective-permute-start(f32[128,128]{0,1:T(8,128)S(1)} %add.130), channel_id=1, source_target_pairs={{0,3},{1,2},{2,1},{3,0},{4,7},{5,6},{6,5},{7,4},{8,11},{9,10},{10,... | collective-permute-start | bytes 196616 | tf_op jit(solution)/shard_map/ppermute | solution.py:18
  97.0 2.5 %collective-permute-done.15 = f32[128,128]{0,1:T(8,128)S(1)} collective-permute-done((f32[128,128]{0,1:T(8,128)S(1)}, f32[128,128]{0,1:T(8,128)S(1)}, u32[]{:S(2)}, u32[]{:S(2)}) %collective-permute-start.15) | collective-permute-done | bytes 65568 | tf_op jit(solution)/shard_map/ppermute | solution.py:18
  101.8 4.7 %shard_map.67 = f32[32,64]{1,0:T(8,128)} custom-call(f32[32,64]{1,0:T(8,128)} %pad_maximum_fusion.aug_ref), custom_call_target="tpu_custom_call" | custom-call | tf_op jit(solution)/shard_map/pallas_call | solution.py:87
  (70 shorter events, 19.5 us)
Async XLA Ops:
  1.5 4.3 %collective-permute-start = (f32[32,512]{1,0:T(8,128)S(1)}, f32[32,512]{1,0:T(8,128)S(1)}, u32[]{:S(2)}, u32[]{:S(2)}) collective-permute-start(f32[32,512]{1,0:T(8,128)S(1)} %bitcast.59), channel_id=1, source_target_pairs={{0,1},{1,0},{2,3},{3,2},{4,5},{5,4},{6,7},{7,6},{8,9},{9,8},{10,11... | collective-permute-start | bytes 196616 | tf_op jit(solution)/shard_map/ppermute | solution.py:18
  5.8 6.3 %collective-permute-start.1 = (f32[32,1024]{1,0:T(8,128)S(1)}, f32[32,1024]{1,0:T(8,128)S(1)}, u32[]{:S(2)}, u32[]{:S(2)}) collective-permute-start(f32[32,1024]{1,0:T(8,128)S(1)} %maximum_select_fusion.1), channel_id=1, source_target_pairs={{0,3},{1,2},{2,1},{3,0},{4,7},{5,6},{6,5},{7,4},{8,11},{9,10},{10,... | collective-permute-start | bytes 393224 | tf_op jit(solution)/shard_map/ppermute | solution.py:18
  15.4 15.0 %copy-start = (f32[1,768,3072]{2,1,0:T(8,128)S(1)}, f32[1,768,3072]{2,1,0:T(8,128)}, u32[]{:S(2)}) copy-start(f32[1,768,3072]{2,1,0:T(8,128)} %param.5) | copy-start | bytes 28311556
  15.4 11.5 %collective-permute-start.2 = (f32[32,512]{1,0:T(8,128)S(1)}, f32[32,512]{1,0:T(8,128)S(1)}, u32[]{:S(2)}, u32[]{:S(2)}) collective-permute-start(f32[32,512]{1,0:T(8,128)S(1)} %get-tuple-element.16), channel_id=1, source_target_pairs={{0,4},{4,8},{8,12},{12,16},{16,20},{20,24},{24,28},{28,32},{32,36}... | collective-permute-start | bytes 196616 | tf_op jit(solution)/shard_map/ppermute | solution.py:13
  17.7 9.1 %collective-permute-start.3 = (f32[32,512]{1,0:T(8,128)S(1)}, f32[32,512]{1,0:T(8,128)S(1)}, u32[]{:S(2)}, u32[]{:S(2)}) collective-permute-start(f32[32,512]{1,0:T(8,128)S(1)} %get-tuple-element.17), channel_id=1, source_target_pairs={{4,0},{8,4},{12,8},{16,12},{20,16},{24,20},{28,24},{32,28},{36,32}... | collective-permute-start | bytes 196616 | tf_op jit(solution)/shard_map/ppermute | solution.py:13
  30.4 20.3 %copy-start.1 = (f32[96,1,512]{2,1,0:T(1,128)S(1)}, f32[96,1,512]{2,1,0:T(1,128)}, u32[]{:S(2)}) copy-start(f32[96,1,512]{2,1,0:T(1,128)} %param.6) | copy-start | bytes 589828
  31.5 7.8 %collective-permute-start.5 = (f32[32,512]{1,0:T(8,128)S(1)}, f32[32,512]{1,0:T(8,128)S(1)}, u32[]{:S(2)}, u32[]{:S(2)}) collective-permute-start(f32[32,512]{1,0:T(8,128)S(1)} %get-tuple-element.15), channel_id=1, source_target_pairs={{0,4},{4,8},{8,12},{12,16},{16,20},{20,24},{24,28},{28,32},{32,36}... | collective-permute-start | bytes 196616 | tf_op jit(solution)/shard_map/ppermute | solution.py:13
  36.0 6.4 %collective-permute-start.4 = (f32[32,512]{1,0:T(8,128)S(1)}, f32[32,512]{1,0:T(8,128)S(1)}, u32[]{:S(2)}, u32[]{:S(2)}) collective-permute-start(f32[32,512]{1,0:T(8,128)S(1)} %get-tuple-element.14), channel_id=1, source_target_pairs={{4,0},{8,4},{12,8},{16,12},{20,16},{24,20},{28,24},{32,28},{36,32}... | collective-permute-start | bytes 196616 | tf_op jit(solution)/shard_map/ppermute | solution.py:13
  44.1 6.3 %collective-permute-start.6 = (f32[32,1024]{1,0:T(8,128)S(1)}, f32[32,1024]{1,0:T(8,128)S(1)}, u32[]{:S(2)}, u32[]{:S(2)}) collective-permute-start(f32[32,1024]{1,0:T(8,128)S(1)} %constant_dynamic-slice_fusion.1), channel_id=1, source_target_pairs={{0,3},{1,2},{2,1},{3,0},{4,7},{5,6},{6,5},{7,4},{8,11},{9,10},{10,... | collective-permute-start | bytes 393224 | tf_op jit(solution)/shard_map/ppermute | solution.py:18
  50.4 4.5 %collective-permute-start.7 = (f32[32,512]{1,0:T(8,128)S(1)}, f32[32,512]{1,0:T(8,128)S(1)}, u32[]{:S(2)}, u32[]{:S(2)}) collective-permute-start(f32[32,512]{1,0:T(8,128)S(1)} %constant_dynamic-slice_fusion), channel_id=1, source_target_pairs={{0,1},{1,0},{2,3},{3,2},{4,5},{5,4},{6,7},{7,6},{8,9},{9,8},{10,11... | collective-permute-start | bytes 196616 | tf_op jit(solution)/shard_map/ppermute | solution.py:18
  55.5 3.7 %collective-permute-start.8 = (f32[128,128]{0,1:T(8,128)S(1)}, f32[128,128]{0,1:T(8,128)S(1)}, u32[]{:S(2)}, u32[]{:S(2)}) collective-permute-start(f32[128,128]{0,1:T(8,128)S(1)} %select_maximum_fusion), channel_id=1, source_target_pairs={{0,4},{4,0},{8,12},{12,8},{16,20},{20,16},{24,28},{28,24},{32,36},... | collective-permute-start | bytes 196616 | tf_op jit(solution)/shard_map/ppermute | solution.py:18
  59.4 4.4 %collective-permute-start.9 = (f32[128,128]{0,1:T(8,128)S(1)}, f32[128,128]{0,1:T(8,128)S(1)}, u32[]{:S(2)}, u32[]{:S(2)}) collective-permute-start(f32[128,128]{0,1:T(8,128)S(1)} %fusion.69), channel_id=1, source_target_pairs={{0,8},{4,12},{8,0},{12,4},{16,24},{20,28},{24,16},{28,20},{32,40},... | collective-permute-start | bytes 196616 | tf_op jit(solution)/shard_map/ppermute | solution.py:18
  63.8 5.6 %collective-permute-start.10 = (f32[128,128]{0,1:T(8,128)S(1)}, f32[128,128]{0,1:T(8,128)S(1)}, u32[]{:S(2)}, u32[]{:S(2)}) collective-permute-start(f32[128,128]{0,1:T(8,128)S(1)} %add.125), channel_id=1, source_target_pairs={{0,24},{4,28},{8,16},{12,20},{16,8},{20,12},{24,0},{28,4},{32,56},... | collective-permute-start | bytes 196616 | tf_op jit(solution)/shard_map/ppermute | solution.py:18
  69.3 4.4 %collective-permute-start.11 = (f32[128,128]{0,1:T(8,128)S(1)}, f32[128,128]{0,1:T(8,128)S(1)}, u32[]{:S(2)}, u32[]{:S(2)}) collective-permute-start(f32[128,128]{0,1:T(8,128)S(1)} %add.126), channel_id=1, source_target_pairs={{0,32},{4,36},{8,40},{12,44},{16,48},{20,52},{24,56},{28,60},{32,0... | collective-permute-start | bytes 196616 | tf_op jit(solution)/shard_map/ppermute | solution.py:18
  73.7 9.2 %collective-permute-start.12 = (f32[128,128]{0,1:T(8,128)S(1)}, f32[128,128]{0,1:T(8,128)S(1)}, u32[]{:S(2)}, u32[]{:S(2)}) collective-permute-start(f32[128,128]{0,1:T(8,128)S(1)} %add.127), channel_id=1, source_target_pairs={{0,64},{4,68},{8,72},{12,76},{16,80},{20,84},{24,88},{28,92},{32,9... | collective-permute-start | bytes 196616 | tf_op jit(solution)/shard_map/ppermute | solution.py:18
  82.9 6.7 %collective-permute-start.13 = (f32[128,128]{0,1:T(8,128)S(1)}, f32[128,128]{0,1:T(8,128)S(1)}, u32[]{:S(2)}, u32[]{:S(2)}) collective-permute-start(f32[128,128]{0,1:T(8,128)S(1)} %add.128), channel_id=1, source_target_pairs={{0,192},{4,196},{8,200},{12,204},{16,208},{20,212},{24,216},{28,22... | collective-permute-start | bytes 196616 | tf_op jit(solution)/shard_map/ppermute | solution.py:18
  89.6 4.4 %collective-permute-start.14 = (f32[128,128]{0,1:T(8,128)S(1)}, f32[128,128]{0,1:T(8,128)S(1)}, u32[]{:S(2)}, u32[]{:S(2)}) collective-permute-start(f32[128,128]{0,1:T(8,128)S(1)} %add.129), channel_id=1, source_target_pairs={{0,1},{1,0},{2,3},{3,2},{4,5},{5,4},{6,7},{7,6},{8,9},{9,8},{10,11... | collective-permute-start | bytes 196616 | tf_op jit(solution)/shard_map/ppermute | solution.py:18
  94.0 5.6 %collective-permute-start.15 = (f32[128,128]{0,1:T(8,128)S(1)}, f32[128,128]{0,1:T(8,128)S(1)}, u32[]{:S(2)}, u32[]{:S(2)}) collective-permute-start(f32[128,128]{0,1:T(8,128)S(1)} %add.130), channel_id=1, source_target_pairs={{0,3},{1,2},{2,1},{3,0},{4,7},{5,6},{6,5},{7,4},{8,11},{9,10},{10,... | collective-permute-start | bytes 196616 | tf_op jit(solution)/shard_map/ppermute | solution.py:18
  99.8 8.3 %copy-start.2 = (f32[96,32]{0,1:T(8,128)}, f32[96,32]{0,1:T(8,128)S(1)}, u32[]{:S(2)}) copy-start(f32[96,32]{0,1:T(8,128)S(1)} %get-tuple-element.20) | copy-start | bytes 36868

commit v8 on v6

--- a/solution.py
+++ b/solution.py
@@ -129,8 +129,8 @@
     select_lower = (index_rows[0][:, None] == all_rows[None, :]).astype(jnp.float32)
     gathered = (
         own_value
-        + jnp.dot(back_upper, select_upper, precision=HIGH)
-        + jnp.dot(back_lower, select_lower, precision=HIGH)
+        + jnp.dot(back_upper, select_upper, precision=three)
+        + jnp.dot(back_lower, select_lower, precision=three)
     )
     block_t = scatter_rows(gathered, "row")
     vectors = basis[:, 0, :]

time: 108 us -> 108 us (level)
  no operation moved by 1% of the time
where the time goes in v8:
time: 108 us; the launch traced here: 107 us
  waiting for transfers between devices  43 us (40%)
  starting transfers between devices  34.1 us (32%)
  matrix products  18 us (17%)
  local copies, waits for them, and re-layouts  5.23 us (5%)
  Pallas kernels  4.68 us (4%)
    ppermute x12, waiting for transfers between devices, swap(): lax.ppermute(value, axis, [(source, source ^ mask) for source in range(co...  41.3 us
    ppermute x12, starting transfers between devices, swap(): lax.ppermute(value, axis, [(source, source ^ mask) for source in range(co...  22.7 us
    ppermute x4, starting transfers between devices, from_behind(): lax.ppermute(value, axis, [(source, source + steps) for source in range(l...  11.4 us
    dot_general x1, matrix products, per_device(): lax.dot_general(whole, factor_rows[:, :sub_rows], by_rows, precision=three)  5.6 us
    pallas_call x1, Pallas kernels, cholesky_parts(): pl.pallas_call(factor_kernel, out_shape=(shape, shape))  4.68 us
    dot_general x1, matrix products, per_device(): lax.dot_general(margins, factor_rows[:, sub_rows:], by_rows, precision=th...  3.35 us
    dot_general x1, matrix products, per_device(): jnp.dot(inner, factor_rows[:, :sub_rows], precision=three)  2.22 us
  transfers between devices with their start and end apart: 16, of which 13 were waited for; matrix products, arithmetic and copies ran while one was open for 11% of the time, Pallas kernels for 0%

profile of v8, /device:TPU:38, one launch (start us, length us, event | category | flops | bytes accessed | tf_op | source)
XLA Modules:
  0.0 107.0 jit_solution(14669057879885029949)
XLA Ops:
  3.8 1.9 %collective-permute-done = f32[32,512]{1,0:T(8,128)S(1)} collective-permute-done((f32[32,512]{1,0:T(8,128)S(1)}, f32[32,512]{1,0:T(8,128)S(1)}, u32[]{:S(2)}, u32[]{:S(2)}) %collective-permute-start) | collective-permute-done | bytes 65568 | tf_op jit(solution)/shard_map/ppermute | solution.py:18
  5.8 3.1 %collective-permute-start.1 = (f32[32,1024]{1,0:T(8,128)S(1)}, f32[32,1024]{1,0:T(8,128)S(1)}, u32[]{:S(2)}, u32[]{:S(2)}) collective-permute-start(f32[32,1024]{1,0:T(8,128)S(1)} %maximum_select_fusion.1), channel_id=1, source_target_pairs={{0,3},{1,2},{2,1},{3,0},{4,7},{5,6},{6,5},{7,4},{8,11},{9,10},{10,... | collective-permute-start | bytes 393224 | tf_op jit(solution)/shard_map/ppermute | solution.py:18
  8.9 3.1 %collective-permute-done.1 = f32[32,1024]{1,0:T(8,128)S(1)} collective-permute-done((f32[32,1024]{1,0:T(8,128)S(1)}, f32[32,1024]{1,0:T(8,128)S(1)}, u32[]{:S(2)}, u32[]{:S(2)}) %collective-permute-start.1) | collective-permute-done | bytes 131104 | tf_op jit(solution)/shard_map/ppermute | solution.py:18
  13.6 1.9 %collective-permute-start.2 = (f32[32,512]{1,0:T(8,128)S(1)}, f32[32,512]{1,0:T(8,128)S(1)}, u32[]{:S(2)}, u32[]{:S(2)}) collective-permute-start(f32[32,512]{1,0:T(8,128)S(1)} %select_bitcast_fusion.1), channel_id=1, source_target_pairs={{0,4},{4,8},{8,12},{12,16},{16,20},{20,24},{24,28},{28,32},{32,36}... | collective-permute-start | bytes 196616 | tf_op jit(solution)/shard_map/ppermute | solution.py:13
  16.6 3.9 %collective-permute-start.3 = (f32[32,512]{1,0:T(8,128)S(1)}, f32[32,512]{1,0:T(8,128)S(1)}, u32[]{:S(2)}, u32[]{:S(2)}) collective-permute-start(f32[32,512]{1,0:T(8,128)S(1)} %select_bitcast_fusion), channel_id=1, source_target_pairs={{4,0},{8,4},{12,8},{16,12},{20,16},{24,20},{28,24},{32,28},{36,32}... | collective-permute-start | bytes 196616 | tf_op jit(solution)/shard_map/ppermute | solution.py:13
  20.6 5.6 %fusion.2 = f32[32,768]{1,0:T(8,128)S(1)} fusion(f32[32,2048]{1,0:T(8,128)S(1)} %maximum_select_fusion, f32[768,3072]{1,0:T(8,128)} %bitcast.51), kind=kOutput, calls=%fused_computation.4 | convolution fusion | flops 301989888 | bytes 6651904 | tf_op jit(solution)/shard_map/dot_general | solution.py:114
  26.2 3.4 %fusion.8 = f32[32,768]{1,0:T(8,128)S(1)} fusion(f32[768,3072]{1,0:T(8,128)} %bitcast.52, f32[32,512]{1,0:T(8,128)S(1)} %collective-permute-done.3, f32[32,512]{1,0:T(8,128)S(1)} %collective-permute-done.2), kind=kOutput, calls=%fused_computation.12 | convolution fusion | flops 151027712 | bytes 3375104 | tf_op jit(solution)/shard_map/dot_general | solution.py:119
  30.8 2.6 %collective-permute-start.5 = (f32[32,512]{1,0:T(8,128)S(1)}, f32[32,512]{1,0:T(8,128)S(1)}, u32[]{:S(2)}, u32[]{:S(2)}) collective-permute-start(f32[32,512]{1,0:T(8,128)S(1)} %get-tuple-element.20), channel_id=1, source_target_pairs={{0,4},{4,8},{8,12},{12,16},{16,20},{20,24},{24,28},{28,32},{32,36}... | collective-permute-start | bytes 196616 | tf_op jit(solution)/shard_map/ppermute | solution.py:13
  33.4 2.2 %fusion.12 = f32[32,2048]{1,0:T(8,128)S(1)} fusion(f32[32,768]{1,0:T(8,128)S(1)} %get-tuple-element.18, f32[768,3072]{1,0:T(8,128)S(1)} %bitcast.54, f32[32,3072]{1,0:T(8,128)S(1)} %get-tuple-element.17), kind=kOutput, calls=%fused_computation.16 | convolution fusion | flops 302055424 | bytes 6914048 | tf_op jit(solution)/shard_map/dot_general | solution.py:126
  35.7 3.0 %collective-permute-start.4 = (f32[32,512]{1,0:T(8,128)S(1)}, f32[32,512]{1,0:T(8,128)S(1)}, u32[]{:S(2)}, u32[]{:S(2)}) collective-permute-start(f32[32,512]{1,0:T(8,128)S(1)} %get-tuple-element.19), channel_id=1, source_target_pairs={{4,0},{8,4},{12,8},{16,12},{20,16},{24,20},{28,24},{32,28},{36,32}... | collective-permute-start | bytes 196616 | tf_op jit(solution)/shard_map/ppermute | solution.py:13
  43.1 3.1 %collective-permute-start.6 = (f32[32,1024]{1,0:T(8,128)S(1)}, f32[32,1024]{1,0:T(8,128)S(1)}, u32[]{:S(2)}, u32[]{:S(2)}) collective-permute-start(f32[32,1024]{1,0:T(8,128)S(1)} %constant_dynamic-slice_fusion.1), channel_id=1, source_target_pairs={{0,3},{1,2},{2,1},{3,0},{4,7},{5,6},{6,5},{7,4},{8,11},{9,10},{10,... | collective-permute-start | bytes 393224 | tf_op jit(solution)/shard_map/ppermute | solution.py:18
  46.1 3.2 %collective-permute-done.6 = f32[32,1024]{1,0:T(8,128)S(1)} collective-permute-done((f32[32,1024]{1,0:T(8,128)S(1)}, f32[32,1024]{1,0:T(8,128)S(1)}, u32[]{:S(2)}, u32[]{:S(2)}) %collective-permute-start.6) | collective-permute-done | bytes 131104 | tf_op jit(solution)/shard_map/ppermute | solution.py:18
  50.0 3.9 %collective-permute-done.7 = f32[32,512]{1,0:T(8,128)S(1)} collective-permute-done((f32[32,512]{1,0:T(8,128)S(1)}, f32[32,512]{1,0:T(8,128)S(1)}, u32[]{:S(2)}, u32[]{:S(2)}) %collective-permute-start.7) | collective-permute-done | bytes 65568 | tf_op jit(solution)/shard_map/ppermute | solution.py:18
  54.5 2.8 %collective-permute-start.8 = (f32[128,128]{0,1:T(8,128)S(1)}, f32[128,128]{0,1:T(8,128)S(1)}, u32[]{:S(2)}, u32[]{:S(2)}) collective-permute-start(f32[128,128]{0,1:T(8,128)S(1)} %select_maximum_fusion), channel_id=1, source_target_pairs={{0,4},{4,0},{8,12},{12,8},{16,20},{20,16},{24,28},{28,24},{32,36},... | collective-permute-start | bytes 196616 | tf_op jit(solution)/shard_map/ppermute | solution.py:18
  58.4 4.3 %collective-permute-done.9 = f32[128,128]{0,1:T(8,128)S(1)} collective-permute-done((f32[128,128]{0,1:T(8,128)S(1)}, f32[128,128]{0,1:T(8,128)S(1)}, u32[]{:S(2)}, u32[]{:S(2)}) %collective-permute-start.9) | collective-permute-done | bytes 65568 | tf_op jit(solution)/shard_map/ppermute | solution.py:18
  63.8 4.5 %collective-permute-done.10 = f32[128,128]{0,1:T(8,128)S(1)} collective-permute-done((f32[128,128]{0,1:T(8,128)S(1)}, f32[128,128]{0,1:T(8,128)S(1)}, u32[]{:S(2)}, u32[]{:S(2)}) %collective-permute-start.10) | collective-permute-done | bytes 65568 | tf_op jit(solution)/shard_map/ppermute | solution.py:18
  68.5 4.2 %collective-permute-done.11 = f32[128,128]{0,1:T(8,128)S(1)} collective-permute-done((f32[128,128]{0,1:T(8,128)S(1)}, f32[128,128]{0,1:T(8,128)S(1)}, u32[]{:S(2)}, u32[]{:S(2)}) %collective-permute-start.11) | collective-permute-done | bytes 65568 | tf_op jit(solution)/shard_map/ppermute | solution.py:18
  72.7 7.0 %collective-permute-start.12 = (f32[128,128]{0,1:T(8,128)S(1)}, f32[128,128]{0,1:T(8,128)S(1)}, u32[]{:S(2)}, u32[]{:S(2)}) collective-permute-start(f32[128,128]{0,1:T(8,128)S(1)} %add.108), channel_id=1, source_target_pairs={{0,64},{4,68},{8,72},{12,76},{16,80},{20,84},{24,88},{28,92},{32,9... | collective-permute-start | bytes 196616 | tf_op jit(solution)/shard_map/ppermute | solution.py:18
  79.7 2.2 %collective-permute-done.12 = f32[128,128]{0,1:T(8,128)S(1)} collective-permute-done((f32[128,128]{0,1:T(8,128)S(1)}, f32[128,128]{0,1:T(8,128)S(1)}, u32[]{:S(2)}, u32[]{:S(2)}) %collective-permute-start.12) | collective-permute-done | bytes 65568 | tf_op jit(solution)/shard_map/ppermute | solution.py:18
  82.0 6.6 %collective-permute-done.13 = f32[128,128]{0,1:T(8,128)S(1)} collective-permute-done((f32[128,128]{0,1:T(8,128)S(1)}, f32[128,128]{0,1:T(8,128)S(1)}, u32[]{:S(2)}, u32[]{:S(2)}) %collective-permute-start.13) | collective-permute-done | bytes 65568 | tf_op jit(solution)/shard_map/ppermute | solution.py:18
  89.0 4.0 %collective-permute-done.14 = f32[128,128]{0,1:T(8,128)S(1)} collective-permute-done((f32[128,128]{0,1:T(8,128)S(1)}, f32[128,128]{0,1:T(8,128)S(1)}, u32[]{:S(2)}, u32[]{:S(2)}) %collective-permute-start.14) | collective-permute-done | bytes 65568 | tf_op jit(solution)/shard_map/ppermute | solution.py:18
  93.0 3.0 %collective-permute-start.15 = (f32[128,128]{0,1:T(8,128)S(1)}, f32[128,128]{0,1:T(8,128)S(1)}, u32[]{:S(2)}, u32[]{:S(2)}) collective-permute-start(f32[128,128]{0,1:T(8,128)S(1)} %add.111), channel_id=1, source_target_pairs={{0,3},{1,2},{2,1},{3,0},{4,7},{5,6},{6,5},{7,4},{8,11},{9,10},{10,... | collective-permute-start | bytes 196616 | tf_op jit(solution)/shard_map/ppermute | solution.py:18
  96.0 2.5 %collective-permute-done.15 = f32[128,128]{0,1:T(8,128)S(1)} collective-permute-done((f32[128,128]{0,1:T(8,128)S(1)}, f32[128,128]{0,1:T(8,128)S(1)}, u32[]{:S(2)}, u32[]{:S(2)}) %collective-permute-start.15) | collective-permute-done | bytes 65568 | tf_op jit(solution)/shard_map/ppermute | solution.py:18
  100.7 4.7 %shard_map.67 = (f32[32,32]{1,0:T(8,128)}, f32[32,32]{1,0:T(8,128)}) custom-call(f32[32,32]{1,0:T(8,128)} %fusion.38.gram_ref), custom_call_target="tpu_custom_call" | custom-call | tf_op jit(solution)/shard_map/pallas_call | solution.py:92
  (69 shorter events, 19.2 us)
Async XLA Ops:
  1.5 4.3 %collective-permute-start = (f32[32,512]{1,0:T(8,128)S(1)}, f32[32,512]{1,0:T(8,128)S(1)}, u32[]{:S(2)}, u32[]{:S(2)}) collective-permute-start(f32[32,512]{1,0:T(8,128)S(1)} %bitcast.55), channel_id=1, source_target_pairs={{0,1},{1,0},{2,3},{3,2},{4,5},{5,4},{6,7},{7,6},{8,9},{9,8},{10,11... | collective-permute-start | bytes 196616 | tf_op jit(solution)/shard_map/ppermute | solution.py:18
  5.8 6.3 %collective-permute-start.1 = (f32[32,1024]{1,0:T(8,128)S(1)}, f32[32,1024]{1,0:T(8,128)S(1)}, u32[]{:S(2)}, u32[]{:S(2)}) collective-permute-start(f32[32,1024]{1,0:T(8,128)S(1)} %maximum_select_fusion.1), channel_id=1, source_target_pairs={{0,3},{1,2},{2,1},{3,0},{4,7},{5,6},{6,5},{7,4},{8,11},{9,10},{10,... | collective-permute-start | bytes 393224 | tf_op jit(solution)/shard_map/ppermute | solution.py:18
  13.6 12.6 %collective-permute-start.2 = (f32[32,512]{1,0:T(8,128)S(1)}, f32[32,512]{1,0:T(8,128)S(1)}, u32[]{:S(2)}, u32[]{:S(2)}) collective-permute-start(f32[32,512]{1,0:T(8,128)S(1)} %select_bitcast_fusion.1), channel_id=1, source_target_pairs={{0,4},{4,8},{8,12},{12,16},{16,20},{20,24},{24,28},{28,32},{32,36}... | collective-permute-start | bytes 196616 | tf_op jit(solution)/shard_map/ppermute | solution.py:13
  16.6 13.0 %copy-start = (f32[1,768,3072]{2,1,0:T(8,128)S(1)}, f32[1,768,3072]{2,1,0:T(8,128)}, u32[]{:S(2)}) copy-start(f32[1,768,3072]{2,1,0:T(8,128)} %param.7) | copy-start | bytes 28311556
  16.6 9.5 %collective-permute-start.3 = (f32[32,512]{1,0:T(8,128)S(1)}, f32[32,512]{1,0:T(8,128)S(1)}, u32[]{:S(2)}, u32[]{:S(2)}) collective-permute-start(f32[32,512]{1,0:T(8,128)S(1)} %select_bitcast_fusion), channel_id=1, source_target_pairs={{4,0},{8,4},{12,8},{16,12},{20,16},{24,20},{28,24},{32,28},{36,32}... | collective-permute-start | bytes 196616 | tf_op jit(solution)/shard_map/ppermute | solution.py:13
  29.7 20.0 %copy-start.1 = (f32[96,1,512]{2,1,0:T(1,128)S(1)}, f32[96,1,512]{2,1,0:T(1,128)}, u32[]{:S(2)}) copy-start(f32[96,1,512]{2,1,0:T(1,128)} %param.8) | copy-start | bytes 589828
  30.8 7.8 %collective-permute-start.5 = (f32[32,512]{1,0:T(8,128)S(1)}, f32[32,512]{1,0:T(8,128)S(1)}, u32[]{:S(2)}, u32[]{:S(2)}) collective-permute-start(f32[32,512]{1,0:T(8,128)S(1)} %get-tuple-element.20), channel_id=1, source_target_pairs={{0,4},{4,8},{8,12},{12,16},{16,20},{20,24},{24,28},{28,32},{32,36}... | collective-permute-start | bytes 196616 | tf_op jit(solution)/shard_map/ppermute | solution.py:13
  35.7 6.0 %collective-permute-start.4 = (f32[32,512]{1,0:T(8,128)S(1)}, f32[32,512]{1,0:T(8,128)S(1)}, u32[]{:S(2)}, u32[]{:S(2)}) collective-permute-start(f32[32,512]{1,0:T(8,128)S(1)} %get-tuple-element.19), channel_id=1, source_target_pairs={{4,0},{8,4},{12,8},{16,12},{20,16},{24,20},{28,24},{32,28},{36,32}... | collective-permute-start | bytes 196616 | tf_op jit(solution)/shard_map/ppermute | solution.py:13
  43.1 6.3 %collective-permute-start.6 = (f32[32,1024]{1,0:T(8,128)S(1)}, f32[32,1024]{1,0:T(8,128)S(1)}, u32[]{:S(2)}, u32[]{:S(2)}) collective-permute-start(f32[32,1024]{1,0:T(8,128)S(1)} %constant_dynamic-slice_fusion.1), channel_id=1, source_target_pairs={{0,3},{1,2},{2,1},{3,0},{4,7},{5,6},{6,5},{7,4},{8,11},{9,10},{10,... | collective-permute-start | bytes 393224 | tf_op jit(solution)/shard_map/ppermute | solution.py:18
  49.4 4.5 %collective-permute-start.7 = (f32[32,512]{1,0:T(8,128)S(1)}, f32[32,512]{1,0:T(8,128)S(1)}, u32[]{:S(2)}, u32[]{:S(2)}) collective-permute-start(f32[32,512]{1,0:T(8,128)S(1)} %constant_dynamic-slice_fusion), channel_id=1, source_target_pairs={{0,1},{1,0},{2,3},{3,2},{4,5},{5,4},{6,7},{7,6},{8,9},{9,8},{10,11... | collective-permute-start | bytes 196616 | tf_op jit(solution)/shard_map/ppermute | solution.py:18
  54.5 3.7 %collective-permute-start.8 = (f32[128,128]{0,1:T(8,128)S(1)}, f32[128,128]{0,1:T(8,128)S(1)}, u32[]{:S(2)}, u32[]{:S(2)}) collective-permute-start(f32[128,128]{0,1:T(8,128)S(1)} %select_maximum_fusion), channel_id=1, source_target_pairs={{0,4},{4,0},{8,12},{12,8},{16,20},{20,16},{24,28},{28,24},{32,36},... | collective-permute-start | bytes 196616 | tf_op jit(solution)/shard_map/ppermute | solution.py:18
  58.3 4.4 %collective-permute-start.9 = (f32[128,128]{0,1:T(8,128)S(1)}, f32[128,128]{0,1:T(8,128)S(1)}, u32[]{:S(2)}, u32[]{:S(2)}) collective-permute-start(f32[128,128]{0,1:T(8,128)S(1)} %fusion.67), channel_id=1, source_target_pairs={{0,8},{4,12},{8,0},{12,4},{16,24},{20,28},{24,16},{28,20},{32,40},... | collective-permute-start | bytes 196616 | tf_op jit(solution)/shard_map/ppermute | solution.py:18
  62.7 5.6 %collective-permute-start.10 = (f32[128,128]{0,1:T(8,128)S(1)}, f32[128,128]{0,1:T(8,128)S(1)}, u32[]{:S(2)}, u32[]{:S(2)}) collective-permute-start(f32[128,128]{0,1:T(8,128)S(1)} %add.106), channel_id=1, source_target_pairs={{0,24},{4,28},{8,16},{12,20},{16,8},{20,12},{24,0},{28,4},{32,56},... | collective-permute-start | bytes 196616 | tf_op jit(solution)/shard_map/ppermute | solution.py:18
  68.3 4.4 %collective-permute-start.11 = (f32[128,128]{0,1:T(8,128)S(1)}, f32[128,128]{0,1:T(8,128)S(1)}, u32[]{:S(2)}, u32[]{:S(2)}) collective-permute-start(f32[128,128]{0,1:T(8,128)S(1)} %add.107), channel_id=1, source_target_pairs={{0,32},{4,36},{8,40},{12,44},{16,48},{20,52},{24,56},{28,60},{32,0... | collective-permute-start | bytes 196616 | tf_op jit(solution)/shard_map/ppermute | solution.py:18
  72.7 9.2 %collective-permute-start.12 = (f32[128,128]{0,1:T(8,128)S(1)}, f32[128,128]{0,1:T(8,128)S(1)}, u32[]{:S(2)}, u32[]{:S(2)}) collective-permute-start(f32[128,128]{0,1:T(8,128)S(1)} %add.108), channel_id=1, source_target_pairs={{0,64},{4,68},{8,72},{12,76},{16,80},{20,84},{24,88},{28,92},{32,9... | collective-permute-start | bytes 196616 | tf_op jit(solution)/shard_map/ppermute | solution.py:18
  81.9 6.7 %collective-permute-start.13 = (f32[128,128]{0,1:T(8,128)S(1)}, f32[128,128]{0,1:T(8,128)S(1)}, u32[]{:S(2)}, u32[]{:S(2)}) collective-permute-start(f32[128,128]{0,1:T(8,128)S(1)} %add.109), channel_id=1, source_target_pairs={{0,192},{4,196},{8,200},{12,204},{16,208},{20,212},{24,216},{28,22... | collective-permute-start | bytes 196616 | tf_op jit(solution)/shard_map/ppermute | solution.py:18
  88.6 4.4 %collective-permute-start.14 = (f32[128,128]{0,1:T(8,128)S(1)}, f32[128,128]{0,1:T(8,128)S(1)}, u32[]{:S(2)}, u32[]{:S(2)}) collective-permute-start(f32[128,128]{0,1:T(8,128)S(1)} %add.110), channel_id=1, source_target_pairs={{0,1},{1,0},{2,3},{3,2},{4,5},{5,4},{6,7},{7,6},{8,9},{9,8},{10,11... | collective-permute-start | bytes 196616 | tf_op jit(solution)/shard_map/ppermute | solution.py:18
  93.0 5.6 %collective-permute-start.15 = (f32[128,128]{0,1:T(8,128)S(1)}, f32[128,128]{0,1:T(8,128)S(1)}, u32[]{:S(2)}, u32[]{:S(2)}) collective-permute-start(f32[128,128]{0,1:T(8,128)S(1)} %add.111), channel_id=1, source_target_pairs={{0,3},{1,2},{2,1},{3,0},{4,7},{5,6},{6,5},{7,4},{8,11},{9,10},{10,... | collective-permute-start | bytes 196616 | tf_op jit(solution)/shard_map/ppermute | solution.py:18
  98.8 8.2 %copy-start.2 = (f32[96,32]{0,1:T(8,128)}, f32[96,32]{0,1:T(8,128)S(1)}, u32[]{:S(2)}) copy-start(f32[96,32]{0,1:T(8,128)S(1)} %get-tuple-element.23) | copy-start | bytes 36868

commit v9 on v6

--- a/solution.py
+++ b/solution.py
@@ -146,7 +146,7 @@
         ],
         axis=0,
     )
-    summed = all_sum(packed, (("sub", (2, 4, lax.axis_size("sub") // 8)), ("row", (row_count,))))
+    summed = all_sum(packed, (("row", (row_count,)), ("sub", (2, 4, lax.axis_size("sub") // 8))))
     first, basis_gram, block_gram = lax.optimization_barrier(
         (summed[:count, :vecs], summed[:count, vecs:], summed[count:, :vecs])
     )

time: 108 us -> 107 us (level)
  the two profiles are of different devices: /device:TPU:38 before, /device:TPU:88 now
where the time goes in v9:
time: 107 us
  waiting for transfers between devices  48.7 us (46%)
  starting transfers between devices  27.7 us (26%)
  matrix products  18.6 us (17%)
  local copies, waits for them, and re-layouts  5.23 us (5%)
  Pallas kernels  4.68 us (4%)
    ppermute x12, waiting for transfers between devices, swap(): lax.ppermute(value, axis, [(source, source ^ mask) for source in range(co...  48.4 us
    ppermute x4, starting transfers between devices, from_behind(): lax.ppermute(value, axis, [(source, source + steps) for source in range(l...  15.6 us
    ppermute x12, starting transfers between devices, swap(): lax.ppermute(value, axis, [(source, source ^ mask) for source in range(co...  12.1 us
    dot_general x1, matrix products, per_device(): lax.dot_general(whole, factor_rows[:, :sub_rows], by_rows, precision=three)  5.6 us
    pallas_call x1, Pallas kernels, cholesky_parts(): pl.pallas_call(factor_kernel, out_shape=(shape, shape))  4.68 us
    dot_general x1, matrix products, per_device(): lax.dot_general(margins, factor_rows[:, sub_rows:], by_rows, precision=th...  3.35 us
    dot_general x1, matrix products, per_device(): jnp.dot(inner, factor_rows[:, :sub_rows], precision=three)  2.22 us
  transfers between devices with their start and end apart: 16, of which 13 were waited for; matrix products, arithmetic and copies ran while one was open for 11% of the time, Pallas kernels for 0%

profile of v9, /device:TPU:88, one launch (start us, length us, event | category | flops | bytes accessed | tf_op | source)
XLA Modules:
  0.0 107.0 jit_solution(9876527873508267146)
XLA Ops:
  3.0 2.7 %collective-permute-done = f32[32,512]{1,0:T(8,128)S(1)} collective-permute-done((f32[32,512]{1,0:T(8,128)S(1)}, f32[32,512]{1,0:T(8,128)S(1)}, u32[]{:S(2)}, u32[]{:S(2)}) %collective-permute-start) | collective-permute-done | bytes 65568 | tf_op jit(solution)/shard_map/ppermute | solution.py:18
  6.1 5.9 %collective-permute-done.1 = f32[32,1024]{1,0:T(8,128)S(1)} collective-permute-done((f32[32,1024]{1,0:T(8,128)S(1)}, f32[32,1024]{1,0:T(8,128)S(1)}, u32[]{:S(2)}, u32[]{:S(2)}) %collective-permute-start.1) | collective-permute-done | bytes 131104 | tf_op jit(solution)/shard_map/ppermute | solution.py:18
  13.5 1.9 %collective-permute-start.2 = (f32[32,512]{1,0:T(8,128)S(1)}, f32[32,512]{1,0:T(8,128)S(1)}, u32[]{:S(2)}, u32[]{:S(2)}) collective-permute-start(f32[32,512]{1,0:T(8,128)S(1)} %select_bitcast_fusion.1), channel_id=1, source_target_pairs={{0,4},{4,8},{8,12},{12,16},{16,20},{20,24},{24,28},{28,32},{32,36}... | collective-permute-start | bytes 196616 | tf_op jit(solution)/shard_map/ppermute | solution.py:13
  16.6 6.0 %collective-permute-start.3 = (f32[32,512]{1,0:T(8,128)S(1)}, f32[32,512]{1,0:T(8,128)S(1)}, u32[]{:S(2)}, u32[]{:S(2)}) collective-permute-start(f32[32,512]{1,0:T(8,128)S(1)} %select_bitcast_fusion), channel_id=1, source_target_pairs={{4,0},{8,4},{12,8},{16,12},{20,16},{24,20},{28,24},{32,28},{36,32}... | collective-permute-start | bytes 196616 | tf_op jit(solution)/shard_map/ppermute | solution.py:13
  22.7 5.6 %fusion.2 = f32[32,768]{1,0:T(8,128)S(1)} fusion(f32[32,2048]{1,0:T(8,128)S(1)} %maximum_select_fusion, f32[768,3072]{1,0:T(8,128)} %bitcast.51), kind=kOutput, calls=%fused_computation.4 | convolution fusion | flops 301989888 | bytes 6651904 | tf_op jit(solution)/shard_map/dot_general | solution.py:114
  28.3 3.4 %fusion.8 = f32[32,768]{1,0:T(8,128)S(1)} fusion(f32[768,3072]{1,0:T(8,128)} %bitcast.52, f32[32,512]{1,0:T(8,128)S(1)} %collective-permute-done.3, f32[32,512]{1,0:T(8,128)S(1)} %collective-permute-done.2), kind=kOutput, calls=%fused_computation.12 | convolution fusion | flops 151027712 | bytes 3375104 | tf_op jit(solution)/shard_map/dot_general | solution.py:119
  32.9 1.9 %collective-permute-start.5 = (f32[32,512]{1,0:T(8,128)S(1)}, f32[32,512]{1,0:T(8,128)S(1)}, u32[]{:S(2)}, u32[]{:S(2)}) collective-permute-start(f32[32,512]{1,0:T(8,128)S(1)} %get-tuple-element.20), channel_id=1, source_target_pairs={{0,4},{4,8},{8,12},{12,16},{16,20},{20,24},{24,28},{28,32},{32,36}... | collective-permute-start | bytes 196616 | tf_op jit(solution)/shard_map/ppermute | solution.py:13
  34.9 2.2 %fusion.12 = f32[32,2048]{1,0:T(8,128)S(1)} fusion(f32[32,768]{1,0:T(8,128)S(1)} %get-tuple-element.18, f32[768,3072]{1,0:T(8,128)S(1)} %bitcast.54, f32[32,3072]{1,0:T(8,128)S(1)} %get-tuple-element.17), kind=kOutput, calls=%fused_computation.16 | convolution fusion | flops 302055424 | bytes 6914048 | tf_op jit(solution)/shard_map/dot_general | solution.py:126
  37.1 5.8 %collective-permute-start.4 = (f32[32,512]{1,0:T(8,128)S(1)}, f32[32,512]{1,0:T(8,128)S(1)}, u32[]{:S(2)}, u32[]{:S(2)}) collective-permute-start(f32[32,512]{1,0:T(8,128)S(1)} %get-tuple-element.19), channel_id=1, source_target_pairs={{4,0},{8,4},{12,8},{16,12},{20,16},{24,20},{28,24},{32,28},{36,32}... | collective-permute-start | bytes 196616 | tf_op jit(solution)/shard_map/ppermute | solution.py:13
  42.9 1.7 %fusion.5 = f32[32,2048]{1,0:T(8,128)S(1)} fusion(f32[32,512]{1,0:T(8,128)S(1)} %collective-permute-done.5, s32[512]{0:T(512)S(1)} %bitcast.62), kind=kOutput, calls=%fused_computation.9 | convolution fusion | flops 403701760 | bytes 329728 | tf_op jit(solution)/shard_map/dot_general | solution.py:133
  44.7 1.7 %fusion.11 = f32[32,2048]{1,0:T(8,128)S(1)} fusion(f32[32,2048]{1,0:T(8,128)S(1)} %fusion.5, f32[32,2048]{1,0:T(8,128)S(1)} %fusion.12, f32[32,512]{1,0:T(8,128)S(1)} %collective-permute-done.4, s32[512]{0:T(512)S(1)} %bitcast.59), kind=kOutput, calls=%fused_computation.15 | convolution fusion | flops 403832832 | bytes 854016 | tf_op jit(solution)/shard_map/dot_general | solution.py:132
  46.7 6.0 %collective-permute-done.6 = f32[32,1024]{1,0:T(8,128)S(1)} collective-permute-done((f32[32,1024]{1,0:T(8,128)S(1)}, f32[32,1024]{1,0:T(8,128)S(1)}, u32[]{:S(2)}, u32[]{:S(2)}) %collective-permute-start.6) | collective-permute-done | bytes 131104 | tf_op jit(solution)/shard_map/ppermute | solution.py:18
  53.4 4.0 %collective-permute-done.7 = f32[32,512]{1,0:T(8,128)S(1)} collective-permute-done((f32[32,512]{1,0:T(8,128)S(1)}, f32[32,512]{1,0:T(8,128)S(1)}, u32[]{:S(2)}, u32[]{:S(2)}) %collective-permute-start.7) | collective-permute-done | bytes 65568 | tf_op jit(solution)/shard_map/ppermute | solution.py:18
  58.3 4.0 %collective-permute-done.8 = f32[128,128]{0,1:T(8,128)S(1)} collective-permute-done((f32[128,128]{0,1:T(8,128)S(1)}, f32[128,128]{0,1:T(8,128)S(1)}, u32[]{:S(2)}, u32[]{:S(2)}) %collective-permute-start.8) | collective-permute-done | bytes 65568 | tf_op jit(solution)/shard_map/ppermute | solution.py:18
  62.7 5.2 %collective-permute-done.9 = f32[128,128]{0,1:T(8,128)S(1)} collective-permute-done((f32[128,128]{0,1:T(8,128)S(1)}, f32[128,128]{0,1:T(8,128)S(1)}, u32[]{:S(2)}, u32[]{:S(2)}) %collective-permute-start.9) | collective-permute-done | bytes 65568 | tf_op jit(solution)/shard_map/ppermute | solution.py:18
  68.0 1.2 %collective-permute-done.10 = f32[128,128]{0,1:T(8,128)S(1)} collective-permute-done((f32[128,128]{0,1:T(8,128)S(1)}, f32[128,128]{0,1:T(8,128)S(1)}, u32[]{:S(2)}, u32[]{:S(2)}) %collective-permute-start.10) | collective-permute-done | bytes 65568 | tf_op jit(solution)/shard_map/ppermute | solution.py:18
  69.3 4.3 %collective-permute-done.11 = f32[128,128]{0,1:T(8,128)S(1)} collective-permute-done((f32[128,128]{0,1:T(8,128)S(1)}, f32[128,128]{0,1:T(8,128)S(1)}, u32[]{:S(2)}, u32[]{:S(2)}) %collective-permute-start.11) | collective-permute-done | bytes 65568 | tf_op jit(solution)/shard_map/ppermute | solution.py:18
  73.7 5.5 %collective-permute-done.12 = f32[128,128]{0,1:T(8,128)S(1)} collective-permute-done((f32[128,128]{0,1:T(8,128)S(1)}, f32[128,128]{0,1:T(8,128)S(1)}, u32[]{:S(2)}, u32[]{:S(2)}) %collective-permute-start.12) | collective-permute-done | bytes 65568 | tf_op jit(solution)/shard_map/ppermute | solution.py:18
  79.2 2.2 %collective-permute-start.13 = (f32[128,128]{0,1:T(8,128)S(1)}, f32[128,128]{0,1:T(8,128)S(1)}, u32[]{:S(2)}, u32[]{:S(2)}) collective-permute-start(f32[128,128]{0,1:T(8,128)S(1)} %add.109), channel_id=1, source_target_pairs={{0,32},{4,36},{8,40},{12,44},{16,48},{20,52},{24,56},{28,60},{32,0... | collective-permute-start | bytes 196616 | tf_op jit(solution)/shard_map/ppermute | solution.py:18
  81.4 2.2 %collective-permute-done.13 = f32[128,128]{0,1:T(8,128)S(1)} collective-permute-done((f32[128,128]{0,1:T(8,128)S(1)}, f32[128,128]{0,1:T(8,128)S(1)}, u32[]{:S(2)}, u32[]{:S(2)}) %collective-permute-start.13) | collective-permute-done | bytes 65568 | tf_op jit(solution)/shard_map/ppermute | solution.py:18
  83.7 5.2 %collective-permute-done.14 = f32[128,128]{0,1:T(8,128)S(1)} collective-permute-done((f32[128,128]{0,1:T(8,128)S(1)}, f32[128,128]{0,1:T(8,128)S(1)}, u32[]{:S(2)}, u32[]{:S(2)}) %collective-permute-start.14) | collective-permute-done | bytes 65568 | tf_op jit(solution)/shard_map/ppermute | solution.py:18
  88.9 7.3 %collective-permute-start.15 = (f32[128,128]{0,1:T(8,128)S(1)}, f32[128,128]{0,1:T(8,128)S(1)}, u32[]{:S(2)}, u32[]{:S(2)}) collective-permute-start(f32[128,128]{0,1:T(8,128)S(1)} %add.111), channel_id=1, source_target_pairs={{0,192},{4,196},{8,200},{12,204},{16,208},{20,212},{24,216},{28,22... | collective-permute-start | bytes 196616 | tf_op jit(solution)/shard_map/ppermute | solution.py:18
  96.2 2.3 %collective-permute-done.15 = f32[128,128]{0,1:T(8,128)S(1)} collective-permute-done((f32[128,128]{0,1:T(8,128)S(1)}, f32[128,128]{0,1:T(8,128)S(1)}, u32[]{:S(2)}, u32[]{:S(2)}) %collective-permute-start.15) | collective-permute-done | bytes 65568 | tf_op jit(solution)/shard_map/ppermute | solution.py:18
  100.7 4.7 %shard_map.67 = (f32[32,32]{1,0:T(8,128)}, f32[32,32]{1,0:T(8,128)}) custom-call(f32[32,32]{1,0:T(8,128)} %fusion.38.gram_ref), custom_call_target="tpu_custom_call" | custom-call | tf_op jit(solution)/shard_map/pallas_call | solution.py:92
  (69 shorter events, 13.2 us)
Async XLA Ops:
  1.5 4.3 %collective-permute-start = (f32[32,512]{1,0:T(8,128)S(1)}, f32[32,512]{1,0:T(8,128)S(1)}, u32[]{:S(2)}, u32[]{:S(2)}) collective-permute-start(f32[32,512]{1,0:T(8,128)S(1)} %bitcast.55), channel_id=1, source_target_pairs={{0,1},{1,0},{2,3},{3,2},{4,5},{5,4},{6,7},{7,6},{8,9},{9,8},{10,11... | collective-permute-start | bytes 196616 | tf_op jit(solution)/shard_map/ppermute | solution.py:18
  5.8 6.3 %collective-permute-start.1 = (f32[32,1024]{1,0:T(8,128)S(1)}, f32[32,1024]{1,0:T(8,128)S(1)}, u32[]{:S(2)}, u32[]{:S(2)}) collective-permute-start(f32[32,1024]{1,0:T(8,128)S(1)} %maximum_select_fusion.1), channel_id=1, source_target_pairs={{0,3},{1,2},{2,1},{3,0},{4,7},{5,6},{6,5},{7,4},{8,11},{9,10},{10,... | collective-permute-start | bytes 393224 | tf_op jit(solution)/shard_map/ppermute | solution.py:18
  13.5 14.7 %collective-permute-start.2 = (f32[32,512]{1,0:T(8,128)S(1)}, f32[32,512]{1,0:T(8,128)S(1)}, u32[]{:S(2)}, u32[]{:S(2)}) collective-permute-start(f32[32,512]{1,0:T(8,128)S(1)} %select_bitcast_fusion.1), channel_id=1, source_target_pairs={{0,4},{4,8},{8,12},{12,16},{16,20},{20,24},{24,28},{28,32},{32,36}... | collective-permute-start | bytes 196616 | tf_op jit(solution)/shard_map/ppermute | solution.py:13
  16.6 15.1 %copy-start = (f32[1,768,3072]{2,1,0:T(8,128)S(1)}, f32[1,768,3072]{2,1,0:T(8,128)}, u32[]{:S(2)}) copy-start(f32[1,768,3072]{2,1,0:T(8,128)} %param.7) | copy-start | bytes 28311556
  16.6 11.6 %collective-permute-start.3 = (f32[32,512]{1,0:T(8,128)S(1)}, f32[32,512]{1,0:T(8,128)S(1)}, u32[]{:S(2)}, u32[]{:S(2)}) collective-permute-start(f32[32,512]{1,0:T(8,128)S(1)} %select_bitcast_fusion), channel_id=1, source_target_pairs={{4,0},{8,4},{12,8},{16,12},{20,16},{24,20},{28,24},{32,28},{36,32}... | collective-permute-start | bytes 196616 | tf_op jit(solution)/shard_map/ppermute | solution.py:13
  31.8 21.3 %copy-start.1 = (f32[96,1,512]{2,1,0:T(1,128)S(1)}, f32[96,1,512]{2,1,0:T(1,128)}, u32[]{:S(2)}) copy-start(f32[96,1,512]{2,1,0:T(1,128)} %param.8) | copy-start | bytes 589828
  32.9 9.9 %collective-permute-start.5 = (f32[32,512]{1,0:T(8,128)S(1)}, f32[32,512]{1,0:T(8,128)S(1)}, u32[]{:S(2)}, u32[]{:S(2)}) collective-permute-start(f32[32,512]{1,0:T(8,128)S(1)} %get-tuple-element.20), channel_id=1, source_target_pairs={{0,4},{4,8},{8,12},{12,16},{16,20},{20,24},{24,28},{28,32},{32,36}... | collective-permute-start | bytes 196616 | tf_op jit(solution)/shard_map/ppermute | solution.py:13
  37.1 7.6 %collective-permute-start.4 = (f32[32,512]{1,0:T(8,128)S(1)}, f32[32,512]{1,0:T(8,128)S(1)}, u32[]{:S(2)}, u32[]{:S(2)}) collective-permute-start(f32[32,512]{1,0:T(8,128)S(1)} %get-tuple-element.19), channel_id=1, source_target_pairs={{4,0},{8,4},{12,8},{16,12},{20,16},{24,20},{28,24},{32,28},{36,32}... | collective-permute-start | bytes 196616 | tf_op jit(solution)/shard_map/ppermute | solution.py:13
  46.4 6.3 %collective-permute-start.6 = (f32[32,1024]{1,0:T(8,128)S(1)}, f32[32,1024]{1,0:T(8,128)S(1)}, u32[]{:S(2)}, u32[]{:S(2)}) collective-permute-start(f32[32,1024]{1,0:T(8,128)S(1)} %constant_dynamic-slice_fusion.1), channel_id=1, source_target_pairs={{0,3},{1,2},{2,1},{3,0},{4,7},{5,6},{6,5},{7,4},{8,11},{9,10},{10,... | collective-permute-start | bytes 393224 | tf_op jit(solution)/shard_map/ppermute | solution.py:18
  52.7 4.6 %collective-permute-start.7 = (f32[32,512]{1,0:T(8,128)S(1)}, f32[32,512]{1,0:T(8,128)S(1)}, u32[]{:S(2)}, u32[]{:S(2)}) collective-permute-start(f32[32,512]{1,0:T(8,128)S(1)} %constant_dynamic-slice_fusion), channel_id=1, source_target_pairs={{0,1},{1,0},{2,3},{3,2},{4,5},{5,4},{6,7},{7,6},{8,9},{9,8},{10,11... | collective-permute-start | bytes 196616 | tf_op jit(solution)/shard_map/ppermute | solution.py:18
  58.0 4.3 %collective-permute-start.8 = (f32[128,128]{0,1:T(8,128)S(1)}, f32[128,128]{0,1:T(8,128)S(1)}, u32[]{:S(2)}, u32[]{:S(2)}) collective-permute-start(f32[128,128]{0,1:T(8,128)S(1)} %select_maximum_fusion), channel_id=1, source_target_pairs={{0,1},{1,0},{2,3},{3,2},{4,5},{5,4},{6,7},{7,6},{8,9},{9,8},{10,11... | collective-permute-start | bytes 196616 | tf_op jit(solution)/shard_map/ppermute | solution.py:18
  62.3 5.5 %collective-permute-start.9 = (f32[128,128]{0,1:T(8,128)S(1)}, f32[128,128]{0,1:T(8,128)S(1)}, u32[]{:S(2)}, u32[]{:S(2)}) collective-permute-start(f32[128,128]{0,1:T(8,128)S(1)} %fusion.67), channel_id=1, source_target_pairs={{0,3},{1,2},{2,1},{3,0},{4,7},{5,6},{6,5},{7,4},{8,11},{9,10},{10,... | collective-permute-start | bytes 196616 | tf_op jit(solution)/shard_map/ppermute | solution.py:18
  67.9 1.3 %collective-permute-start.10 = (f32[128,128]{0,1:T(8,128)S(1)}, f32[128,128]{0,1:T(8,128)S(1)}, u32[]{:S(2)}, u32[]{:S(2)}) collective-permute-start(f32[128,128]{0,1:T(8,128)S(1)} %add.106), channel_id=1, source_target_pairs={{0,4},{4,0},{8,12},{12,8},{16,20},{20,16},{24,28},{28,24},{32,36},... | collective-permute-start | bytes 196616 | tf_op jit(solution)/shard_map/ppermute | solution.py:18
  69.2 4.4 %collective-permute-start.11 = (f32[128,128]{0,1:T(8,128)S(1)}, f32[128,128]{0,1:T(8,128)S(1)}, u32[]{:S(2)}, u32[]{:S(2)}) collective-permute-start(f32[128,128]{0,1:T(8,128)S(1)} %add.107), channel_id=1, source_target_pairs={{0,8},{4,12},{8,0},{12,4},{16,24},{20,28},{24,16},{28,20},{32,40},... | collective-permute-start | bytes 196616 | tf_op jit(solution)/shard_map/ppermute | solution.py:18
  73.6 5.6 %collective-permute-start.12 = (f32[128,128]{0,1:T(8,128)S(1)}, f32[128,128]{0,1:T(8,128)S(1)}, u32[]{:S(2)}, u32[]{:S(2)}) collective-permute-start(f32[128,128]{0,1:T(8,128)S(1)} %add.108), channel_id=1, source_target_pairs={{0,24},{4,28},{8,16},{12,20},{16,8},{20,12},{24,0},{28,4},{32,56},... | collective-permute-start | bytes 196616 | tf_op jit(solution)/shard_map/ppermute | solution.py:18
  79.2 4.5 %collective-permute-start.13 = (f32[128,128]{0,1:T(8,128)S(1)}, f32[128,128]{0,1:T(8,128)S(1)}, u32[]{:S(2)}, u32[]{:S(2)}) collective-permute-start(f32[128,128]{0,1:T(8,128)S(1)} %add.109), channel_id=1, source_target_pairs={{0,32},{4,36},{8,40},{12,44},{16,48},{20,52},{24,56},{28,60},{32,0... | collective-permute-start | bytes 196616 | tf_op jit(solution)/shard_map/ppermute | solution.py:18
  83.6 5.3 %collective-permute-start.14 = (f32[128,128]{0,1:T(8,128)S(1)}, f32[128,128]{0,1:T(8,128)S(1)}, u32[]{:S(2)}, u32[]{:S(2)}) collective-permute-start(f32[128,128]{0,1:T(8,128)S(1)} %add.110), channel_id=1, source_target_pairs={{0,64},{4,68},{8,72},{12,76},{16,80},{20,84},{24,88},{28,92},{32,9... | collective-permute-start | bytes 196616 | tf_op jit(solution)/shard_map/ppermute | solution.py:18
  88.9 9.6 %collective-permute-start.15 = (f32[128,128]{0,1:T(8,128)S(1)}, f32[128,128]{0,1:T(8,128)S(1)}, u32[]{:S(2)}, u32[]{:S(2)}) collective-permute-start(f32[128,128]{0,1:T(8,128)S(1)} %add.111), channel_id=1, source_target_pairs={{0,192},{4,196},{8,200},{12,204},{16,208},{20,212},{24,216},{28,22... | collective-permute-start | bytes 196616 | tf_op jit(solution)/shard_map/ppermute | solution.py:18
  98.7 8.2 %copy-start.2 = (f32[96,32]{0,1:T(8,128)}, f32[96,32]{0,1:T(8,128)S(1)}, u32[]{:S(2)}) copy-start(f32[96,32]{0,1:T(8,128)S(1)} %get-tuple-element.23) | copy-start | bytes 36868

commit v10 on v6

--- a/solution.py
+++ b/solution.py
@@ -69,6 +69,7 @@
 def factor_kernel(gram_ref, upper_ref, inverse_ref):
     size = gram_ref.shape[0]
     mat = gram_ref[...]
+    mat = (mat + mat.T) * 0.5
     rows = lax.broadcasted_iota(jnp.int32, (size, size), 0)
     cols = lax.broadcasted_iota(jnp.int32, (size, size), 1)
     inv = (rows == cols).astype(jnp.float32)
@@ -78,10 +79,12 @@
         inv_row = jnp.sum(jnp.where(rows == j, inv, 0.0), axis=0, keepdims=True)
         pivot = jnp.sum(jnp.where(rows[:, :1] == j, col, 0.0), axis=0, keepdims=True)
         scale = 1.0 / jnp.sqrt(pivot)
-        ratio = jnp.where(rows[:, :1] > j, col / pivot, 0.0)
+        lower_col = jnp.where(rows[:, :1] > j, col * scale, 0.0)
+        row = row * scale
+        inv_row = inv_row * scale
         here = rows == j
-        mat = jnp.where(here, row * scale, mat - ratio * row)
-        inv = jnp.where(here, inv_row * scale, inv - ratio * inv_row)
+        mat = jnp.where(here, row, mat - lower_col * row)
+        inv = jnp.where(here, inv_row, inv - lower_col * inv_row)
     upper_ref[...] = jnp.where(rows <= cols, mat, 0.0)
     inverse_ref[...] = jnp.where(rows >= cols, inv, 0.0)
 
@@ -89,8 +92,7 @@
 def cholesky_parts(gram):
     size = gram.shape[0]
     shape = jax.ShapeDtypeStruct((size, size), jnp.float32)
-    return pl.pallas_call(factor_kernel, out_shape=(shape, shape))((gram + gram.T) * 0.5)
-
+    return pl.pallas_call(factor_kernel, out_shape=(shape, shape))(gram)
 
 def per_device(residual, factor, basis, send_rows):
     slab = residual.shape[2]

time: 108 us -> 109 us (level)
    unnamed x8 -> x7, local copies, waits for them, and re-layouts: 1.56 us -> 2.23 us
where the time goes in v10:
time: 109 us; the launch traced here: 108 us
  waiting for transfers between devices  42.7 us (39%)
  starting transfers between devices  34.2 us (31%)
  matrix products  19.3 us (18%)
  local copies, waits for them, and re-layouts  5.83 us (5%)
  Pallas kernels  4.98 us (5%)
    ppermute x12, waiting for transfers between devices, swap(): lax.ppermute(value, axis, [(source, source ^ mask) for source in range(co...  41.3 us
    ppermute x12, starting transfers between devices, swap(): lax.ppermute(value, axis, [(source, source ^ mask) for source in range(co...  22.8 us
    ppermute x4, starting transfers between devices, from_behind(): lax.ppermute(value, axis, [(source, source + steps) for source in range(l...  11.4 us
    dot_general x1, matrix products, per_device(): lax.dot_general(whole, factor_rows[:, :sub_rows], by_rows, precision=three)  5.6 us
    pallas_call x1, Pallas kernels, cholesky_parts(): return pl.pallas_call(factor_kernel, out_shape=(shape, shape))(gram)  4.98 us
    dot_general x1, matrix products, per_device(): lax.dot_general(margins, factor_rows[:, sub_rows:], by_rows, precision=th...  3.35 us
    unnamed x7, local copies, waits for them, and re-layouts  2.23 us
    dot_general x1, matrix products, per_device(): jnp.dot(inner, factor_rows[:, :sub_rows], precision=three)  2.22 us
  transfers between devices with their start and end apart: 16, of which 13 were waited for; matrix products, arithmetic and copies ran while one was open for 11% of the time, Pallas kernels for 0%

profile of v10, /device:TPU:38, one launch (start us, length us, event | category | flops | bytes accessed | tf_op | source)
XLA Modules:
  0.0 108.5 jit_solution(12595551419263530604)
XLA Ops:
  3.8 1.9 %collective-permute-done = f32[32,512]{1,0:T(8,128)S(1)} collective-permute-done((f32[32,512]{1,0:T(8,128)S(1)}, f32[32,512]{1,0:T(8,128)S(1)}, u32[]{:S(2)}, u32[]{:S(2)}) %collective-permute-start) | collective-permute-done | bytes 65568 | tf_op jit(solution)/shard_map/ppermute | solution.py:18
  5.8 3.1 %collective-permute-start.1 = (f32[32,1024]{1,0:T(8,128)S(1)}, f32[32,1024]{1,0:T(8,128)S(1)}, u32[]{:S(2)}, u32[]{:S(2)}) collective-permute-start(f32[32,1024]{1,0:T(8,128)S(1)} %maximum_select_fusion.1), channel_id=1, source_target_pairs={{0,3},{1,2},{2,1},{3,0},{4,7},{5,6},{6,5},{7,4},{8,11},{9,10},{10,... | collective-permute-start | bytes 393224 | tf_op jit(solution)/shard_map/ppermute | solution.py:18
  8.9 3.1 %collective-permute-done.1 = f32[32,1024]{1,0:T(8,128)S(1)} collective-permute-done((f32[32,1024]{1,0:T(8,128)S(1)}, f32[32,1024]{1,0:T(8,128)S(1)}, u32[]{:S(2)}, u32[]{:S(2)}) %collective-permute-start.1) | collective-permute-done | bytes 131104 | tf_op jit(solution)/shard_map/ppermute | solution.py:18
  13.5 1.9 %collective-permute-start.2 = (f32[32,512]{1,0:T(8,128)S(1)}, f32[32,512]{1,0:T(8,128)S(1)}, u32[]{:S(2)}, u32[]{:S(2)}) collective-permute-start(f32[32,512]{1,0:T(8,128)S(1)} %select_bitcast_fusion.1), channel_id=1, source_target_pairs={{0,4},{4,8},{8,12},{12,16},{16,20},{20,24},{24,28},{28,32},{32,36}... | collective-permute-start | bytes 196616 | tf_op jit(solution)/shard_map/ppermute | solution.py:13
  16.6 3.9 %collective-permute-start.3 = (f32[32,512]{1,0:T(8,128)S(1)}, f32[32,512]{1,0:T(8,128)S(1)}, u32[]{:S(2)}, u32[]{:S(2)}) collective-permute-start(f32[32,512]{1,0:T(8,128)S(1)} %select_bitcast_fusion), channel_id=1, source_target_pairs={{4,0},{8,4},{12,8},{16,12},{20,16},{24,20},{28,24},{32,28},{36,32}... | collective-permute-start | bytes 196616 | tf_op jit(solution)/shard_map/ppermute | solution.py:13
  20.6 5.6 %fusion.2 = f32[32,768]{1,0:T(8,128)S(1)} fusion(f32[32,2048]{1,0:T(8,128)S(1)} %maximum_select_fusion, f32[768,3072]{1,0:T(8,128)} %bitcast.47), kind=kOutput, calls=%fused_computation.4 | convolution fusion | flops 301989888 | bytes 6651904 | tf_op jit(solution)/shard_map/dot_general | solution.py:116
  26.2 3.4 %fusion.8 = f32[32,768]{1,0:T(8,128)S(1)} fusion(f32[768,3072]{1,0:T(8,128)} %bitcast.48, f32[32,512]{1,0:T(8,128)S(1)} %collective-permute-done.3, f32[32,512]{1,0:T(8,128)S(1)} %collective-permute-done.2), kind=kOutput, calls=%fused_computation.12 | convolution fusion | flops 151027712 | bytes 3375104 | tf_op jit(solution)/shard_map/dot_general | solution.py:121
  30.8 2.6 %collective-permute-start.5 = (f32[32,512]{1,0:T(8,128)S(1)}, f32[32,512]{1,0:T(8,128)S(1)}, u32[]{:S(2)}, u32[]{:S(2)}) collective-permute-start(f32[32,512]{1,0:T(8,128)S(1)} %get-tuple-element.20), channel_id=1, source_target_pairs={{0,4},{4,8},{8,12},{12,16},{16,20},{20,24},{24,28},{28,32},{32,36}... | collective-permute-start | bytes 196616 | tf_op jit(solution)/shard_map/ppermute | solution.py:13
  33.4 2.2 %fusion.12 = f32[32,2048]{1,0:T(8,128)S(1)} fusion(f32[32,768]{1,0:T(8,128)S(1)} %get-tuple-element.18, f32[768,3072]{1,0:T(8,128)S(1)} %bitcast.50, f32[32,3072]{1,0:T(8,128)S(1)} %get-tuple-element.17), kind=kOutput, calls=%fused_computation.16 | convolution fusion | flops 302055424 | bytes 6914048 | tf_op jit(solution)/shard_map/dot_general | solution.py:128
  35.7 3.0 %collective-permute-start.4 = (f32[32,512]{1,0:T(8,128)S(1)}, f32[32,512]{1,0:T(8,128)S(1)}, u32[]{:S(2)}, u32[]{:S(2)}) collective-permute-start(f32[32,512]{1,0:T(8,128)S(1)} %get-tuple-element.19), channel_id=1, source_target_pairs={{4,0},{8,4},{12,8},{16,12},{20,16},{24,20},{28,24},{32,28},{36,32}... | collective-permute-start | bytes 196616 | tf_op jit(solution)/shard_map/ppermute | solution.py:13
  43.4 3.1 %collective-permute-start.6 = (f32[32,1024]{1,0:T(8,128)S(1)}, f32[32,1024]{1,0:T(8,128)S(1)}, u32[]{:S(2)}, u32[]{:S(2)}) collective-permute-start(f32[32,1024]{1,0:T(8,128)S(1)} %constant_dynamic-slice_fusion.1), channel_id=1, source_target_pairs={{0,3},{1,2},{2,1},{3,0},{4,7},{5,6},{6,5},{7,4},{8,11},{9,10},{10,... | collective-permute-start | bytes 393224 | tf_op jit(solution)/shard_map/ppermute | solution.py:18
  46.5 3.2 %collective-permute-done.6 = f32[32,1024]{1,0:T(8,128)S(1)} collective-permute-done((f32[32,1024]{1,0:T(8,128)S(1)}, f32[32,1024]{1,0:T(8,128)S(1)}, u32[]{:S(2)}, u32[]{:S(2)}) %collective-permute-start.6) | collective-permute-done | bytes 131104 | tf_op jit(solution)/shard_map/ppermute | solution.py:18
  50.3 3.9 %collective-permute-done.7 = f32[32,512]{1,0:T(8,128)S(1)} collective-permute-done((f32[32,512]{1,0:T(8,128)S(1)}, f32[32,512]{1,0:T(8,128)S(1)}, u32[]{:S(2)}, u32[]{:S(2)}) %collective-permute-start.7) | collective-permute-done | bytes 65568 | tf_op jit(solution)/shard_map/ppermute | solution.py:18
  54.8 2.9 %collective-permute-start.8 = (f32[128,128]{1,0:T(8,128)S(1)}, f32[128,128]{1,0:T(8,128)S(1)}, u32[]{:S(2)}, u32[]{:S(2)}) collective-permute-start(f32[128,128]{1,0:T(8,128)S(1)} %select_maximum_fusion), channel_id=1, source_target_pairs={{0,4},{4,0},{8,12},{12,8},{16,20},{20,16},{24,28},{28,24},{32,36},... | collective-permute-start | bytes 196616 | tf_op jit(solution)/shard_map/ppermute | solution.py:18
  58.8 4.3 %collective-permute-done.9 = f32[128,128]{1,0:T(8,128)S(1)} collective-permute-done((f32[128,128]{1,0:T(8,128)S(1)}, f32[128,128]{1,0:T(8,128)S(1)}, u32[]{:S(2)}, u32[]{:S(2)}) %collective-permute-start.9) | collective-permute-done | bytes 65568 | tf_op jit(solution)/shard_map/ppermute | solution.py:18
  64.2 4.5 %collective-permute-done.10 = f32[128,128]{1,0:T(8,128)S(1)} collective-permute-done((f32[128,128]{1,0:T(8,128)S(1)}, f32[128,128]{1,0:T(8,128)S(1)}, u32[]{:S(2)}, u32[]{:S(2)}) %collective-permute-start.10) | collective-permute-done | bytes 65568 | tf_op jit(solution)/shard_map/ppermute | solution.py:18
  68.9 4.2 %collective-permute-done.11 = f32[128,128]{1,0:T(8,128)S(1)} collective-permute-done((f32[128,128]{1,0:T(8,128)S(1)}, f32[128,128]{1,0:T(8,128)S(1)}, u32[]{:S(2)}, u32[]{:S(2)}) %collective-permute-start.11) | collective-permute-done | bytes 65568 | tf_op jit(solution)/shard_map/ppermute | solution.py:18
  73.1 7.0 %collective-permute-start.12 = (f32[128,128]{1,0:T(8,128)S(1)}, f32[128,128]{1,0:T(8,128)S(1)}, u32[]{:S(2)}, u32[]{:S(2)}) collective-permute-start(f32[128,128]{1,0:T(8,128)S(1)} %add.105), channel_id=1, source_target_pairs={{0,64},{4,68},{8,72},{12,76},{16,80},{20,84},{24,88},{28,92},{32,9... | collective-permute-start | bytes 196616 | tf_op jit(solution)/shard_map/ppermute | solution.py:18
  80.1 2.2 %collective-permute-done.12 = f32[128,128]{1,0:T(8,128)S(1)} collective-permute-done((f32[128,128]{1,0:T(8,128)S(1)}, f32[128,128]{1,0:T(8,128)S(1)}, u32[]{:S(2)}, u32[]{:S(2)}) %collective-permute-start.12) | collective-permute-done | bytes 65568 | tf_op jit(solution)/shard_map/ppermute | solution.py:18
  82.5 6.6 %collective-permute-done.13 = f32[128,128]{1,0:T(8,128)S(1)} collective-permute-done((f32[128,128]{1,0:T(8,128)S(1)}, f32[128,128]{1,0:T(8,128)S(1)}, u32[]{:S(2)}, u32[]{:S(2)}) %collective-permute-start.13) | collective-permute-done | bytes 65568 | tf_op jit(solution)/shard_map/ppermute | solution.py:18
  89.4 4.0 %collective-permute-done.14 = f32[128,128]{1,0:T(8,128)S(1)} collective-permute-done((f32[128,128]{1,0:T(8,128)S(1)}, f32[128,128]{1,0:T(8,128)S(1)}, u32[]{:S(2)}, u32[]{:S(2)}) %collective-permute-start.14) | collective-permute-done | bytes 65568 | tf_op jit(solution)/shard_map/ppermute | solution.py:18
  93.4 3.0 %collective-permute-start.15 = (f32[128,128]{1,0:T(8,128)S(1)}, f32[128,128]{1,0:T(8,128)S(1)}, u32[]{:S(2)}, u32[]{:S(2)}) collective-permute-start(f32[128,128]{1,0:T(8,128)S(1)} %add.108), channel_id=1, source_target_pairs={{0,3},{1,2},{2,1},{3,0},{4,7},{5,6},{6,5},{7,4},{8,11},{9,10},{10,... | collective-permute-start | bytes 196616 | tf_op jit(solution)/shard_map/ppermute | solution.py:18
  96.4 2.5 %collective-permute-done.15 = f32[128,128]{1,0:T(8,128)S(1)} collective-permute-done((f32[128,128]{1,0:T(8,128)S(1)}, f32[128,128]{1,0:T(8,128)S(1)}, u32[]{:S(2)}, u32[]{:S(2)}) %collective-permute-start.15) | collective-permute-done | bytes 65568 | tf_op jit(solution)/shard_map/ppermute | solution.py:18
  101.9 5.0 %shard_map.67 = (f32[32,32]{1,0:T(8,128)}, f32[32,32]{1,0:T(8,128)}) custom-call(f32[32,32]{1,0:T(8,128)} %fusion.21.gram_ref), custom_call_target="tpu_custom_call" | custom-call | tf_op jit(solution)/shard_map/pallas_call | solution.py:95
  (66 shorter events, 20.3 us)
Async XLA Ops:
  1.5 4.3 %collective-permute-start = (f32[32,512]{1,0:T(8,128)S(1)}, f32[32,512]{1,0:T(8,128)S(1)}, u32[]{:S(2)}, u32[]{:S(2)}) collective-permute-start(f32[32,512]{1,0:T(8,128)S(1)} %bitcast.51), channel_id=1, source_target_pairs={{0,1},{1,0},{2,3},{3,2},{4,5},{5,4},{6,7},{7,6},{8,9},{9,8},{10,11... | collective-permute-start | bytes 196616 | tf_op jit(solution)/shard_map/ppermute | solution.py:18
  5.8 6.3 %collective-permute-start.1 = (f32[32,1024]{1,0:T(8,128)S(1)}, f32[32,1024]{1,0:T(8,128)S(1)}, u32[]{:S(2)}, u32[]{:S(2)}) collective-permute-start(f32[32,1024]{1,0:T(8,128)S(1)} %maximum_select_fusion.1), channel_id=1, source_target_pairs={{0,3},{1,2},{2,1},{3,0},{4,7},{5,6},{6,5},{7,4},{8,11},{9,10},{10,... | collective-permute-start | bytes 393224 | tf_op jit(solution)/shard_map/ppermute | solution.py:18
  13.5 12.6 %collective-permute-start.2 = (f32[32,512]{1,0:T(8,128)S(1)}, f32[32,512]{1,0:T(8,128)S(1)}, u32[]{:S(2)}, u32[]{:S(2)}) collective-permute-start(f32[32,512]{1,0:T(8,128)S(1)} %select_bitcast_fusion.1), channel_id=1, source_target_pairs={{0,4},{4,8},{8,12},{12,16},{16,20},{20,24},{24,28},{28,32},{32,36}... | collective-permute-start | bytes 196616 | tf_op jit(solution)/shard_map/ppermute | solution.py:13
  16.6 13.0 %copy-start = (f32[1,768,3072]{2,1,0:T(8,128)S(1)}, f32[1,768,3072]{2,1,0:T(8,128)}, u32[]{:S(2)}) copy-start(f32[1,768,3072]{2,1,0:T(8,128)} %param.7) | copy-start | bytes 28311556
  16.6 9.5 %collective-permute-start.3 = (f32[32,512]{1,0:T(8,128)S(1)}, f32[32,512]{1,0:T(8,128)S(1)}, u32[]{:S(2)}, u32[]{:S(2)}) collective-permute-start(f32[32,512]{1,0:T(8,128)S(1)} %select_bitcast_fusion), channel_id=1, source_target_pairs={{4,0},{8,4},{12,8},{16,12},{20,16},{24,20},{28,24},{32,28},{36,32}... | collective-permute-start | bytes 196616 | tf_op jit(solution)/shard_map/ppermute | solution.py:13
  29.7 20.3 %copy-start.1 = (f32[96,1,512]{2,1,0:T(1,128)S(1)}, f32[96,1,512]{2,1,0:T(1,128)}, u32[]{:S(2)}) copy-start(f32[96,1,512]{2,1,0:T(1,128)} %param.8) | copy-start | bytes 589828
  30.8 7.8 %collective-permute-start.5 = (f32[32,512]{1,0:T(8,128)S(1)}, f32[32,512]{1,0:T(8,128)S(1)}, u32[]{:S(2)}, u32[]{:S(2)}) collective-permute-start(f32[32,512]{1,0:T(8,128)S(1)} %get-tuple-element.20), channel_id=1, source_target_pairs={{0,4},{4,8},{8,12},{12,16},{16,20},{20,24},{24,28},{28,32},{32,36}... | collective-permute-start | bytes 196616 | tf_op jit(solution)/shard_map/ppermute | solution.py:13
  35.7 6.0 %collective-permute-start.4 = (f32[32,512]{1,0:T(8,128)S(1)}, f32[32,512]{1,0:T(8,128)S(1)}, u32[]{:S(2)}, u32[]{:S(2)}) collective-permute-start(f32[32,512]{1,0:T(8,128)S(1)} %get-tuple-element.19), channel_id=1, source_target_pairs={{4,0},{8,4},{12,8},{16,12},{20,16},{24,20},{28,24},{32,28},{36,32}... | collective-permute-start | bytes 196616 | tf_op jit(solution)/shard_map/ppermute | solution.py:13
  43.4 6.3 %collective-permute-start.6 = (f32[32,1024]{1,0:T(8,128)S(1)}, f32[32,1024]{1,0:T(8,128)S(1)}, u32[]{:S(2)}, u32[]{:S(2)}) collective-permute-start(f32[32,1024]{1,0:T(8,128)S(1)} %constant_dynamic-slice_fusion.1), channel_id=1, source_target_pairs={{0,3},{1,2},{2,1},{3,0},{4,7},{5,6},{6,5},{7,4},{8,11},{9,10},{10,... | collective-permute-start | bytes 393224 | tf_op jit(solution)/shard_map/ppermute | solution.py:18
  49.7 4.5 %collective-permute-start.7 = (f32[32,512]{1,0:T(8,128)S(1)}, f32[32,512]{1,0:T(8,128)S(1)}, u32[]{:S(2)}, u32[]{:S(2)}) collective-permute-start(f32[32,512]{1,0:T(8,128)S(1)} %constant_dynamic-slice_fusion), channel_id=1, source_target_pairs={{0,1},{1,0},{2,3},{3,2},{4,5},{5,4},{6,7},{7,6},{8,9},{9,8},{10,11... | collective-permute-start | bytes 196616 | tf_op jit(solution)/shard_map/ppermute | solution.py:18
  54.8 3.8 %collective-permute-start.8 = (f32[128,128]{1,0:T(8,128)S(1)}, f32[128,128]{1,0:T(8,128)S(1)}, u32[]{:S(2)}, u32[]{:S(2)}) collective-permute-start(f32[128,128]{1,0:T(8,128)S(1)} %select_maximum_fusion), channel_id=1, source_target_pairs={{0,4},{4,0},{8,12},{12,8},{16,20},{20,16},{24,28},{28,24},{32,36},... | collective-permute-start | bytes 196616 | tf_op jit(solution)/shard_map/ppermute | solution.py:18
  58.7 4.4 %collective-permute-start.9 = (f32[128,128]{1,0:T(8,128)S(1)}, f32[128,128]{1,0:T(8,128)S(1)}, u32[]{:S(2)}, u32[]{:S(2)}) collective-permute-start(f32[128,128]{1,0:T(8,128)S(1)} %fusion.66), channel_id=1, source_target_pairs={{0,8},{4,12},{8,0},{12,4},{16,24},{20,28},{24,16},{28,20},{32,40},... | collective-permute-start | bytes 196616 | tf_op jit(solution)/shard_map/ppermute | solution.py:18
  63.2 5.6 %collective-permute-start.10 = (f32[128,128]{1,0:T(8,128)S(1)}, f32[128,128]{1,0:T(8,128)S(1)}, u32[]{:S(2)}, u32[]{:S(2)}) collective-permute-start(f32[128,128]{1,0:T(8,128)S(1)} %add.103), channel_id=1, source_target_pairs={{0,24},{4,28},{8,16},{12,20},{16,8},{20,12},{24,0},{28,4},{32,56},... | collective-permute-start | bytes 196616 | tf_op jit(solution)/shard_map/ppermute | solution.py:18
  68.7 4.4 %collective-permute-start.11 = (f32[128,128]{1,0:T(8,128)S(1)}, f32[128,128]{1,0:T(8,128)S(1)}, u32[]{:S(2)}, u32[]{:S(2)}) collective-permute-start(f32[128,128]{1,0:T(8,128)S(1)} %add.104), channel_id=1, source_target_pairs={{0,32},{4,36},{8,40},{12,44},{16,48},{20,52},{24,56},{28,60},{32,0... | collective-permute-start | bytes 196616 | tf_op jit(solution)/shard_map/ppermute | solution.py:18
  73.1 9.2 %collective-permute-start.12 = (f32[128,128]{1,0:T(8,128)S(1)}, f32[128,128]{1,0:T(8,128)S(1)}, u32[]{:S(2)}, u32[]{:S(2)}) collective-permute-start(f32[128,128]{1,0:T(8,128)S(1)} %add.105), channel_id=1, source_target_pairs={{0,64},{4,68},{8,72},{12,76},{16,80},{20,84},{24,88},{28,92},{32,9... | collective-permute-start | bytes 196616 | tf_op jit(solution)/shard_map/ppermute | solution.py:18
  82.4 6.7 %collective-permute-start.13 = (f32[128,128]{1,0:T(8,128)S(1)}, f32[128,128]{1,0:T(8,128)S(1)}, u32[]{:S(2)}, u32[]{:S(2)}) collective-permute-start(f32[128,128]{1,0:T(8,128)S(1)} %add.106), channel_id=1, source_target_pairs={{0,192},{4,196},{8,200},{12,204},{16,208},{20,212},{24,216},{28,22... | collective-permute-start | bytes 196616 | tf_op jit(solution)/shard_map/ppermute | solution.py:18
  89.0 4.4 %collective-permute-start.14 = (f32[128,128]{1,0:T(8,128)S(1)}, f32[128,128]{1,0:T(8,128)S(1)}, u32[]{:S(2)}, u32[]{:S(2)}) collective-permute-start(f32[128,128]{1,0:T(8,128)S(1)} %add.107), channel_id=1, source_target_pairs={{0,1},{1,0},{2,3},{3,2},{4,5},{5,4},{6,7},{7,6},{8,9},{9,8},{10,11... | collective-permute-start | bytes 196616 | tf_op jit(solution)/shard_map/ppermute | solution.py:18
  93.4 5.6 %collective-permute-start.15 = (f32[128,128]{1,0:T(8,128)S(1)}, f32[128,128]{1,0:T(8,128)S(1)}, u32[]{:S(2)}, u32[]{:S(2)}) collective-permute-start(f32[128,128]{1,0:T(8,128)S(1)} %add.108), channel_id=1, source_target_pairs={{0,3},{1,2},{2,1},{3,0},{4,7},{5,6},{6,5},{7,4},{8,11},{9,10},{10,... | collective-permute-start | bytes 196616 | tf_op jit(solution)/shard_map/ppermute | solution.py:18

commit v11 on v6

--- a/solution.py
+++ b/solution.py
@@ -111,13 +111,9 @@
     three = lax.Precision.HIGH
     by_rows = (((1,), (1,)), ((), ()))
     start = row_pos * share
-    inner_own = lax.optimization_barrier(lax.dot_general(whole, factor_rows[:, :sub_rows], by_rows, precision=three))
-    margins = jnp.concatenate([from_lower, from_upper], axis=1)
-    extended = jnp.concatenate([whole, margins], axis=1)
-    inner = (
-        inner_own
-        + lax.dot_general(margins, factor_rows[:, sub_rows:], by_rows, precision=three)
-        + lax.dynamic_slice_in_dim(extended, start, share, 1)
+    extended = jnp.concatenate([whole, from_lower, from_upper], axis=1)
+    inner = lax.dynamic_slice_in_dim(extended, start, share, 1) + lax.dot_general(
+        extended, factor_rows, by_rows, precision=three
     )
     placed = lax.dynamic_update_slice_in_dim(jnp.zeros(extended.shape, jnp.float32), inner, start, 1)
     margin_value = jnp.dot(inner, factor_rows[:, sub_rows:], precision=three) + placed[:, sub_rows:]

time: 108 us -> 109 us (level)
    ppermute x4, starting transfers between devices: 11.4 us -> 12.7 us  [from_behind(): lax.ppermute(value, axis, [(source, source + steps) for source in range(l...]
    dot_general x2 -> x1, matrix products: 8.96 us -> 8.61 us  [per_device(): lax.dot_general(extended, factor_rows, by_rows, precision=three)]
  transfers between devices with their start and end apart: 16 -> 16, of which waited for: 13 -> 14; matrix products, arithmetic and copies ran while one was open for 11% -> 6% of each run, Pallas kernels for 0% -> 0%
where the time goes in v11:
time: 109 us
  waiting for transfers between devices  43.4 us (40%)
  starting transfers between devices  35 us (32%)
  matrix products  18.3 us (17%)
  local copies, waits for them, and re-layouts  5.23 us (5%)
  Pallas kernels  4.68 us (4%)
    ppermute x12, waiting for transfers between devices, swap(): lax.ppermute(value, axis, [(source, source ^ mask) for source in range(co...  41.3 us
    ppermute x12, starting transfers between devices, swap(): lax.ppermute(value, axis, [(source, source ^ mask) for source in range(co...  22.2 us
    ppermute x4, starting transfers between devices, from_behind(): lax.ppermute(value, axis, [(source, source + steps) for source in range(l...  12.7 us
    dot_general x1, matrix products, per_device(): lax.dot_general(extended, factor_rows, by_rows, precision=three)  8.61 us
    pallas_call x1, Pallas kernels, cholesky_parts(): pl.pallas_call(factor_kernel, out_shape=(shape, shape))  4.68 us
    dot_general x1, matrix products, per_device(): jnp.dot(inner, factor_rows[:, :sub_rows], precision=three)  2.22 us
  transfers between devices with their start and end apart: 16, of which 14 were waited for; matrix products, arithmetic and copies ran while one was open for 6% of the time, Pallas kernels for 0%

profile of v11, /device:TPU:38, one launch (start us, length us, event | category | flops | bytes accessed | tf_op | source)
XLA Modules:
  0.0 108.6 jit_solution(11125825026878654980)
XLA Ops:
  3.8 1.9 %collective-permute-done = f32[32,512]{1,0:T(8,128)S(1)} collective-permute-done((f32[32,512]{1,0:T(8,128)S(1)}, f32[32,512]{1,0:T(8,128)S(1)}, u32[]{:S(2)}, u32[]{:S(2)}) %collective-permute-start) | collective-permute-done | bytes 65568 | tf_op jit(solution)/shard_map/ppermute | solution.py:18
  5.8 3.1 %collective-permute-start.1 = (f32[32,1024]{1,0:T(8,128)S(1)}, f32[32,1024]{1,0:T(8,128)S(1)}, u32[]{:S(2)}, u32[]{:S(2)}) collective-permute-start(f32[32,1024]{1,0:T(8,128)S(1)} %maximum_select_fusion.1), channel_id=1, source_target_pairs={{0,3},{1,2},{2,1},{3,0},{4,7},{5,6},{6,5},{7,4},{8,11},{9,10},{10,... | collective-permute-start | bytes 393224 | tf_op jit(solution)/shard_map/ppermute | solution.py:18
  8.9 3.1 %collective-permute-done.1 = f32[32,1024]{1,0:T(8,128)S(1)} collective-permute-done((f32[32,1024]{1,0:T(8,128)S(1)}, f32[32,1024]{1,0:T(8,128)S(1)}, u32[]{:S(2)}, u32[]{:S(2)}) %collective-permute-start.1) | collective-permute-done | bytes 131104 | tf_op jit(solution)/shard_map/ppermute | solution.py:18
  13.5 1.9 %collective-permute-start.2 = (f32[32,512]{1,0:T(8,128)S(1)}, f32[32,512]{1,0:T(8,128)S(1)}, u32[]{:S(2)}, u32[]{:S(2)}) collective-permute-start(f32[32,512]{1,0:T(8,128)S(1)} %select_bitcast_fusion.1), channel_id=1, source_target_pairs={{0,4},{4,8},{8,12},{12,16},{16,20},{20,24},{24,28},{28,32},{32,36}... | collective-permute-start | bytes 196616 | tf_op jit(solution)/shard_map/ppermute | solution.py:13
  16.6 3.6 %collective-permute-start.3 = (f32[32,512]{1,0:T(8,128)S(1)}, f32[32,512]{1,0:T(8,128)S(1)}, u32[]{:S(2)}, u32[]{:S(2)}) collective-permute-start(f32[32,512]{1,0:T(8,128)S(1)} %select_bitcast_fusion), channel_id=1, source_target_pairs={{4,0},{8,4},{12,8},{16,12},{20,16},{24,20},{28,24},{32,28},{36,32}... | collective-permute-start | bytes 196616 | tf_op jit(solution)/shard_map/ppermute | solution.py:13
  20.4 1.8 %collective-permute-done.3 = f32[32,512]{1,0:T(8,128)S(1)} collective-permute-done((f32[32,512]{1,0:T(8,128)S(1)}, f32[32,512]{1,0:T(8,128)S(1)}, u32[]{:S(2)}, u32[]{:S(2)}) %collective-permute-start.3) | collective-permute-done | bytes 65568 | tf_op jit(solution)/shard_map/ppermute | solution.py:13
  22.2 8.6 %constant_dynamic-update-slice_fusion = (f32[32,3072]{1,0:T(8,128)S(1)}, f32[32,768]{1,0:T(8,128)S(1)}) fusion(f32[32,3072]{1,0:T(8,128)S(1)} %broadcast_in_dim.18, s32[]{:T(128)S(6)} %select_n.59, f32[32,3072]{1,0:T(8,128)S(1)} %pad_maximum_fusion, f32[1,768,3072]{2,1,0:T(8,128)} %param.7), kind=kOutput, calls=%fused_computation.55 | convolution fusion | flops 453009408 | bytes 10125316 | tf_op jit(solution)/shard_map/dot_general | solution.py:115
  32.0 5.3 %collective-permute-start.5 = (f32[32,512]{1,0:T(8,128)S(1)}, f32[32,512]{1,0:T(8,128)S(1)}, u32[]{:S(2)}, u32[]{:S(2)}) collective-permute-start(f32[32,512]{1,0:T(8,128)S(1)} %get-tuple-element.18), channel_id=1, source_target_pairs={{0,4},{4,8},{8,12},{12,16},{16,20},{20,24},{24,28},{28,32},{32,36}... | collective-permute-start | bytes 196616 | tf_op jit(solution)/shard_map/ppermute | solution.py:13
  37.3 2.2 %fusion.8 = f32[32,2048]{1,0:T(8,128)S(1)} fusion(f32[32,768]{1,0:T(8,128)S(1)} %get-tuple-element.22, f32[768,3072]{1,0:T(8,128)S(1)} %bitcast.58, f32[32,3072]{1,0:T(8,128)S(1)} %get-tuple-element.21), kind=kOutput, calls=%fused_computation.12 | convolution fusion | flops 302055424 | bytes 6914048 | tf_op jit(solution)/shard_map/dot_general | solution.py:122
  39.5 1.9 %collective-permute-start.4 = (f32[32,512]{1,0:T(8,128)S(1)}, f32[32,512]{1,0:T(8,128)S(1)}, u32[]{:S(2)}, u32[]{:S(2)}) collective-permute-start(f32[32,512]{1,0:T(8,128)S(1)} %get-tuple-element.17), channel_id=1, source_target_pairs={{4,0},{8,4},{12,8},{16,12},{20,16},{24,20},{28,24},{32,28},{36,32}... | collective-permute-start | bytes 196616 | tf_op jit(solution)/shard_map/ppermute | solution.py:13
  45.0 3.1 %collective-permute-start.6 = (f32[32,1024]{1,0:T(8,128)S(1)}, f32[32,1024]{1,0:T(8,128)S(1)}, u32[]{:S(2)}, u32[]{:S(2)}) collective-permute-start(f32[32,1024]{1,0:T(8,128)S(1)} %constant_dynamic-slice_fusion.1), channel_id=1, source_target_pairs={{0,3},{1,2},{2,1},{3,0},{4,7},{5,6},{6,5},{7,4},{8,11},{9,10},{10,... | collective-permute-start | bytes 393224 | tf_op jit(solution)/shard_map/ppermute | solution.py:18
  48.1 3.2 %collective-permute-done.6 = f32[32,1024]{1,0:T(8,128)S(1)} collective-permute-done((f32[32,1024]{1,0:T(8,128)S(1)}, f32[32,1024]{1,0:T(8,128)S(1)}, u32[]{:S(2)}, u32[]{:S(2)}) %collective-permute-start.6) | collective-permute-done | bytes 131104 | tf_op jit(solution)/shard_map/ppermute | solution.py:18
  52.0 3.9 %collective-permute-done.7 = f32[32,512]{1,0:T(8,128)S(1)} collective-permute-done((f32[32,512]{1,0:T(8,128)S(1)}, f32[32,512]{1,0:T(8,128)S(1)}, u32[]{:S(2)}, u32[]{:S(2)}) %collective-permute-start.7) | collective-permute-done | bytes 65568 | tf_op jit(solution)/shard_map/ppermute | solution.py:18
  56.5 2.4 %collective-permute-start.8 = (f32[128,128]{0,1:T(8,128)S(1)}, f32[128,128]{0,1:T(8,128)S(1)}, u32[]{:S(2)}, u32[]{:S(2)}) collective-permute-start(f32[128,128]{0,1:T(8,128)S(1)} %select_maximum_fusion), channel_id=1, source_target_pairs={{0,4},{4,0},{8,12},{12,8},{16,20},{20,16},{24,28},{28,24},{32,36},... | collective-permute-start | bytes 196616 | tf_op jit(solution)/shard_map/ppermute | solution.py:18
  59.9 4.3 %collective-permute-done.9 = f32[128,128]{0,1:T(8,128)S(1)} collective-permute-done((f32[128,128]{0,1:T(8,128)S(1)}, f32[128,128]{0,1:T(8,128)S(1)}, u32[]{:S(2)}, u32[]{:S(2)}) %collective-permute-start.9) | collective-permute-done | bytes 65568 | tf_op jit(solution)/shard_map/ppermute | solution.py:18
  65.3 4.5 %collective-permute-done.10 = f32[128,128]{0,1:T(8,128)S(1)} collective-permute-done((f32[128,128]{0,1:T(8,128)S(1)}, f32[128,128]{0,1:T(8,128)S(1)}, u32[]{:S(2)}, u32[]{:S(2)}) %collective-permute-start.10) | collective-permute-done | bytes 65568 | tf_op jit(solution)/shard_map/ppermute | solution.py:18
  70.0 4.2 %collective-permute-done.11 = f32[128,128]{0,1:T(8,128)S(1)} collective-permute-done((f32[128,128]{0,1:T(8,128)S(1)}, f32[128,128]{0,1:T(8,128)S(1)}, u32[]{:S(2)}, u32[]{:S(2)}) %collective-permute-start.11) | collective-permute-done | bytes 65568 | tf_op jit(solution)/shard_map/ppermute | solution.py:18
  74.2 7.0 %collective-permute-start.12 = (f32[128,128]{0,1:T(8,128)S(1)}, f32[128,128]{0,1:T(8,128)S(1)}, u32[]{:S(2)}, u32[]{:S(2)}) collective-permute-start(f32[128,128]{0,1:T(8,128)S(1)} %add.104), channel_id=1, source_target_pairs={{0,64},{4,68},{8,72},{12,76},{16,80},{20,84},{24,88},{28,92},{32,9... | collective-permute-start | bytes 196616 | tf_op jit(solution)/shard_map/ppermute | solution.py:18
  81.2 2.2 %collective-permute-done.12 = f32[128,128]{0,1:T(8,128)S(1)} collective-permute-done((f32[128,128]{0,1:T(8,128)S(1)}, f32[128,128]{0,1:T(8,128)S(1)}, u32[]{:S(2)}, u32[]{:S(2)}) %collective-permute-start.12) | collective-permute-done | bytes 65568 | tf_op jit(solution)/shard_map/ppermute | solution.py:18
  83.5 6.6 %collective-permute-done.13 = f32[128,128]{0,1:T(8,128)S(1)} collective-permute-done((f32[128,128]{0,1:T(8,128)S(1)}, f32[128,128]{0,1:T(8,128)S(1)}, u32[]{:S(2)}, u32[]{:S(2)}) %collective-permute-start.13) | collective-permute-done | bytes 65568 | tf_op jit(solution)/shard_map/ppermute | solution.py:18
  90.5 4.0 %collective-permute-done.14 = f32[128,128]{0,1:T(8,128)S(1)} collective-permute-done((f32[128,128]{0,1:T(8,128)S(1)}, f32[128,128]{0,1:T(8,128)S(1)}, u32[]{:S(2)}, u32[]{:S(2)}) %collective-permute-start.14) | collective-permute-done | bytes 65568 | tf_op jit(solution)/shard_map/ppermute | solution.py:18
  94.5 3.0 %collective-permute-start.15 = (f32[128,128]{0,1:T(8,128)S(1)}, f32[128,128]{0,1:T(8,128)S(1)}, u32[]{:S(2)}, u32[]{:S(2)}) collective-permute-start(f32[128,128]{0,1:T(8,128)S(1)} %add.107), channel_id=1, source_target_pairs={{0,3},{1,2},{2,1},{3,0},{4,7},{5,6},{6,5},{7,4},{8,11},{9,10},{10,... | collective-permute-start | bytes 196616 | tf_op jit(solution)/shard_map/ppermute | solution.py:18
  97.5 2.5 %collective-permute-done.15 = f32[128,128]{0,1:T(8,128)S(1)} collective-permute-done((f32[128,128]{0,1:T(8,128)S(1)}, f32[128,128]{0,1:T(8,128)S(1)}, u32[]{:S(2)}, u32[]{:S(2)}) %collective-permute-start.15) | collective-permute-done | bytes 65568 | tf_op jit(solution)/shard_map/ppermute | solution.py:18
  102.3 4.7 %shard_map.67 = (f32[32,32]{1,0:T(8,128)}, f32[32,32]{1,0:T(8,128)}) custom-call(f32[32,32]{1,0:T(8,128)} %fusion.28.gram_ref), custom_call_target="tpu_custom_call" | custom-call | tf_op jit(solution)/shard_map/pallas_call | solution.py:92
  (68 shorter events, 18.4 us)
Async XLA Ops:
  1.5 4.3 %collective-permute-start = (f32[32,512]{1,0:T(8,128)S(1)}, f32[32,512]{1,0:T(8,128)S(1)}, u32[]{:S(2)}, u32[]{:S(2)}) collective-permute-start(f32[32,512]{1,0:T(8,128)S(1)} %bitcast.59), channel_id=1, source_target_pairs={{0,1},{1,0},{2,3},{3,2},{4,5},{5,4},{6,7},{7,6},{8,9},{9,8},{10,11... | collective-permute-start | bytes 196616 | tf_op jit(solution)/shard_map/ppermute | solution.py:18
  5.8 6.3 %collective-permute-start.1 = (f32[32,1024]{1,0:T(8,128)S(1)}, f32[32,1024]{1,0:T(8,128)S(1)}, u32[]{:S(2)}, u32[]{:S(2)}) collective-permute-start(f32[32,1024]{1,0:T(8,128)S(1)} %maximum_select_fusion.1), channel_id=1, source_target_pairs={{0,3},{1,2},{2,1},{3,0},{4,7},{5,6},{6,5},{7,4},{8,11},{9,10},{10,... | collective-permute-start | bytes 393224 | tf_op jit(solution)/shard_map/ppermute | solution.py:18
  13.5 6.8 %collective-permute-start.2 = (f32[32,512]{1,0:T(8,128)S(1)}, f32[32,512]{1,0:T(8,128)S(1)}, u32[]{:S(2)}, u32[]{:S(2)}) collective-permute-start(f32[32,512]{1,0:T(8,128)S(1)} %select_bitcast_fusion.1), channel_id=1, source_target_pairs={{0,4},{4,8},{8,12},{12,16},{16,20},{20,24},{24,28},{28,32},{32,36}... | collective-permute-start | bytes 196616 | tf_op jit(solution)/shard_map/ppermute | solution.py:13
  16.6 5.5 %collective-permute-start.3 = (f32[32,512]{1,0:T(8,128)S(1)}, f32[32,512]{1,0:T(8,128)S(1)}, u32[]{:S(2)}, u32[]{:S(2)}) collective-permute-start(f32[32,512]{1,0:T(8,128)S(1)} %select_bitcast_fusion), channel_id=1, source_target_pairs={{4,0},{8,4},{12,8},{16,12},{20,16},{24,20},{28,24},{32,28},{36,32}... | collective-permute-start | bytes 196616 | tf_op jit(solution)/shard_map/ppermute | solution.py:13
  20.3 10.5 %copy-start = (f32[1,768,3072]{2,1,0:T(8,128)S(1)}, f32[1,768,3072]{2,1,0:T(8,128)}, u32[]{:S(2)}) copy-start(f32[1,768,3072]{2,1,0:T(8,128)} %param.7) | copy-start | bytes 28311556
  30.9 20.8 %copy-start.1 = (f32[96,1,512]{2,1,0:T(1,128)S(1)}, f32[96,1,512]{2,1,0:T(1,128)}, u32[]{:S(2)}) copy-start(f32[96,1,512]{2,1,0:T(1,128)} %param.8) | copy-start | bytes 589828
  32.0 9.4 %collective-permute-start.5 = (f32[32,512]{1,0:T(8,128)S(1)}, f32[32,512]{1,0:T(8,128)S(1)}, u32[]{:S(2)}, u32[]{:S(2)}) collective-permute-start(f32[32,512]{1,0:T(8,128)S(1)} %get-tuple-element.18), channel_id=1, source_target_pairs={{0,4},{4,8},{8,12},{12,16},{16,20},{20,24},{24,28},{28,32},{32,36}... | collective-permute-start | bytes 196616 | tf_op jit(solution)/shard_map/ppermute | solution.py:13
  39.5 3.8 %collective-permute-start.4 = (f32[32,512]{1,0:T(8,128)S(1)}, f32[32,512]{1,0:T(8,128)S(1)}, u32[]{:S(2)}, u32[]{:S(2)}) collective-permute-start(f32[32,512]{1,0:T(8,128)S(1)} %get-tuple-element.17), channel_id=1, source_target_pairs={{4,0},{8,4},{12,8},{16,12},{20,16},{24,20},{28,24},{32,28},{36,32}... | collective-permute-start | bytes 196616 | tf_op jit(solution)/shard_map/ppermute | solution.py:13
  45.0 6.3 %collective-permute-start.6 = (f32[32,1024]{1,0:T(8,128)S(1)}, f32[32,1024]{1,0:T(8,128)S(1)}, u32[]{:S(2)}, u32[]{:S(2)}) collective-permute-start(f32[32,1024]{1,0:T(8,128)S(1)} %constant_dynamic-slice_fusion.1), channel_id=1, source_target_pairs={{0,3},{1,2},{2,1},{3,0},{4,7},{5,6},{6,5},{7,4},{8,11},{9,10},{10,... | collective-permute-start | bytes 393224 | tf_op jit(solution)/shard_map/ppermute | solution.py:18
  51.3 4.5 %collective-permute-start.7 = (f32[32,512]{1,0:T(8,128)S(1)}, f32[32,512]{1,0:T(8,128)S(1)}, u32[]{:S(2)}, u32[]{:S(2)}) collective-permute-start(f32[32,512]{1,0:T(8,128)S(1)} %constant_dynamic-slice_fusion), channel_id=1, source_target_pairs={{0,1},{1,0},{2,3},{3,2},{4,5},{5,4},{6,7},{7,6},{8,9},{9,8},{10,11... | collective-permute-start | bytes 196616 | tf_op jit(solution)/shard_map/ppermute | solution.py:18
  56.5 3.3 %collective-permute-start.8 = (f32[128,128]{0,1:T(8,128)S(1)}, f32[128,128]{0,1:T(8,128)S(1)}, u32[]{:S(2)}, u32[]{:S(2)}) collective-permute-start(f32[128,128]{0,1:T(8,128)S(1)} %select_maximum_fusion), channel_id=1, source_target_pairs={{0,4},{4,0},{8,12},{12,8},{16,20},{20,16},{24,28},{28,24},{32,36},... | collective-permute-start | bytes 196616 | tf_op jit(solution)/shard_map/ppermute | solution.py:18
  59.9 4.4 %collective-permute-start.9 = (f32[128,128]{0,1:T(8,128)S(1)}, f32[128,128]{0,1:T(8,128)S(1)}, u32[]{:S(2)}, u32[]{:S(2)}) collective-permute-start(f32[128,128]{0,1:T(8,128)S(1)} %fusion.59), channel_id=1, source_target_pairs={{0,8},{4,12},{8,0},{12,4},{16,24},{20,28},{24,16},{28,20},{32,40},... | collective-permute-start | bytes 196616 | tf_op jit(solution)/shard_map/ppermute | solution.py:18
  64.3 5.6 %collective-permute-start.10 = (f32[128,128]{0,1:T(8,128)S(1)}, f32[128,128]{0,1:T(8,128)S(1)}, u32[]{:S(2)}, u32[]{:S(2)}) collective-permute-start(f32[128,128]{0,1:T(8,128)S(1)} %add.102), channel_id=1, source_target_pairs={{0,24},{4,28},{8,16},{12,20},{16,8},{20,12},{24,0},{28,4},{32,56},... | collective-permute-start | bytes 196616 | tf_op jit(solution)/shard_map/ppermute | solution.py:18
  69.8 4.4 %collective-permute-start.11 = (f32[128,128]{0,1:T(8,128)S(1)}, f32[128,128]{0,1:T(8,128)S(1)}, u32[]{:S(2)}, u32[]{:S(2)}) collective-permute-start(f32[128,128]{0,1:T(8,128)S(1)} %add.103), channel_id=1, source_target_pairs={{0,32},{4,36},{8,40},{12,44},{16,48},{20,52},{24,56},{28,60},{32,0... | collective-permute-start | bytes 196616 | tf_op jit(solution)/shard_map/ppermute | solution.py:18
  74.2 9.2 %collective-permute-start.12 = (f32[128,128]{0,1:T(8,128)S(1)}, f32[128,128]{0,1:T(8,128)S(1)}, u32[]{:S(2)}, u32[]{:S(2)}) collective-permute-start(f32[128,128]{0,1:T(8,128)S(1)} %add.104), channel_id=1, source_target_pairs={{0,64},{4,68},{8,72},{12,76},{16,80},{20,84},{24,88},{28,92},{32,9... | collective-permute-start | bytes 196616 | tf_op jit(solution)/shard_map/ppermute | solution.py:18
  83.4 6.7 %collective-permute-start.13 = (f32[128,128]{0,1:T(8,128)S(1)}, f32[128,128]{0,1:T(8,128)S(1)}, u32[]{:S(2)}, u32[]{:S(2)}) collective-permute-start(f32[128,128]{0,1:T(8,128)S(1)} %add.105), channel_id=1, source_target_pairs={{0,192},{4,196},{8,200},{12,204},{16,208},{20,212},{24,216},{28,22... | collective-permute-start | bytes 196616 | tf_op jit(solution)/shard_map/ppermute | solution.py:18
  90.1 4.4 %collective-permute-start.14 = (f32[128,128]{0,1:T(8,128)S(1)}, f32[128,128]{0,1:T(8,128)S(1)}, u32[]{:S(2)}, u32[]{:S(2)}) collective-permute-start(f32[128,128]{0,1:T(8,128)S(1)} %add.106), channel_id=1, source_target_pairs={{0,1},{1,0},{2,3},{3,2},{4,5},{5,4},{6,7},{7,6},{8,9},{9,8},{10,11... | collective-permute-start | bytes 196616 | tf_op jit(solution)/shard_map/ppermute | solution.py:18
  94.5 5.6 %collective-permute-start.15 = (f32[128,128]{0,1:T(8,128)S(1)}, f32[128,128]{0,1:T(8,128)S(1)}, u32[]{:S(2)}, u32[]{:S(2)}) collective-permute-start(f32[128,128]{0,1:T(8,128)S(1)} %add.107), channel_id=1, source_target_pairs={{0,3},{1,2},{2,1},{3,0},{4,7},{5,6},{6,5},{7,4},{8,11},{9,10},{10,... | collective-permute-start | bytes 196616 | tf_op jit(solution)/shard_map/ppermute | solution.py:18
  100.3 8.2 %copy-start.2 = (f32[96,32]{0,1:T(8,128)}, f32[96,32]{0,1:T(8,128)S(1)}, u32[]{:S(2)}) copy-start(f32[96,32]{0,1:T(8,128)S(1)} %get-tuple-element.23) | copy-start | bytes 36868

commit v12 on v8

--- a/solution.py
+++ b/solution.py
@@ -3,6 +3,7 @@
 from jax import lax
 from jax.experimental import pallas as pl
 from jax.sharding import PartitionSpec as P
+
 
 HIGH = lax.Precision.HIGHEST
 
@@ -39,18 +40,6 @@
         other = swap(block, axis, mask)
         upper = (pos & step) != 0
         block = jnp.where(upper, jnp.concatenate([other, block], axis=1), jnp.concatenate([block, other], axis=1))
-    return block
-
-
-def scatter_rows(value, axis):
-    pos = lax.axis_index(axis)
-    block = value
-    for step, mask in reversed(ring_masks(lax.axis_size(axis))):
-        half = block.shape[1] // 2
-        upper = ((pos // step) % 2).astype(jnp.int32)
-        keep = lax.dynamic_slice_in_dim(block, upper * half, half, 1)
-        send = lax.dynamic_slice_in_dim(block, (1 - upper) * half, half, 1)
-        block = keep + swap(send, axis, mask)
     return block
 
 
@@ -124,15 +113,27 @@
     back_upper = from_behind(margin_value[:, :margin], "sub", -1)
     back_lower = from_behind(margin_value[:, margin:], "sub", 1)
     own_value = jnp.dot(inner, factor_rows[:, :sub_rows], precision=three) + placed[:, :sub_rows]
-    all_rows = lax.iota(jnp.int32, sub_rows)
-    select_upper = (index_rows[1][:, None] == all_rows[None, :]).astype(jnp.float32)
-    select_lower = (index_rows[0][:, None] == all_rows[None, :]).astype(jnp.float32)
-    gathered = (
-        own_value
-        + jnp.dot(back_upper, select_upper, precision=three)
-        + jnp.dot(back_lower, select_lower, precision=three)
-    )
-    block_t = scatter_rows(gathered, "row")
+    half = sub_rows // 2
+
+    def half_value(which):
+        rows_here = which * half + lax.iota(jnp.int32, half)
+        select_upper = (index_rows[1][:, None] == rows_here[None, :]).astype(jnp.float32)
+        select_lower = (index_rows[0][:, None] == rows_here[None, :]).astype(jnp.float32)
+        return (
+            lax.dynamic_slice_in_dim(own_value, which * half, half, 1)
+            + jnp.dot(back_upper, select_upper, precision=HIGH)
+            + jnp.dot(back_lower, select_lower, precision=HIGH)
+        )
+
+    (step, mask), rest = ring_masks(row_count)[-1], ring_masks(row_count)[:-1]
+    keep_upper = ((row_pos // step) % 2).astype(jnp.int32)
+    block_t = half_value(keep_upper) + swap(half_value(1 - keep_upper), "row", mask)
+    for step, mask in reversed(rest):
+        part = block_t.shape[1] // 2
+        upper = ((row_pos // step) % 2).astype(jnp.int32)
+        keep = lax.dynamic_slice_in_dim(block_t, upper * part, part, 1)
+        send = lax.dynamic_slice_in_dim(block_t, (1 - upper) * part, part, 1)
+        block_t = keep + swap(send, "row", mask)
     vectors = basis[:, 0, :]
     count = vectors.shape[0]
     vecs = block_t.shape[0]
@@ -170,6 +171,7 @@
         P(None, "sub", "row"),
         P("sub", None, None),
     )
+
     return jax.shard_map(
         per_device,
         mesh=mesh,

time: 108 us -> 108 us (level)
    dot_general x2 -> x4, matrix products: 2.66 us -> 3.41 us  [the longest x2 1.71 us: half_value(): jnp.dot(back_upper, select_upper, precision=HIGH)]
where the time goes in v12:
time: 108 us; the launch traced here: 107 us
  waiting for transfers between devices  42.6 us (39%)
  starting transfers between devices  34.1 us (32%)
  matrix products  18.7 us (17%)
  local copies, waits for them, and re-layouts  5.21 us (5%)
  Pallas kernels  4.68 us (4%)
  between operations  1.09 us (1%)
    ppermute x12, waiting for transfers between devices, swap(): lax.ppermute(value, axis, [(source, source ^ mask) for source in range(co...  40.4 us
    ppermute x12, starting transfers between devices, swap(): lax.ppermute(value, axis, [(source, source ^ mask) for source in range(co...  22.7 us
    ppermute x4, starting transfers between devices, from_behind(): lax.ppermute(value, axis, [(source, source + steps) for source in range(l...  11.4 us
    dot_general x1, matrix products, per_device(): lax.dot_general(whole, factor_rows[:, :sub_rows], by_rows, precision=three)  5.6 us
    pallas_call x1, Pallas kernels, cholesky_parts(): pl.pallas_call(factor_kernel, out_shape=(shape, shape))  4.68 us
    dot_general x1, matrix products, per_device(): lax.dot_general(margins, factor_rows[:, sub_rows:], by_rows, precision=th...  3.35 us
    dot_general x1, matrix products, per_device(): jnp.dot(inner, factor_rows[:, :sub_rows], precision=three)  2.22 us
    ppermute x4, waiting for transfers between devices, from_behind(): lax.ppermute(value, axis, [(source, source + steps) for source in range(l...  2.17 us
  transfers between devices with their start and end apart: 16, of which 13 were waited for; matrix products, arithmetic and copies ran while one was open for 11% of the time, Pallas kernels for 0%

profile of v12, /device:TPU:38, one launch (start us, length us, event | category | flops | bytes accessed | tf_op | source)
XLA Modules:
  0.0 107.4 jit_solution(4196354439589324494)
XLA Ops:
  5.8 3.1 %collective-permute-start.1 = (f32[32,1024]{1,0:T(8,128)S(1)}, f32[32,1024]{1,0:T(8,128)S(1)}, u32[]{:S(2)}, u32[]{:S(2)}) collective-permute-start(f32[32,1024]{1,0:T(8,128)S(1)} %maximum_select_fusion.1), channel_id=1, source_target_pairs={{0,3},{1,2},{2,1},{3,0},{4,7},{5,6},{6,5},{7,4},{8,11},{9,10},{10,... | collective-permute-start | bytes 393224 | tf_op jit(solution)/shard_map/ppermute | solution.py:19
  8.9 3.2 %collective-permute-done.1 = f32[32,1024]{1,0:T(8,128)S(1)} collective-permute-done((f32[32,1024]{1,0:T(8,128)S(1)}, f32[32,1024]{1,0:T(8,128)S(1)}, u32[]{:S(2)}, u32[]{:S(2)}) %collective-permute-start.1) | collective-permute-done | bytes 131104 | tf_op jit(solution)/shard_map/ppermute | solution.py:19
  13.6 1.9 %collective-permute-start.2 = (f32[32,512]{1,0:T(8,128)S(1)}, f32[32,512]{1,0:T(8,128)S(1)}, u32[]{:S(2)}, u32[]{:S(2)}) collective-permute-start(f32[32,512]{1,0:T(8,128)S(1)} %select_bitcast_fusion.1), channel_id=1, source_target_pairs={{0,4},{4,8},{8,12},{12,16},{16,20},{20,24},{24,28},{28,32},{32,36}... | collective-permute-start | bytes 196616 | tf_op jit(solution)/shard_map/ppermute | solution.py:14
  16.6 3.9 %collective-permute-start.3 = (f32[32,512]{1,0:T(8,128)S(1)}, f32[32,512]{1,0:T(8,128)S(1)}, u32[]{:S(2)}, u32[]{:S(2)}) collective-permute-start(f32[32,512]{1,0:T(8,128)S(1)} %select_bitcast_fusion), channel_id=1, source_target_pairs={{4,0},{8,4},{12,8},{16,12},{20,16},{24,20},{28,24},{32,28},{36,32}... | collective-permute-start | bytes 196616 | tf_op jit(solution)/shard_map/ppermute | solution.py:14
  20.6 5.6 %fusion.2 = f32[32,768]{1,0:T(8,128)S(1)} fusion(f32[32,2048]{1,0:T(8,128)S(1)} %maximum_select_fusion, f32[768,3072]{1,0:T(8,128)} %bitcast.53), kind=kOutput, calls=%fused_computation.4 | convolution fusion | flops 301989888 | bytes 6651904 | tf_op jit(solution)/shard_map/dot_general | solution.py:103
  26.2 3.4 %fusion.6 = f32[32,768]{1,0:T(8,128)S(1)} fusion(f32[768,3072]{1,0:T(8,128)} %bitcast.54, f32[32,512]{1,0:T(8,128)S(1)} %collective-permute-done.3, f32[32,512]{1,0:T(8,128)S(1)} %collective-permute-done.2), kind=kOutput, calls=%fused_computation.8 | convolution fusion | flops 151027712 | bytes 3375104 | tf_op jit(solution)/shard_map/dot_general | solution.py:108
  30.8 2.6 %collective-permute-start.5 = (f32[32,512]{1,0:T(8,128)S(1)}, f32[32,512]{1,0:T(8,128)S(1)}, u32[]{:S(2)}, u32[]{:S(2)}) collective-permute-start(f32[32,512]{1,0:T(8,128)S(1)} %get-tuple-element.20), channel_id=1, source_target_pairs={{0,4},{4,8},{8,12},{12,16},{16,20},{20,24},{24,28},{28,32},{32,36}... | collective-permute-start | bytes 196616 | tf_op jit(solution)/shard_map/ppermute | solution.py:14
  33.4 2.2 %fusion.8 = f32[32,2048]{1,0:T(8,128)S(1)} fusion(f32[32,768]{1,0:T(8,128)S(1)} %get-tuple-element.18, f32[768,3072]{1,0:T(8,128)S(1)} %bitcast.56, f32[32,3072]{1,0:T(8,128)S(1)} %get-tuple-element.17), kind=kOutput, calls=%fused_computation.10 | convolution fusion | flops 302055424 | bytes 6914048 | tf_op jit(solution)/shard_map/dot_general | solution.py:115
  35.7 3.0 %collective-permute-start.4 = (f32[32,512]{1,0:T(8,128)S(1)}, f32[32,512]{1,0:T(8,128)S(1)}, u32[]{:S(2)}, u32[]{:S(2)}) collective-permute-start(f32[32,512]{1,0:T(8,128)S(1)} %get-tuple-element.19), channel_id=1, source_target_pairs={{4,0},{8,4},{12,8},{16,12},{20,16},{24,20},{28,24},{32,28},{36,32}... | collective-permute-start | bytes 196616 | tf_op jit(solution)/shard_map/ppermute | solution.py:14
  39.5 2.2 %collective-permute-done.4 = f32[32,512]{1,0:T(8,128)S(1)} collective-permute-done((f32[32,512]{1,0:T(8,128)S(1)}, f32[32,512]{1,0:T(8,128)S(1)}, u32[]{:S(2)}, u32[]{:S(2)}) %collective-permute-start.4) | collective-permute-done | bytes 65568 | tf_op jit(solution)/shard_map/ppermute | solution.py:14
  42.5 3.1 %collective-permute-start.6 = (f32[32,1024]{1,0:T(8,128)S(1)}, f32[32,1024]{1,0:T(8,128)S(1)}, u32[]{:S(2)}, u32[]{:S(2)}) collective-permute-start(f32[32,1024]{1,0:T(8,128)S(1)} %fusion.34), channel_id=1, source_target_pairs={{0,3},{1,2},{2,1},{3,0},{4,7},{5,6},{6,5},{7,4},{8,11},{9,10},{10,... | collective-permute-start | bytes 393224 | tf_op jit(solution)/shard_map/ppermute | solution.py:19
  46.5 2.3 %collective-permute-done.6 = f32[32,1024]{1,0:T(8,128)S(1)} collective-permute-done((f32[32,1024]{1,0:T(8,128)S(1)}, f32[32,1024]{1,0:T(8,128)S(1)}, u32[]{:S(2)}, u32[]{:S(2)}) %collective-permute-start.6) | collective-permute-done | bytes 131104 | tf_op jit(solution)/shard_map/ppermute | solution.py:19
  50.3 3.9 %collective-permute-done.7 = f32[32,512]{1,0:T(8,128)S(1)} collective-permute-done((f32[32,512]{1,0:T(8,128)S(1)}, f32[32,512]{1,0:T(8,128)S(1)}, u32[]{:S(2)}, u32[]{:S(2)}) %collective-permute-start.7) | collective-permute-done | bytes 65568 | tf_op jit(solution)/shard_map/ppermute | solution.py:19
  54.8 2.8 %collective-permute-start.8 = (f32[128,128]{0,1:T(8,128)S(1)}, f32[128,128]{0,1:T(8,128)S(1)}, u32[]{:S(2)}, u32[]{:S(2)}) collective-permute-start(f32[128,128]{0,1:T(8,128)S(1)} %select_maximum_fusion), channel_id=1, source_target_pairs={{0,4},{4,0},{8,12},{12,8},{16,20},{20,16},{24,28},{28,24},{32,36},... | collective-permute-start | bytes 196616 | tf_op jit(solution)/shard_map/ppermute | solution.py:19
  58.7 4.3 %collective-permute-done.9 = f32[128,128]{0,1:T(8,128)S(1)} collective-permute-done((f32[128,128]{0,1:T(8,128)S(1)}, f32[128,128]{0,1:T(8,128)S(1)}, u32[]{:S(2)}, u32[]{:S(2)}) %collective-permute-start.9) | collective-permute-done | bytes 65568 | tf_op jit(solution)/shard_map/ppermute | solution.py:19
  64.1 4.5 %collective-permute-done.10 = f32[128,128]{0,1:T(8,128)S(1)} collective-permute-done((f32[128,128]{0,1:T(8,128)S(1)}, f32[128,128]{0,1:T(8,128)S(1)}, u32[]{:S(2)}, u32[]{:S(2)}) %collective-permute-start.10) | collective-permute-done | bytes 65568 | tf_op jit(solution)/shard_map/ppermute | solution.py:19
  68.8 4.2 %collective-permute-done.11 = f32[128,128]{0,1:T(8,128)S(1)} collective-permute-done((f32[128,128]{0,1:T(8,128)S(1)}, f32[128,128]{0,1:T(8,128)S(1)}, u32[]{:S(2)}, u32[]{:S(2)}) %collective-permute-start.11) | collective-permute-done | bytes 65568 | tf_op jit(solution)/shard_map/ppermute | solution.py:19
  73.0 7.0 %collective-permute-start.12 = (f32[128,128]{0,1:T(8,128)S(1)}, f32[128,128]{0,1:T(8,128)S(1)}, u32[]{:S(2)}, u32[]{:S(2)}) collective-permute-start(f32[128,128]{0,1:T(8,128)S(1)} %add.140), channel_id=1, source_target_pairs={{0,64},{4,68},{8,72},{12,76},{16,80},{20,84},{24,88},{28,92},{32,9... | collective-permute-start | bytes 196616 | tf_op jit(solution)/shard_map/ppermute | solution.py:19
  80.0 2.2 %collective-permute-done.12 = f32[128,128]{0,1:T(8,128)S(1)} collective-permute-done((f32[128,128]{0,1:T(8,128)S(1)}, f32[128,128]{0,1:T(8,128)S(1)}, u32[]{:S(2)}, u32[]{:S(2)}) %collective-permute-start.12) | collective-permute-done | bytes 65568 | tf_op jit(solution)/shard_map/ppermute | solution.py:19
  82.3 6.6 %collective-permute-done.13 = f32[128,128]{0,1:T(8,128)S(1)} collective-permute-done((f32[128,128]{0,1:T(8,128)S(1)}, f32[128,128]{0,1:T(8,128)S(1)}, u32[]{:S(2)}, u32[]{:S(2)}) %collective-permute-start.13) | collective-permute-done | bytes 65568 | tf_op jit(solution)/shard_map/ppermute | solution.py:19
  89.3 4.0 %collective-permute-done.14 = f32[128,128]{0,1:T(8,128)S(1)} collective-permute-done((f32[128,128]{0,1:T(8,128)S(1)}, f32[128,128]{0,1:T(8,128)S(1)}, u32[]{:S(2)}, u32[]{:S(2)}) %collective-permute-start.14) | collective-permute-done | bytes 65568 | tf_op jit(solution)/shard_map/ppermute | solution.py:19
  93.3 3.0 %collective-permute-start.15 = (f32[128,128]{0,1:T(8,128)S(1)}, f32[128,128]{0,1:T(8,128)S(1)}, u32[]{:S(2)}, u32[]{:S(2)}) collective-permute-start(f32[128,128]{0,1:T(8,128)S(1)} %add.143), channel_id=1, source_target_pairs={{0,3},{1,2},{2,1},{3,0},{4,7},{5,6},{6,5},{7,4},{8,11},{9,10},{10,... | collective-permute-start | bytes 196616 | tf_op jit(solution)/shard_map/ppermute | solution.py:19
  96.3 2.5 %collective-permute-done.15 = f32[128,128]{0,1:T(8,128)S(1)} collective-permute-done((f32[128,128]{0,1:T(8,128)S(1)}, f32[128,128]{0,1:T(8,128)S(1)}, u32[]{:S(2)}, u32[]{:S(2)}) %collective-permute-start.15) | collective-permute-done | bytes 65568 | tf_op jit(solution)/shard_map/ppermute | solution.py:19
  101.1 4.7 %shard_map.67 = (f32[32,32]{1,0:T(8,128)}, f32[32,32]{1,0:T(8,128)}) custom-call(f32[32,32]{1,0:T(8,128)} %fusion.63.gram_ref), custom_call_target="tpu_custom_call" | custom-call | tf_op jit(solution)/shard_map/pallas_call | solution.py:81
  (71 shorter events, 20.1 us)
Async XLA Ops:
  1.5 4.3 %collective-permute-start = (f32[32,512]{1,0:T(8,128)S(1)}, f32[32,512]{1,0:T(8,128)S(1)}, u32[]{:S(2)}, u32[]{:S(2)}) collective-permute-start(f32[32,512]{1,0:T(8,128)S(1)} %bitcast.57), channel_id=1, source_target_pairs={{0,1},{1,0},{2,3},{3,2},{4,5},{5,4},{6,7},{7,6},{8,9},{9,8},{10,11... | collective-permute-start | bytes 196616 | tf_op jit(solution)/shard_map/ppermute | solution.py:19
  5.8 6.3 %collective-permute-start.1 = (f32[32,1024]{1,0:T(8,128)S(1)}, f32[32,1024]{1,0:T(8,128)S(1)}, u32[]{:S(2)}, u32[]{:S(2)}) collective-permute-start(f32[32,1024]{1,0:T(8,128)S(1)} %maximum_select_fusion.1), channel_id=1, source_target_pairs={{0,3},{1,2},{2,1},{3,0},{4,7},{5,6},{6,5},{7,4},{8,11},{9,10},{10,... | collective-permute-start | bytes 393224 | tf_op jit(solution)/shard_map/ppermute | solution.py:19
  13.6 12.6 %collective-permute-start.2 = (f32[32,512]{1,0:T(8,128)S(1)}, f32[32,512]{1,0:T(8,128)S(1)}, u32[]{:S(2)}, u32[]{:S(2)}) collective-permute-start(f32[32,512]{1,0:T(8,128)S(1)} %select_bitcast_fusion.1), channel_id=1, source_target_pairs={{0,4},{4,8},{8,12},{12,16},{16,20},{20,24},{24,28},{28,32},{32,36}... | collective-permute-start | bytes 196616 | tf_op jit(solution)/shard_map/ppermute | solution.py:14
  16.6 13.0 %copy-start = (f32[1,768,3072]{2,1,0:T(8,128)S(1)}, f32[1,768,3072]{2,1,0:T(8,128)}, u32[]{:S(2)}) copy-start(f32[1,768,3072]{2,1,0:T(8,128)} %param.7) | copy-start | bytes 28311556
  16.6 9.5 %collective-permute-start.3 = (f32[32,512]{1,0:T(8,128)S(1)}, f32[32,512]{1,0:T(8,128)S(1)}, u32[]{:S(2)}, u32[]{:S(2)}) collective-permute-start(f32[32,512]{1,0:T(8,128)S(1)} %select_bitcast_fusion), channel_id=1, source_target_pairs={{4,0},{8,4},{12,8},{16,12},{20,16},{24,20},{28,24},{32,28},{36,32}... | collective-permute-start | bytes 196616 | tf_op jit(solution)/shard_map/ppermute | solution.py:14
  29.7 20.3 %copy-start.1 = (f32[96,1,512]{2,1,0:T(1,128)S(1)}, f32[96,1,512]{2,1,0:T(1,128)}, u32[]{:S(2)}) copy-start(f32[96,1,512]{2,1,0:T(1,128)} %param.8) | copy-start | bytes 589828
  30.8 7.8 %collective-permute-start.5 = (f32[32,512]{1,0:T(8,128)S(1)}, f32[32,512]{1,0:T(8,128)S(1)}, u32[]{:S(2)}, u32[]{:S(2)}) collective-permute-start(f32[32,512]{1,0:T(8,128)S(1)} %get-tuple-element.20), channel_id=1, source_target_pairs={{0,4},{4,8},{8,12},{12,16},{16,20},{20,24},{24,28},{28,32},{32,36}... | collective-permute-start | bytes 196616 | tf_op jit(solution)/shard_map/ppermute | solution.py:14
  35.7 6.0 %collective-permute-start.4 = (f32[32,512]{1,0:T(8,128)S(1)}, f32[32,512]{1,0:T(8,128)S(1)}, u32[]{:S(2)}, u32[]{:S(2)}) collective-permute-start(f32[32,512]{1,0:T(8,128)S(1)} %get-tuple-element.19), channel_id=1, source_target_pairs={{4,0},{8,4},{12,8},{16,12},{20,16},{24,20},{28,24},{32,28},{36,32}... | collective-permute-start | bytes 196616 | tf_op jit(solution)/shard_map/ppermute | solution.py:14
  42.5 6.3 %collective-permute-start.6 = (f32[32,1024]{1,0:T(8,128)S(1)}, f32[32,1024]{1,0:T(8,128)S(1)}, u32[]{:S(2)}, u32[]{:S(2)}) collective-permute-start(f32[32,1024]{1,0:T(8,128)S(1)} %fusion.34), channel_id=1, source_target_pairs={{0,3},{1,2},{2,1},{3,0},{4,7},{5,6},{6,5},{7,4},{8,11},{9,10},{10,... | collective-permute-start | bytes 393224 | tf_op jit(solution)/shard_map/ppermute | solution.py:19
  49.7 4.5 %collective-permute-start.7 = (f32[32,512]{1,0:T(8,128)S(1)}, f32[32,512]{1,0:T(8,128)S(1)}, u32[]{:S(2)}, u32[]{:S(2)}) collective-permute-start(f32[32,512]{1,0:T(8,128)S(1)} %constant_dynamic-slice_fusion), channel_id=1, source_target_pairs={{0,1},{1,0},{2,3},{3,2},{4,5},{5,4},{6,7},{7,6},{8,9},{9,8},{10,11... | collective-permute-start | bytes 196616 | tf_op jit(solution)/shard_map/ppermute | solution.py:19
  54.8 3.7 %collective-permute-start.8 = (f32[128,128]{0,1:T(8,128)S(1)}, f32[128,128]{0,1:T(8,128)S(1)}, u32[]{:S(2)}, u32[]{:S(2)}) collective-permute-start(f32[128,128]{0,1:T(8,128)S(1)} %select_maximum_fusion), channel_id=1, source_target_pairs={{0,4},{4,0},{8,12},{12,8},{16,20},{20,16},{24,28},{28,24},{32,36},... | collective-permute-start | bytes 196616 | tf_op jit(solution)/shard_map/ppermute | solution.py:19
  58.7 4.4 %collective-permute-start.9 = (f32[128,128]{0,1:T(8,128)S(1)}, f32[128,128]{0,1:T(8,128)S(1)}, u32[]{:S(2)}, u32[]{:S(2)}) collective-permute-start(f32[128,128]{0,1:T(8,128)S(1)} %fusion.94), channel_id=1, source_target_pairs={{0,8},{4,12},{8,0},{12,4},{16,24},{20,28},{24,16},{28,20},{32,40},... | collective-permute-start | bytes 196616 | tf_op jit(solution)/shard_map/ppermute | solution.py:19
  63.0 5.6 %collective-permute-start.10 = (f32[128,128]{0,1:T(8,128)S(1)}, f32[128,128]{0,1:T(8,128)S(1)}, u32[]{:S(2)}, u32[]{:S(2)}) collective-permute-start(f32[128,128]{0,1:T(8,128)S(1)} %add.138), channel_id=1, source_target_pairs={{0,24},{4,28},{8,16},{12,20},{16,8},{20,12},{24,0},{28,4},{32,56},... | collective-permute-start | bytes 196616 | tf_op jit(solution)/shard_map/ppermute | solution.py:19
  68.6 4.4 %collective-permute-start.11 = (f32[128,128]{0,1:T(8,128)S(1)}, f32[128,128]{0,1:T(8,128)S(1)}, u32[]{:S(2)}, u32[]{:S(2)}) collective-permute-start(f32[128,128]{0,1:T(8,128)S(1)} %add.139), channel_id=1, source_target_pairs={{0,32},{4,36},{8,40},{12,44},{16,48},{20,52},{24,56},{28,60},{32,0... | collective-permute-start | bytes 196616 | tf_op jit(solution)/shard_map/ppermute | solution.py:19
  73.0 9.2 %collective-permute-start.12 = (f32[128,128]{0,1:T(8,128)S(1)}, f32[128,128]{0,1:T(8,128)S(1)}, u32[]{:S(2)}, u32[]{:S(2)}) collective-permute-start(f32[128,128]{0,1:T(8,128)S(1)} %add.140), channel_id=1, source_target_pairs={{0,64},{4,68},{8,72},{12,76},{16,80},{20,84},{24,88},{28,92},{32,9... | collective-permute-start | bytes 196616 | tf_op jit(solution)/shard_map/ppermute | solution.py:19
  82.2 6.7 %collective-permute-start.13 = (f32[128,128]{0,1:T(8,128)S(1)}, f32[128,128]{0,1:T(8,128)S(1)}, u32[]{:S(2)}, u32[]{:S(2)}) collective-permute-start(f32[128,128]{0,1:T(8,128)S(1)} %add.141), channel_id=1, source_target_pairs={{0,192},{4,196},{8,200},{12,204},{16,208},{20,212},{24,216},{28,22... | collective-permute-start | bytes 196616 | tf_op jit(solution)/shard_map/ppermute | solution.py:19
  88.9 4.4 %collective-permute-start.14 = (f32[128,128]{0,1:T(8,128)S(1)}, f32[128,128]{0,1:T(8,128)S(1)}, u32[]{:S(2)}, u32[]{:S(2)}) collective-permute-start(f32[128,128]{0,1:T(8,128)S(1)} %add.142), channel_id=1, source_target_pairs={{0,1},{1,0},{2,3},{3,2},{4,5},{5,4},{6,7},{7,6},{8,9},{9,8},{10,11... | collective-permute-start | bytes 196616 | tf_op jit(solution)/shard_map/ppermute | solution.py:19
  93.3 5.6 %collective-permute-start.15 = (f32[128,128]{0,1:T(8,128)S(1)}, f32[128,128]{0,1:T(8,128)S(1)}, u32[]{:S(2)}, u32[]{:S(2)}) collective-permute-start(f32[128,128]{0,1:T(8,128)S(1)} %add.143), channel_id=1, source_target_pairs={{0,3},{1,2},{2,1},{3,0},{4,7},{5,6},{6,5},{7,4},{8,11},{9,10},{10,... | collective-permute-start | bytes 196616 | tf_op jit(solution)/shard_map/ppermute | solution.py:19
  99.1 8.2 %copy-start.2 = (f32[96,32]{0,1:T(8,128)}, f32[96,32]{0,1:T(8,128)S(1)}, u32[]{:S(2)}) copy-start(f32[96,32]{0,1:T(8,128)S(1)} %get-tuple-element.23) | copy-start | bytes 36868
